TPU v7x, 256 devices: a whole 4x4x8 slice. The times are simulated.
256 devices in a mesh: section: 4 (over y), expert: 64 (over z, x, core).
Axes of the slice: x: 4, y: 4, z: 8, core: 2. Of those that a mesh axis runs over, the one named last changes fastest.
Arguments:
- in_flight: bfloat16 [4, 4096, 2048], P('section', 'expert'), may hold values from -6 to 6
- entering: bfloat16 [1, 4096, 2048], P(None, 'expert'), may hold values from -6 to 6
- norm_gain: bfloat16 [4, 2048], P('section'), may hold values from 0.5 to 1.5
- w_gate: bfloat16 [4, 64, 2048, 768], P('section', 'expert'), may hold values from -0.125 to 0.125
- w_up: bfloat16 [4, 64, 2048, 768], P('section', 'expert'), may hold values from -0.125 to 0.125
- w_down: bfloat16 [4, 64, 768, 2048], P('section', 'expert'), may hold values from -0.21875 to 0.21875
- routes: int32 [4, 2, 4096, 8], P('section', None, 'expert'), may hold values from 0 to 63, all different within a row; in each aligned block of 32 rows (0 to 31, 32 to 63, ..., all dimensions but the last counted through in order) at most 6 rows name the same one
- combine_weight: float32 [4, 2, 4096, 8], P('section', None, 'expert'), may hold values from 0.2 to 0.6
Outputs:
- trace: bfloat16 [2, 4, 4096, 2048], P(None, 'section', 'expert')
Inputs may be any that keep to these rules, and one draw needn't show every extreme that they name: `routes`: each row names 8 different experts. In each aligned block of 32 rows (all leading dimensions taken together, in order) no expert is named by more than 6 rows, a bound that some block reaches.
All inputs are finite; a program needn't handle non-finite values.
Results may differ from a plain program's by a relative error of at most 0.0085.
Values may be sent and summed in bfloat16 or wider, within the bound.
No kernel may reach another device: no remote copies, remote signals or barrier semaphores. Data moves between devices by JAX's collectives and lax.ppermute only.
A program may use at most 128 MiB of HBM per device.

v0:
```python
import jax
import jax.numpy as jnp
from jax import lax
from jax.sharding import PartitionSpec as P

TICKS = 2


EPSILON = 1e-06


def passed_along(x, axis, by):
    devices = lax.axis_size(axis)
    pairs = [(i, i + by) for i in range(devices) if 0 <= i + by < devices]
    return lax.ppermute(x, axis, pairs)


def rms_normed(hidden_rows, norm_gain):
    as_float = hidden_rows.astype(jnp.float32)
    inv_scale = lax.rsqrt(jnp.mean(as_float * as_float, axis=-1, keepdims=True) + EPSILON)
    return (as_float * inv_scale * norm_gain.astype(jnp.float32)).astype(jnp.bfloat16)


def slot_table(route_ids, experts, capacity):
    group_count, row_count, top_count = route_ids.shape
    expert_marks = (route_ids[..., None] == jnp.arange(experts, dtype=jnp.int32)).astype(jnp.int32)
    expert_marks = expert_marks.reshape(group_count, row_count * top_count, experts)
    earlier_marks = jnp.cumsum(expert_marks, axis=1) - expert_marks
    slot_index = jnp.sum(earlier_marks * expert_marks, axis=-1).reshape(
        group_count, row_count, top_count
    )
    group_index = jnp.arange(group_count, dtype=jnp.int32)[:, None, None]
    group_width = group_count * capacity
    positions = route_ids * group_width + group_index * capacity + slot_index
    return positions.reshape(group_count * row_count, top_count)


def mix_block(
    hidden_rows, normed_rows, route_ids, combine, gate_w, up_w, down_w, experts, capacity
):
    group_count = route_ids.shape[0]
    row_count = hidden_rows.shape[0]
    top_count = route_ids.shape[-1]
    model_width = hidden_rows.shape[1]
    positions = slot_table(route_ids, experts, capacity)
    slot_total = experts * group_count * capacity
    flat_slots = positions.reshape(-1)
    pick_table = flat_slots[None, :] == jnp.arange(slot_total, dtype=jnp.int32)[:, None]
    pick_table = jnp.sum(
        pick_table.reshape(slot_total, row_count, top_count).astype(jnp.int32), axis=-1
    ).astype(jnp.bfloat16)
    outgoing = jnp.dot(pick_table, normed_rows, preferred_element_type=jnp.float32).astype(
        jnp.bfloat16
    )
    outgoing = outgoing.reshape(experts, group_count * capacity, model_width)
    received = lax.all_to_all(outgoing, "expert", split_axis=0, concat_axis=0, tiled=True)
    row_shape = received.shape
    inputs = received.reshape(-1, row_shape[-1])
    gate_sum = jnp.dot(inputs, gate_w, preferred_element_type=jnp.float32)
    up_sum = jnp.dot(inputs, up_w, preferred_element_type=jnp.float32)
    hidden = (jax.nn.silu(gate_sum) * up_sum).astype(jnp.bfloat16)
    result = jnp.dot(hidden, down_w, preferred_element_type=jnp.float32).astype(jnp.bfloat16)
    returned = lax.all_to_all(
        result.reshape(row_shape), "expert", split_axis=0, concat_axis=0, tiled=True
    )
    returned = returned.reshape(slot_total, model_width)
    residual = hidden_rows.astype(jnp.float32)
    hit_table = (flat_slots[:, None] == jnp.arange(slot_total, dtype=jnp.int32)[None, :]).astype(
        jnp.float32
    )
    mixing = jnp.sum(
        hit_table.reshape(row_count, top_count, slot_total) * combine[:, :, None], axis=1
    )
    mixing_high = mixing.astype(jnp.bfloat16)
    mixing_low = (mixing - mixing_high.astype(jnp.float32)).astype(jnp.bfloat16)
    branch_sum = jnp.dot(mixing_high, returned, preferred_element_type=jnp.float32)
    branch_sum = branch_sum + jnp.dot(mixing_low, returned, preferred_element_type=jnp.float32)
    return (residual + branch_sum).astype(jnp.bfloat16)


def apply_layer(hidden_rows, norm_gain, route_ids, combine, gate_w, up_w, down_w, experts):
    normed_rows = rms_normed(hidden_rows, norm_gain)
    half_rows = hidden_rows.shape[0] // 2
    top_count = route_ids.shape[-1]
    capacity = max(2, min(half_rows, half_rows * top_count // experts * 3 // 2))
    first_part = mix_block(
        hidden_rows[:half_rows],
        normed_rows[:half_rows],
        route_ids[:half_rows][None],
        combine[:half_rows],
        gate_w,
        up_w,
        down_w,
        experts,
        capacity,
    )
    second_part = mix_block(
        hidden_rows[half_rows:],
        normed_rows[half_rows:],
        route_ids[half_rows:][None],
        combine[half_rows:],
        gate_w,
        up_w,
        down_w,
        experts,
        capacity,
    )
    return jnp.concatenate([first_part, second_part], axis=0)


def local(in_flight, entering, norm_gain, w_gate, w_up, w_down, routes, combine_weight):
    section_index = lax.axis_index("section")
    experts = lax.axis_size("expert") * w_gate.shape[1]
    carried = in_flight[0]
    traced = []
    for tick_index in range(TICKS):
        layer_out = apply_layer(
            carried,
            norm_gain[0],
            routes[0, tick_index],
            combine_weight[0, tick_index],
            w_gate[0, 0],
            w_up[0, 0],
            w_down[0, 0],
            experts,
        )
        traced.append(layer_out)
        if tick_index + 1 < TICKS:
            shifted = passed_along(layer_out, "section", 1)
            carried = jnp.where(section_index == 0, entering[tick_index], shifted)
    return jnp.stack(traced)[:, None]


def solution(mesh):
    placed = (
        P("section", "expert", None),
        P(None, "expert", None),
        P("section", None),
        P("section", "expert", None, None),
        P("section", "expert", None, None),
        P("section", "expert", None, None),
        P("section", None, "expert", None),
        P("section", None, "expert", None),
    )
    return jax.shard_map(
        local,
        mesh=mesh,
        in_specs=placed,
        out_specs=P(None, "section", "expert", None),
        check_vma=False,
    )
```

profile of v0, /device:TPU:16, one launch (start us, length us, event | category | flops | bytes accessed | tf_op | source)
XLA Modules:
  0.0 503.8 jit_solution(11462351339408094624)
XLA Ops:
  11.7 12.2 %all-to-all-start = ((bf16[64,6,2048]{2,1,0:T(8,128)(2,1)}), bf16[64,6,2048]{2,1,0:T(8,128)(2,1)}, u32[]{:S(2)}, u32[]{:S(2)}) async-start(bf16[64,6,2048]{2,1,0:T(8,128)(2,1)} %reshape.663), calls=%async_computation | async-start | bytes 4194304 | tf_op jit(solution)/shard_map/all_to_all | solution.py:56
  33.8 3.7 reshape.672
  37.5 37.6 %all-to-all-done = bf16[64,6,2048]{2,1,0:T(8,128)(2,1)} async-done(((bf16[64,6,2048]{2,1,0:T(8,128)(2,1)}), bf16[64,6,2048]{2,1,0:T(8,128)(2,1)}, u32[]{:S(2)}, u32[]{:S(2)}) %all-to-all-start) | async-done | bytes 1572896 | tf_op jit(solution)/shard_map/all_to_all | solution.py:56
  75.1 5.6 %all-to-all-start.2 = ((bf16[64,6,2048]{2,1,0:T(8,128)(2,1)}), bf16[64,6,2048]{2,1,0:T(8,128)(2,1)}, u32[]{:S(2)}, u32[]{:S(2)}) async-start(bf16[64,6,2048]{2,1,0:T(8,128)(2,1)} %reshape.672), calls=%async_computation.2 | async-start | bytes 4194304 | tf_op jit(solution)/shard_map/all_to_all | solution.py:56
  80.7 3.7 reshape.664
  84.4 4.8 fusion.22
  89.2 7.0 %fusion.24 = bf16[384,2048]{1,0:T(8,128)(2,1)} fusion(bf16[1,1,768,2048]{3,2,1,0:T(8,128)(2,1)S(1)} %copy-done, bf16[384,2048]{1,0:T(8,128)(2,1)} %reshape.664, bf16[1,1,2048,768]{3,2,1,0:T(8,128)(2,1)} %param.12, f32[384,768]{1,0:T(8,128)} %fusion.22), kind=kOutput, calls=%fused_computation.24 | convolution fusion | flops 2418475008 | bytes 10616832 | tf_op jit(solution)/shard_map/dot_general | solution.py:62
  96.2 3.7 reshape.665
  99.9 32.1 %all-to-all-done.2 = bf16[64,6,2048]{2,1,0:T(8,128)(2,1)} async-done(((bf16[64,6,2048]{2,1,0:T(8,128)(2,1)}), bf16[64,6,2048]{2,1,0:T(8,128)(2,1)}, u32[]{:S(2)}, u32[]{:S(2)}) %all-to-all-start.2) | async-done | bytes 1572896 | tf_op jit(solution)/shard_map/all_to_all | solution.py:56
  131.9 5.8 %all-to-all-start.1 = ((bf16[64,6,2048]{2,1,0:T(8,128)(2,1)}), bf16[64,6,2048]{2,1,0:T(8,128)(2,1)}, u32[]{:S(2)}, u32[]{:S(2)}) async-start(bf16[64,6,2048]{2,1,0:T(8,128)(2,1)} %reshape.665), calls=%async_computation.1 | async-start | bytes 4194304 | tf_op jit(solution)/shard_map/all_to_all | solution.py:63
  141.4 4.8 fusion.20
  146.2 7.0 %fusion.27 = bf16[384,2048]{1,0:T(8,128)(2,1)} fusion(bf16[1,1,768,2048]{3,2,1,0:T(8,128)(2,1)S(1)} %copy-done, bf16[384,2048]{1,0:T(8,128)(2,1)} %reshape.673, bf16[1,1,2048,768]{3,2,1,0:T(8,128)(2,1)} %param.12, f32[384,768]{1,0:T(8,128)} %fusion.20), kind=kOutput, calls=%fused_computation.25 | convolution fusion | flops 2418475008 | bytes 10616832 | tf_op jit(solution)/shard_map/dot_general | solution.py:62
  156.8 31.9 %all-to-all-done.1 = bf16[64,6,2048]{2,1,0:T(8,128)(2,1)} async-done(((bf16[64,6,2048]{2,1,0:T(8,128)(2,1)}), bf16[64,6,2048]{2,1,0:T(8,128)(2,1)}, u32[]{:S(2)}, u32[]{:S(2)}) %all-to-all-start.1) | async-done | bytes 1572896 | tf_op jit(solution)/shard_map/all_to_all | solution.py:63
  188.7 5.6 %all-to-all-start.3 = ((bf16[64,6,2048]{2,1,0:T(8,128)(2,1)}), bf16[64,6,2048]{2,1,0:T(8,128)(2,1)}, u32[]{:S(2)}, u32[]{:S(2)}) async-start(bf16[64,6,2048]{2,1,0:T(8,128)(2,1)} %reshape.674), calls=%async_computation.3 | async-start | bytes 4194304 | tf_op jit(solution)/shard_map/all_to_all | solution.py:63
  205.3 40.2 %all-to-all-done.3 = bf16[64,6,2048]{2,1,0:T(8,128)(2,1)} async-done(((bf16[64,6,2048]{2,1,0:T(8,128)(2,1)}), bf16[64,6,2048]{2,1,0:T(8,128)(2,1)}, u32[]{:S(2)}, u32[]{:S(2)}) %all-to-all-start.3) | async-done | bytes 1572896 | tf_op jit(solution)/shard_map/all_to_all | solution.py:63
  245.6 3.7 reshape.675
  255.8 5.1 %collective-permute-done = bf16[64,2048]{1,0:T(8,128)(2,1)S(1)} collective-permute-done((bf16[64,2048]{1,0:T(8,128)(2,1)S(1)}, bf16[64,2048]{1,0:T(8,128)(2,1)S(1)}, u32[]{:S(2)}, u32[]{:S(2)}) %collective-permute-start) | collective-permute-done | bytes 262176 | tf_op jit(solution)/shard_map/ppermute | solution.py:15
  267.4 7.2 %all-to-all-start.4 = ((bf16[64,6,2048]{2,1,0:T(8,128)(2,1)}), bf16[64,6,2048]{2,1,0:T(8,128)(2,1)}, u32[]{:S(2)}, u32[]{:S(2)}) async-start(bf16[64,6,2048]{2,1,0:T(8,128)(2,1)} %reshape.681), calls=%async_computation.4 | async-start | bytes 4194304 | tf_op jit(solution)/shard_map/all_to_all | solution.py:56
  285.3 3.7 reshape.690
  289.0 36.8 %all-to-all-done.4 = bf16[64,6,2048]{2,1,0:T(8,128)(2,1)} async-done(((bf16[64,6,2048]{2,1,0:T(8,128)(2,1)}), bf16[64,6,2048]{2,1,0:T(8,128)(2,1)}, u32[]{:S(2)}, u32[]{:S(2)}) %all-to-all-start.4) | async-done | bytes 1572896 | tf_op jit(solution)/shard_map/all_to_all | solution.py:56
  325.7 5.8 %all-to-all-start.6 = ((bf16[64,6,2048]{2,1,0:T(8,128)(2,1)}), bf16[64,6,2048]{2,1,0:T(8,128)(2,1)}, u32[]{:S(2)}, u32[]{:S(2)}) async-start(bf16[64,6,2048]{2,1,0:T(8,128)(2,1)} %reshape.690), calls=%async_computation.6 | async-start | bytes 4194304 | tf_op jit(solution)/shard_map/all_to_all | solution.py:56
  335.2 4.9 fusion.18
  340.1 6.9 %fusion.30 = bf16[384,2048]{1,0:T(8,128)(2,1)} fusion(bf16[1,1,768,2048]{3,2,1,0:T(8,128)(2,1)S(1)} %copy-done, bf16[384,2048]{1,0:T(8,128)(2,1)} %reshape.682, bf16[1,1,2048,768]{3,2,1,0:T(8,128)(2,1)} %param.12, f32[384,768]{1,0:T(8,128)} %fusion.18), kind=kOutput, calls=%fused_computation.26 | convolution fusion | flops 2418475008 | bytes 10616832 | tf_op jit(solution)/shard_map/dot_general | solution.py:62
  350.7 32.0 %all-to-all-done.6 = bf16[64,6,2048]{2,1,0:T(8,128)(2,1)} async-done(((bf16[64,6,2048]{2,1,0:T(8,128)(2,1)}), bf16[64,6,2048]{2,1,0:T(8,128)(2,1)}, u32[]{:S(2)}, u32[]{:S(2)}) %all-to-all-start.6) | async-done | bytes 1572896 | tf_op jit(solution)/shard_map/all_to_all | solution.py:56
  382.7 5.6 %all-to-all-start.5 = ((bf16[64,6,2048]{2,1,0:T(8,128)(2,1)}), bf16[64,6,2048]{2,1,0:T(8,128)(2,1)}, u32[]{:S(2)}, u32[]{:S(2)}) async-start(bf16[64,6,2048]{2,1,0:T(8,128)(2,1)} %reshape.683), calls=%async_computation.5 | async-start | bytes 4194304 | tf_op jit(solution)/shard_map/all_to_all | solution.py:63
  388.3 3.7 reshape.691
  392.1 4.8 fusion.16
  396.8 7.0 %fusion.33 = bf16[384,2048]{1,0:T(8,128)(2,1)} fusion(bf16[1,1,768,2048]{3,2,1,0:T(8,128)(2,1)S(1)} %copy-done, bf16[384,2048]{1,0:T(8,128)(2,1)} %reshape.691, bf16[1,1,2048,768]{3,2,1,0:T(8,128)(2,1)} %param.12, f32[384,768]{1,0:T(8,128)} %fusion.16), kind=kOutput, calls=%fused_computation.27 | convolution fusion | flops 2418475008 | bytes 10616832 | tf_op jit(solution)/shard_map/dot_general | solution.py:62
  407.5 32.0 %all-to-all-done.5 = bf16[64,6,2048]{2,1,0:T(8,128)(2,1)} async-done(((bf16[64,6,2048]{2,1,0:T(8,128)(2,1)}), bf16[64,6,2048]{2,1,0:T(8,128)(2,1)}, u32[]{:S(2)}, u32[]{:S(2)}) %all-to-all-start.5) | async-done | bytes 1572896 | tf_op jit(solution)/shard_map/all_to_all | solution.py:63
  439.5 5.6 %all-to-all-start.7 = ((bf16[64,6,2048]{2,1,0:T(8,128)(2,1)}), bf16[64,6,2048]{2,1,0:T(8,128)(2,1)}, u32[]{:S(2)}, u32[]{:S(2)}) async-start(bf16[64,6,2048]{2,1,0:T(8,128)(2,1)} %reshape.692), calls=%async_computation.7 | async-start | bytes 4194304 | tf_op jit(solution)/shard_map/all_to_all | solution.py:63
  453.2 43.1 %all-to-all-done.7 = bf16[64,6,2048]{2,1,0:T(8,128)(2,1)} async-done(((bf16[64,6,2048]{2,1,0:T(8,128)(2,1)}), bf16[64,6,2048]{2,1,0:T(8,128)(2,1)}, u32[]{:S(2)}, u32[]{:S(2)}) %all-to-all-start.7) | async-done | bytes 1572896 | tf_op jit(solution)/shard_map/all_to_all | solution.py:63
  496.3 3.7 reshape.693
  (156 shorter events, 86.1 us)
Async XLA Ops:
  0.0 89.2 %copy-start = (bf16[1,1,768,2048]{3,2,1,0:T(8,128)(2,1)S(1)}, bf16[1,1,768,2048]{3,2,1,0:T(8,128)(2,1)}, u32[]{:S(2)}) copy-start(bf16[1,1,768,2048]{3,2,1,0:T(8,128)(2,1)} %param.13) | copy-start | bytes 9437188
  4.1 7.6 %copy-start.17 = (f32[1,2048]{1,0:T(1,128)}, f32[1,2048]{1,0:T(1,128)S(1)}, u32[]{:S(2)}) copy-start(f32[1,2048]{1,0:T(1,128)S(1)} %mul.225) | copy-start | bytes 24580
  11.7 63.4 %all-to-all-start = ((bf16[64,6,2048]{2,1,0:T(8,128)(2,1)}), bf16[64,6,2048]{2,1,0:T(8,128)(2,1)}, u32[]{:S(2)}, u32[]{:S(2)}) async-start(bf16[64,6,2048]{2,1,0:T(8,128)(2,1)} %reshape.663), calls=%async_computation | async-start | bytes 4194304 | tf_op jit(solution)/shard_map/all_to_all | solution.py:56
  75.1 56.8 %all-to-all-start.2 = ((bf16[64,6,2048]{2,1,0:T(8,128)(2,1)}), bf16[64,6,2048]{2,1,0:T(8,128)(2,1)}, u32[]{:S(2)}, u32[]{:S(2)}) async-start(bf16[64,6,2048]{2,1,0:T(8,128)(2,1)} %reshape.672), calls=%async_computation.2 | async-start | bytes 4194304 | tf_op jit(solution)/shard_map/all_to_all | solution.py:56
  131.9 56.8 %all-to-all-start.1 = ((bf16[64,6,2048]{2,1,0:T(8,128)(2,1)}), bf16[64,6,2048]{2,1,0:T(8,128)(2,1)}, u32[]{:S(2)}, u32[]{:S(2)}) async-start(bf16[64,6,2048]{2,1,0:T(8,128)(2,1)} %reshape.665), calls=%async_computation.1 | async-start | bytes 4194304 | tf_op jit(solution)/shard_map/all_to_all | solution.py:63
  156.8 37.5 %copy-start.20 = (f32[1,2,64,8]{2,3,1,0:T(8,128)S(1)}, f32[1,2,64,8]{2,3,1,0:T(8,128)}, u32[]{:S(2)}) copy-start(f32[1,2,64,8]{2,3,1,0:T(8,128)} %param.15) | copy-start | bytes 12292
  156.8 38.3 %copy-start.24 = (s32[1,1,32,8]{2,3,1,0:T(8,128)S(1)}, s32[1,1,32,8]{2,3,1,0:T(8,128)}, u32[]{:S(2)}) copy-start(s32[1,1,32,8]{2,3,1,0:T(8,128)} %get-tuple-element.13) | copy-start | bytes 3076
  188.7 56.8 %all-to-all-start.3 = ((bf16[64,6,2048]{2,1,0:T(8,128)(2,1)}), bf16[64,6,2048]{2,1,0:T(8,128)(2,1)}, u32[]{:S(2)}, u32[]{:S(2)}) async-start(bf16[64,6,2048]{2,1,0:T(8,128)(2,1)} %reshape.674), calls=%async_computation.3 | async-start | bytes 4194304 | tf_op jit(solution)/shard_map/all_to_all | solution.py:63
  195.3 6.9 %copy-start.13 = (s32[1,1,32,8]{3,2,1,0:T(8,128)}, s32[1,1,32,8]{3,2,1,0:T(8,128)S(1)}, u32[]{:S(2)}) copy-start(s32[1,1,32,8]{3,2,1,0:T(8,128)S(1)} %copy.66) | copy-start | bytes 3076
  197.6 4.5 copy-start.10
  202.1 1.9 copy-start.2
  202.1 1.9 copy-start.5
  249.3 1.9 copy-start.3
  249.3 2.0 copy-start.9
  251.2 4.4 copy-start.14
  251.3 4.4 copy-start.19
  251.3 9.6 %copy-start.12 = (bf16[1,64,2048]{2,1,0:T(8,128)(2,1)S(1)}, bf16[1,64,2048]{2,1,0:T(8,128)(2,1)}, u32[]{:S(2)}) copy-start(bf16[1,64,2048]{2,1,0:T(8,128)(2,1)} %param.9) | copy-start | bytes 786436
  251.3 9.8 %copy-start.18 = (f32[1,2048]{1,0:T(1,128)S(1)}, f32[1,2048]{1,0:T(1,128)}, u32[]{:S(2)}) copy-start(f32[1,2048]{1,0:T(1,128)} %copy-done.17) | copy-start | bytes 24580
  252.4 8.5 %collective-permute-start = (bf16[64,2048]{1,0:T(8,128)(2,1)S(1)}, bf16[64,2048]{1,0:T(8,128)(2,1)S(1)}, u32[]{:S(2)}, u32[]{:S(2)}) collective-permute-start(bf16[64,2048]{1,0:T(8,128)(2,1)S(1)} %get-tuple-element.8), channel_id=1, source_target_pairs={{0,64},{64,128},{128,192},{1,65},{65,129},{129,193},{2,66},{66,130... | collective-permute-start | bytes 786440 | tf_op jit(solution)/shard_map/ppermute | solution.py:15
  261.2 0.7 copy-start.7
  267.4 7.2 %copy-start.21 = (s32[1,1,32,8]{2,3,1,0:T(8,128)S(1)}, s32[1,1,32,8]{2,3,1,0:T(8,128)}, u32[]{:S(2)}) copy-start(s32[1,1,32,8]{2,3,1,0:T(8,128)} %get-tuple-element.16) | copy-start | bytes 3076
  267.4 58.4 %all-to-all-start.4 = ((bf16[64,6,2048]{2,1,0:T(8,128)(2,1)}), bf16[64,6,2048]{2,1,0:T(8,128)(2,1)}, u32[]{:S(2)}, u32[]{:S(2)}) async-start(bf16[64,6,2048]{2,1,0:T(8,128)(2,1)} %reshape.681), calls=%async_computation.4 | async-start | bytes 4194304 | tf_op jit(solution)/shard_map/all_to_all | solution.py:56
  325.7 57.0 %all-to-all-start.6 = ((bf16[64,6,2048]{2,1,0:T(8,128)(2,1)}), bf16[64,6,2048]{2,1,0:T(8,128)(2,1)}, u32[]{:S(2)}, u32[]{:S(2)}) async-start(bf16[64,6,2048]{2,1,0:T(8,128)(2,1)} %reshape.690), calls=%async_computation.6 | async-start | bytes 4194304 | tf_op jit(solution)/shard_map/all_to_all | solution.py:56
  382.7 56.8 %all-to-all-start.5 = ((bf16[64,6,2048]{2,1,0:T(8,128)(2,1)}), bf16[64,6,2048]{2,1,0:T(8,128)(2,1)}, u32[]{:S(2)}, u32[]{:S(2)}) async-start(bf16[64,6,2048]{2,1,0:T(8,128)(2,1)} %reshape.683), calls=%async_computation.5 | async-start | bytes 4194304 | tf_op jit(solution)/shard_map/all_to_all | solution.py:63
  407.5 37.7 %copy-start.23 = (f32[32,8]{0,1:T(8,128)S(1)}, f32[32,8]{0,1:T(8,128)}, u32[]{:S(2)}) copy-start(f32[32,8]{0,1:T(8,128)} %get-tuple-element.9) | copy-start | bytes 3076
  407.5 37.7 %copy-start.22 = (f32[32,8]{0,1:T(8,128)S(1)}, f32[32,8]{0,1:T(8,128)}, u32[]{:S(2)}) copy-start(f32[32,8]{0,1:T(8,128)} %get-tuple-element.12) | copy-start | bytes 3076
  439.5 56.8 %all-to-all-start.7 = ((bf16[64,6,2048]{2,1,0:T(8,128)(2,1)}), bf16[64,6,2048]{2,1,0:T(8,128)(2,1)}, u32[]{:S(2)}, u32[]{:S(2)}) async-start(bf16[64,6,2048]{2,1,0:T(8,128)(2,1)} %reshape.692), calls=%async_computation.7 | async-start | bytes 4194304 | tf_op jit(solution)/shard_map/all_to_all | solution.py:63
  445.5 4.5 copy-start.11
  450.0 1.9 copy-start.4
  500.1 1.9 copy-start.1
  500.1 2.0 copy-start.8
  502.0 1.0 copy-start.6
  (4 other events, 2.3 us)
where the time goes:
time: 507 us; the launch traced here: 504 us
  waiting for transfers between devices  291 us (57%)
  local copies, waits for them, and re-layouts  73.9 us (15%)
  matrix products  65.8 us (13%)
  starting transfers between devices  56.5 us (11%)
  other arithmetic  16.2 us (3%)
    all_to_all x4, waiting for transfers between devices, mix_block(): lax.all_to_all(result.reshape(row_shape), 'expert', split_axis=0, concat_...  147 us
    all_to_all x4, waiting for transfers between devices, mix_block(): lax.all_to_all(outgoing, 'expert', split_axis=0, concat_axis=0, tiled=True)  139 us
    all_to_all x4, starting transfers between devices, mix_block(): lax.all_to_all(outgoing, 'expert', split_axis=0, concat_axis=0, tiled=True)  30.7 us
    dot_general x4, matrix products, mix_block(): jnp.dot(hidden, down_w, preferred_element_type=jnp.float32)  27.7 us
    all_to_all x4, starting transfers between devices, mix_block(): lax.all_to_all(result.reshape(row_shape), 'expert', split_axis=0, concat_...  22.6 us
    dot_general x4, matrix products, mix_block(): gate_sum = jnp.dot(inputs, gate_w, preferred_element_type=jnp.float32)  19.2 us
    reshape x4, local copies, waits for them, and re-layouts, mix_block(): returned = returned.reshape(slot_total, model_width)  14.9 us
    reshape x4, local copies, waits for them, and re-layouts, mix_block(): inputs = received.reshape(-1, row_shape[-1])  14.8 us
  transfers between devices with their start and end apart: 9, of which 9 were waited for; matrix products, arithmetic and copies ran while one was open for 24% of the time, Pallas kernels for 0%

commit v1 on v0

--- a/solution.py
+++ b/solution.py
@@ -7,6 +7,9 @@
 
 
 EPSILON = 1e-06
+BLOCK_ROWS = 32
+LANE = 128
+SUBLANE = 8
 
 
 def passed_along(x, axis, by):
@@ -35,14 +38,29 @@
     return positions.reshape(group_count * row_count, top_count)
 
 
-def mix_block(
-    hidden_rows, normed_rows, route_ids, combine, gate_w, up_w, down_w, experts, capacity
-):
-    group_count = route_ids.shape[0]
-    row_count = hidden_rows.shape[0]
+def wire_shape(rows, width):
+    total = rows * width
+    if total % (SUBLANE * LANE) == 0:
+        return (SUBLANE, total // SUBLANE)
+    return (rows, width)
+
+
+def exchange(chunks):
+    experts, rows, width = chunks.shape
+    wire = chunks.reshape((experts,) + wire_shape(rows, width))
+    moved = lax.all_to_all(wire, "expert", split_axis=0, concat_axis=0, tiled=True)
+    return moved.reshape(experts, rows, width)
+
+
+def apply_layer(hidden_rows, norm_gain, route_ids, combine, gate_w, up_w, down_w, experts):
+    normed_rows = rms_normed(hidden_rows, norm_gain)
+    row_count, model_width = hidden_rows.shape
     top_count = route_ids.shape[-1]
-    model_width = hidden_rows.shape[1]
-    positions = slot_table(route_ids, experts, capacity)
+    block_rows = min(BLOCK_ROWS, row_count)
+    group_count = row_count // block_rows
+    capacity = max(2, min(block_rows, block_rows * top_count // experts * 3 // 2))
+    groups = route_ids.reshape(group_count, block_rows, top_count)
+    positions = slot_table(groups, experts, capacity)
     slot_total = experts * group_count * capacity
     flat_slots = positions.reshape(-1)
     pick_table = flat_slots[None, :] == jnp.arange(slot_total, dtype=jnp.int32)[:, None]
@@ -52,17 +70,13 @@
     outgoing = jnp.dot(pick_table, normed_rows, preferred_element_type=jnp.float32).astype(
         jnp.bfloat16
     )
-    outgoing = outgoing.reshape(experts, group_count * capacity, model_width)
-    received = lax.all_to_all(outgoing, "expert", split_axis=0, concat_axis=0, tiled=True)
-    row_shape = received.shape
-    inputs = received.reshape(-1, row_shape[-1])
+    received = exchange(outgoing.reshape(experts, group_count * capacity, model_width))
+    inputs = received.reshape(slot_total, model_width)
     gate_sum = jnp.dot(inputs, gate_w, preferred_element_type=jnp.float32)
     up_sum = jnp.dot(inputs, up_w, preferred_element_type=jnp.float32)
     hidden = (jax.nn.silu(gate_sum) * up_sum).astype(jnp.bfloat16)
     result = jnp.dot(hidden, down_w, preferred_element_type=jnp.float32).astype(jnp.bfloat16)
-    returned = lax.all_to_all(
-        result.reshape(row_shape), "expert", split_axis=0, concat_axis=0, tiled=True
-    )
+    returned = exchange(result.reshape(experts, group_count * capacity, model_width))
     returned = returned.reshape(slot_total, model_width)
     residual = hidden_rows.astype(jnp.float32)
     hit_table = (flat_slots[:, None] == jnp.arange(slot_total, dtype=jnp.int32)[None, :]).astype(
@@ -76,36 +90,6 @@
     branch_sum = jnp.dot(mixing_high, returned, preferred_element_type=jnp.float32)
     branch_sum = branch_sum + jnp.dot(mixing_low, returned, preferred_element_type=jnp.float32)
     return (residual + branch_sum).astype(jnp.bfloat16)
-
-
-def apply_layer(hidden_rows, norm_gain, route_ids, combine, gate_w, up_w, down_w, experts):
-    normed_rows = rms_normed(hidden_rows, norm_gain)
-    half_rows = hidden_rows.shape[0] // 2
-    top_count = route_ids.shape[-1]
-    capacity = max(2, min(half_rows, half_rows * top_count // experts * 3 // 2))
-    first_part = mix_block(
-        hidden_rows[:half_rows],
-        normed_rows[:half_rows],
-        route_ids[:half_rows][None],
-        combine[:half_rows],
-        gate_w,
-        up_w,
-        down_w,
-        experts,
-        capacity,
-    )
-    second_part = mix_block(
-        hidden_rows[half_rows:],
-        normed_rows[half_rows:],
-        route_ids[half_rows:][None],
-        combine[half_rows:],
-        gate_w,
-        up_w,
-        down_w,
-        experts,
-        capacity,
-    )
-    return jnp.concatenate([first_part, second_part], axis=0)
 
 
 def local(in_flight, entering, norm_gain, w_gate, w_up, w_down, routes, combine_weight):

time: 507 us -> 443 us (0.87)
  blocking collectives: 0 us -> 166 us
  waiting for transfers between devices: 291 us -> 151 us
  starting transfers between devices: 56.5 us -> 14.9 us
  local copies, waits for them, and re-layouts: 73.9 us -> 48.6 us
  matrix products: 65.8 us -> 49.7 us
  other arithmetic: 16.2 us -> 10.5 us
    all_to_all x0 -> x2, blocking collectives: none -> 166 us  [exchange(): lax.all_to_all(wire, 'expert', split_axis=0, concat_axis=0, tiled=True)]
    all_to_all x8 -> x2, waiting for transfers between devices: 286 us -> 146 us  [exchange(): lax.all_to_all(wire, 'expert', split_axis=0, concat_axis=0, tiled=True)]
    reshape x17 -> x2, local copies, waits for them, and re-layouts: 59.2 us -> 0.18 us  [slot_table(): jnp.sum(earlier_marks * expert_marks, axis=-1)]
    all_to_all x8 -> x2, starting transfers between devices: 53.3 us -> 11.7 us  [exchange(): lax.all_to_all(wire, 'expert', split_axis=0, concat_axis=0, tiled=True)]
    another operation x22 -> x11, local copies, waits for them, and re-layouts: 5.57 us -> 46.2 us  [the longest x4 23.1 us: exchange(): wire = chunks.reshape((experts,) + wire_shape(rows, width))]
    dot_general x20 -> x10, matrix products: 65.8 us -> 49.7 us  [the longest x2 22.1 us: apply_layer(): jnp.dot(hidden, down_w, preferred_element_type=jnp.float32)]
  transfers between devices with their start and end apart: 9 -> 3, of which waited for: 9 -> 3; matrix products, arithmetic and copies ran while one was open for 24% -> 1% of each run, Pallas kernels for 0% -> 0%
where the time goes in v1:
time: 443 us; the launch traced here: 441 us
  blocking collectives  166 us (37%)
  waiting for transfers between devices  151 us (34%)
  matrix products  49.7 us (11%)
  local copies, waits for them, and re-layouts  48.6 us (11%)
  starting transfers between devices  14.9 us (3%)
  other arithmetic  10.5 us (2%)
    all_to_all x2, blocking collectives, exchange(): lax.all_to_all(wire, 'expert', split_axis=0, concat_axis=0, tiled=True)  166 us
    all_to_all x2, waiting for transfers between devices, exchange(): lax.all_to_all(wire, 'expert', split_axis=0, concat_axis=0, tiled=True)  146 us
    another operation x4, local copies, waits for them, and re-layouts, exchange(): wire = chunks.reshape((experts,) + wire_shape(rows, width))  23.1 us
    dot_general x2, matrix products, apply_layer(): jnp.dot(hidden, down_w, preferred_element_type=jnp.float32)  22.1 us
    dot_general x2, matrix products, apply_layer(): up_sum = jnp.dot(inputs, up_w, preferred_element_type=jnp.float32)  13.7 us
    all_to_all x2, starting transfers between devices, exchange(): lax.all_to_all(wire, 'expert', split_axis=0, concat_axis=0, tiled=True)  11.7 us
    another operation x2, local copies, waits for them, and re-layouts, apply_layer(): inputs = received.reshape(slot_total, model_width)  11.4 us
    another operation x2, local copies, waits for them, and re-layouts, apply_layer(): returned = returned.reshape(slot_total, model_width)  11.4 us
  transfers between devices with their start and end apart: 3, of which 3 were waited for; matrix products, arithmetic and copies ran while one was open for 1% of the time, Pallas kernels for 0%

profile of v1, /device:TPU:16, one launch (start us, length us, event | category | flops | bytes accessed | tf_op | source)
XLA Modules:
  0.0 441.2 jit_solution(6869264069083255077)
XLA Ops:
  0.0 0.9 fusion.56
  1.4 1.2 reduce-window.14
  3.2 1.2 reduce-window.16
  6.4 1.1 fusion.26
  7.5 3.7 convolution_convert_fusion.3
  11.2 5.8 %reshape_reshape.24 = bf16[64,8,3072]{2,1,0:T(8,128)(2,1)} reshape(bf16[768,2048]{1,0:T(8,128)(2,1)} %convolution_convert_fusion.3) | data formatting | bytes 6291456 | tf_op jit(solution)/shard_map/reshape;reshape | solution.py:50
  16.9 85.9 %all_to_all.20 = bf16[64,8,3072]{2,1,0:T(8,128)(2,1)} all-to-all(bf16[64,8,3072]{2,1,0:T(8,128)(2,1)} %reshape_reshape.24), channel_id=1, replica_groups=mesh['section'=4,'expert'=64] {'expert'}, dimensions={0} | all-to-all | bytes 6291456 | tf_op jit(solution)/shard_map/all_to_all | solution.py:51
  102.8 5.7 %reshape_reshape.25 = bf16[768,2048]{1,0:T(8,128)(2,1)} reshape(bf16[64,8,3072]{2,1,0:T(8,128)(2,1)} %all_to_all.20) | data formatting | bytes 6291456 | tf_op jit(solution)/shard_map/reshape;reshape | solution.py:74
  108.5 6.9 %fusion.4 = f32[768,768]{1,0:T(8,128)} fusion(bf16[768,2048]{1,0:T(8,128)(2,1)} %reshape_reshape.25, bf16[1,1,2048,768]{3,2,1,0:T(8,128)(2,1)} %param.12), kind=kOutput, calls=%fused_computation.8 | convolution fusion | flops 2415919104 | bytes 8650752 | tf_op jit(solution)/shard_map/dot_general | solution.py:76
  115.4 11.0 %convolution_convert_fusion.2 = bf16[768,2048]{1,0:T(8,128)(2,1)} fusion(bf16[1,1,768,2048]{3,2,1,0:T(8,128)(2,1)S(1)} %copy-done, f32[768,768]{1,0:T(8,128)} %fusion.4, bf16[768,2048]{1,0:T(8,128)(2,1)} %reshape_reshape.25, bf16[1,1,2048,768]{3,2,1,0:T(8,128)(2,1)} %param.11), kind=kOutput, calls=%fused_computation.2 | convolution fusion | flops 4836950016 | bytes 14942208 | tf_op jit(solution)/shard_map/dot_general | solution.py:78
  126.4 5.8 %reshape_reshape.26 = bf16[64,8,3072]{2,1,0:T(8,128)(2,1)} reshape(bf16[768,2048]{1,0:T(8,128)(2,1)} %convolution_convert_fusion.2) | data formatting | bytes 6291456 | tf_op jit(solution)/shard_map/reshape;reshape | solution.py:50
  132.2 5.9 %all-to-all-start.1 = ((bf16[64,8,3072]{2,1,0:T(8,128)(2,1)}), bf16[64,8,3072]{2,1,0:T(8,128)(2,1)}, u32[]{:S(2)}, u32[]{:S(2)}) async-start(bf16[64,8,3072]{2,1,0:T(8,128)(2,1)} %reshape_reshape.26), calls=%async_computation.1 | async-start | bytes 6291456 | tf_op jit(solution)/shard_map/all_to_all | solution.py:51
  138.8 73.1 %all-to-all-done.1 = bf16[64,8,3072]{2,1,0:T(8,128)(2,1)} async-done(((bf16[64,8,3072]{2,1,0:T(8,128)(2,1)}), bf16[64,8,3072]{2,1,0:T(8,128)(2,1)}, u32[]{:S(2)}, u32[]{:S(2)}) %all-to-all-start.1) | async-done | bytes 3145760 | tf_op jit(solution)/shard_map/all_to_all | solution.py:51
  211.9 5.7 %reshape_reshape.27 = bf16[768,2048]{1,0:T(8,128)(2,1)} reshape(bf16[64,8,3072]{2,1,0:T(8,128)(2,1)} %all-to-all-done.1) | data formatting | bytes 6291456 | tf_op jit(solution)/shard_map/reshape;reshape | solution.py:80
  217.6 2.7 fusion.50
  220.4 1.4 fusion.12
  221.8 3.2 collective-permute-start
  225.5 5.4 %collective-permute-done = bf16[64,2048]{1,0:T(8,128)(2,1)} collective-permute-done((bf16[64,2048]{1,0:T(8,128)(2,1)}, bf16[64,2048]{1,0:T(8,128)(2,1)}, u32[]{:S(2)}, u32[]{:S(2)}) %collective-permute-start) | collective-permute-done | bytes 262176 | tf_op jit(solution)/shard_map/ppermute | solution.py:18
  231.0 1.2 fusion.23
  232.2 2.8 convolution_convert_fusion.1
  235.0 5.8 %reshape_reshape.28 = bf16[64,8,3072]{2,1,0:T(8,128)(2,1)} reshape(bf16[768,2048]{1,0:T(8,128)(2,1)} %convolution_convert_fusion.1) | data formatting | bytes 6291456 | tf_op jit(solution)/shard_map/reshape;reshape | solution.py:50
  240.7 80.4 %all_to_all.21 = bf16[64,8,3072]{2,1,0:T(8,128)(2,1)} all-to-all(bf16[64,8,3072]{2,1,0:T(8,128)(2,1)} %reshape_reshape.28), channel_id=1, replica_groups=mesh['section'=4,'expert'=64] {'expert'}, dimensions={0} | all-to-all | bytes 6291456 | tf_op jit(solution)/shard_map/all_to_all | solution.py:51
  321.2 5.7 %reshape_reshape.29 = bf16[768,2048]{1,0:T(8,128)(2,1)} reshape(bf16[64,8,3072]{2,1,0:T(8,128)(2,1)} %all_to_all.21) | data formatting | bytes 6291456 | tf_op jit(solution)/shard_map/reshape;reshape | solution.py:74
  326.9 6.9 %fusion.2 = f32[768,768]{1,0:T(8,128)} fusion(bf16[768,2048]{1,0:T(8,128)(2,1)} %reshape_reshape.29, bf16[1,1,2048,768]{3,2,1,0:T(8,128)(2,1)} %param.12), kind=kOutput, calls=%fused_computation.6 | convolution fusion | flops 2415919104 | bytes 8650752 | tf_op jit(solution)/shard_map/dot_general | solution.py:76
  333.7 11.0 %convolution_convert_fusion = bf16[768,2048]{1,0:T(8,128)(2,1)} fusion(bf16[1,1,768,2048]{3,2,1,0:T(8,128)(2,1)S(1)} %copy-done, f32[768,768]{1,0:T(8,128)} %fusion.2, bf16[768,2048]{1,0:T(8,128)(2,1)} %reshape_reshape.29, bf16[1,1,2048,768]{3,2,1,0:T(8,128)(2,1)} %param.11), kind=kOutput, calls=%fused_computation | convolution fusion | flops 4836950016 | bytes 14942208 | tf_op jit(solution)/shard_map/dot_general | solution.py:78
  344.8 5.8 %reshape_reshape.30 = bf16[64,8,3072]{2,1,0:T(8,128)(2,1)} reshape(bf16[768,2048]{1,0:T(8,128)(2,1)} %convolution_convert_fusion) | data formatting | bytes 6291456 | tf_op jit(solution)/shard_map/reshape;reshape | solution.py:50
  350.6 5.8 %all-to-all-start.3 = ((bf16[64,8,3072]{2,1,0:T(8,128)(2,1)}), bf16[64,8,3072]{2,1,0:T(8,128)(2,1)}, u32[]{:S(2)}, u32[]{:S(2)}) async-start(bf16[64,8,3072]{2,1,0:T(8,128)(2,1)} %reshape_reshape.30), calls=%async_computation.3 | async-start | bytes 6291456 | tf_op jit(solution)/shard_map/all_to_all | solution.py:51
  356.5 1.2 select_reduce_fusion
  357.7 72.4 %all-to-all-done.3 = bf16[64,8,3072]{2,1,0:T(8,128)(2,1)} async-done(((bf16[64,8,3072]{2,1,0:T(8,128)(2,1)}), bf16[64,8,3072]{2,1,0:T(8,128)(2,1)}, u32[]{:S(2)}, u32[]{:S(2)}) %all-to-all-start.3) | async-done | bytes 3145760 | tf_op jit(solution)/shard_map/all_to_all | solution.py:51
  430.1 5.7 %reshape_reshape.31 = bf16[768,2048]{1,0:T(8,128)(2,1)} reshape(bf16[64,8,3072]{2,1,0:T(8,128)(2,1)} %all-to-all-done.3) | data formatting | bytes 6291456 | tf_op jit(solution)/shard_map/reshape;reshape | solution.py:80
  435.8 2.8 fusion.47
  439.4 1.8 maximum_bitcast_fusion
  (44 shorter events, 5.2 us)
Async XLA Ops:
  0.0 115.4 %copy-start = (bf16[1,1,768,2048]{3,2,1,0:T(8,128)(2,1)S(1)}, bf16[1,1,768,2048]{3,2,1,0:T(8,128)(2,1)}, u32[]{:S(2)}) copy-start(bf16[1,1,768,2048]{3,2,1,0:T(8,128)(2,1)} %param.13) | copy-start | bytes 9437188
  132.2 5.9 %copy-start.5 = (f32[1,2,64,8]{2,3,1,0:T(8,128)S(1)}, f32[1,2,64,8]{2,3,1,0:T(8,128)}, u32[]{:S(2)}) copy-start(f32[1,2,64,8]{2,3,1,0:T(8,128)} %param.15) | copy-start | bytes 12292
  132.2 79.7 %all-to-all-start.1 = ((bf16[64,8,3072]{2,1,0:T(8,128)(2,1)}), bf16[64,8,3072]{2,1,0:T(8,128)(2,1)}, u32[]{:S(2)}, u32[]{:S(2)}) async-start(bf16[64,8,3072]{2,1,0:T(8,128)(2,1)} %reshape_reshape.26), calls=%async_computation.1 | async-start | bytes 6291456 | tf_op jit(solution)/shard_map/all_to_all | solution.py:51
  217.6 2.8 copy-start.2
  217.6 2.8 copy-start.3
  221.8 9.2 %collective-permute-start = (bf16[64,2048]{1,0:T(8,128)(2,1)}, bf16[64,2048]{1,0:T(8,128)(2,1)}, u32[]{:S(2)}, u32[]{:S(2)}) collective-permute-start(bf16[64,2048]{1,0:T(8,128)(2,1)} %fusion.12), channel_id=1, source_target_pairs={{0,64},{64,128},{128,192},{1,65},{65,129},{129,193},{2,66},{66,130... | collective-permute-start | bytes 786440 | tf_op jit(solution)/shard_map/ppermute | solution.py:18
  350.6 79.5 %all-to-all-start.3 = ((bf16[64,8,3072]{2,1,0:T(8,128)(2,1)}), bf16[64,8,3072]{2,1,0:T(8,128)(2,1)}, u32[]{:S(2)}, u32[]{:S(2)}) async-start(bf16[64,8,3072]{2,1,0:T(8,128)(2,1)} %reshape_reshape.30), calls=%async_computation.3 | async-start | bytes 6291456 | tf_op jit(solution)/shard_map/all_to_all | solution.py:51
  435.8 2.9 copy-start.1
  435.8 2.9 copy-start.4

commit v2 on v1

--- a/solution.py
+++ b/solution.py
@@ -8,7 +8,6 @@
 
 EPSILON = 1e-06
 BLOCK_ROWS = 32
-LANE = 128
 SUBLANE = 8
 
 
@@ -38,18 +37,15 @@
     return positions.reshape(group_count * row_count, top_count)
 
 
-def wire_shape(rows, width):
-    total = rows * width
-    if total % (SUBLANE * LANE) == 0:
-        return (SUBLANE, total // SUBLANE)
-    return (rows, width)
-
-
-def exchange(chunks):
-    experts, rows, width = chunks.shape
-    wire = chunks.reshape((experts,) + wire_shape(rows, width))
-    moved = lax.all_to_all(wire, "expert", split_axis=0, concat_axis=0, tiled=True)
-    return moved.reshape(experts, rows, width)
+def wire_slots(experts, width):
+    extra = width - SUBLANE
+    pieces = SUBLANE // extra
+    row = jnp.arange(SUBLANE, dtype=jnp.int32)
+    base = jnp.arange(experts, dtype=jnp.int32)[:, None] * width
+    full_slot = (base + row[None, :]).reshape(-1)
+    part_slot = (base + SUBLANE + row[None, :] % extra).reshape(-1)
+    part_piece = jnp.broadcast_to(row[None, :] // extra, (experts, SUBLANE)).reshape(-1)
+    return full_slot, part_slot, part_piece, pieces
 
 
 def apply_layer(hidden_rows, norm_gain, route_ids, combine, gate_w, up_w, down_w, experts):
@@ -59,36 +55,100 @@
     block_rows = min(BLOCK_ROWS, row_count)
     group_count = row_count // block_rows
     capacity = max(2, min(block_rows, block_rows * top_count // experts * 3 // 2))
+    width = group_count * capacity
     groups = route_ids.reshape(group_count, block_rows, top_count)
     positions = slot_table(groups, experts, capacity)
-    slot_total = experts * group_count * capacity
-    flat_slots = positions.reshape(-1)
-    pick_table = flat_slots[None, :] == jnp.arange(slot_total, dtype=jnp.int32)[:, None]
-    pick_table = jnp.sum(
-        pick_table.reshape(slot_total, row_count, top_count).astype(jnp.int32), axis=-1
-    ).astype(jnp.bfloat16)
-    outgoing = jnp.dot(pick_table, normed_rows, preferred_element_type=jnp.float32).astype(
-        jnp.bfloat16
+    full_slot, part_slot, part_piece, pieces = wire_slots(experts, width)
+    piece_width = model_width // pieces
+    wire_rows = experts * SUBLANE
+
+    hits_full = positions[:, :, None] == full_slot[None, None, :]
+    hits_part = positions[:, :, None] == part_slot[None, None, :]
+    pick_full = jnp.sum(hits_full.astype(jnp.int32), axis=1).astype(jnp.bfloat16).T
+    pick_part = jnp.sum(hits_part.astype(jnp.int32), axis=1).astype(jnp.bfloat16).T
+    send_full = jnp.dot(pick_full, normed_rows, preferred_element_type=jnp.float32)
+    send_part = jnp.zeros((wire_rows, piece_width), jnp.float32)
+    for piece in range(pieces):
+        chosen = (part_piece == piece)[:, None]
+        lanes = normed_rows[:, piece * piece_width:(piece + 1) * piece_width]
+        send_part = send_part + jnp.dot(
+            jnp.where(chosen, pick_part, jnp.zeros_like(pick_part)),
+            lanes,
+            preferred_element_type=jnp.float32,
+        )
+    outgoing = jnp.concatenate(
+        [
+            send_full.astype(jnp.bfloat16).reshape(experts, SUBLANE, model_width),
+            send_part.astype(jnp.bfloat16).reshape(experts, SUBLANE, piece_width),
+        ],
+        axis=-1,
     )
-    received = exchange(outgoing.reshape(experts, group_count * capacity, model_width))
-    inputs = received.reshape(slot_total, model_width)
+    received = lax.all_to_all(outgoing, "expert", split_axis=0, concat_axis=0, tiled=True)
+
+    extra = width - SUBLANE
+    full_rows = received[:, :, :model_width].reshape(wire_rows, model_width)
+    part_rows = received[:, :, model_width:].reshape(wire_rows, piece_width)
+    joined_row = (
+        jnp.arange(experts, dtype=jnp.int32)[:, None] * extra
+        + jnp.arange(extra, dtype=jnp.int32)[None, :]
+    ).reshape(-1)
+    joined_count = experts * extra
+    wire_joined = (
+        jnp.arange(experts, dtype=jnp.int32)[:, None] * extra
+        + jnp.arange(SUBLANE, dtype=jnp.int32)[None, :] % extra
+    ).reshape(-1)
+    gather_pieces = []
+    spread = []
+    for piece in range(pieces):
+        table = (wire_joined[None, :] == joined_row[:, None]) & (part_piece == piece)[None, :]
+        table = table.astype(jnp.bfloat16)
+        spread.append(table)
+        gather_pieces.append(
+            jnp.dot(table, part_rows, preferred_element_type=jnp.float32).astype(jnp.bfloat16)
+        )
+    joined_rows = jnp.concatenate(gather_pieces, axis=-1)
+    inputs = jnp.concatenate([full_rows, joined_rows], axis=0)
     gate_sum = jnp.dot(inputs, gate_w, preferred_element_type=jnp.float32)
     up_sum = jnp.dot(inputs, up_w, preferred_element_type=jnp.float32)
     hidden = (jax.nn.silu(gate_sum) * up_sum).astype(jnp.bfloat16)
     result = jnp.dot(hidden, down_w, preferred_element_type=jnp.float32).astype(jnp.bfloat16)
-    returned = exchange(result.reshape(experts, group_count * capacity, model_width))
-    returned = returned.reshape(slot_total, model_width)
+    result_full = result[:wire_rows]
+    result_joined = result[wire_rows:]
+    back_part = jnp.zeros((wire_rows, piece_width), jnp.float32)
+    for piece in range(pieces):
+        back_part = back_part + jnp.dot(
+            spread[piece].T,
+            result_joined[:, piece * piece_width:(piece + 1) * piece_width],
+            preferred_element_type=jnp.float32,
+        )
+    back = jnp.concatenate(
+        [
+            result_full.reshape(experts, SUBLANE, model_width),
+            back_part.astype(jnp.bfloat16).reshape(experts, SUBLANE, piece_width),
+        ],
+        axis=-1,
+    )
+    returned = lax.all_to_all(back, "expert", split_axis=0, concat_axis=0, tiled=True)
+    back_full = returned[:, :, :model_width].reshape(wire_rows, model_width)
+    back_rows = returned[:, :, model_width:].reshape(wire_rows, piece_width)
+
+    weights = combine[:, :, None]
+    mix_full = jnp.sum(jnp.where(hits_full, weights, 0.0), axis=1)
+    mix_part = jnp.sum(jnp.where(hits_part, weights, 0.0), axis=1)
+
+    def mixed(mix, rows):
+        high = mix.astype(jnp.bfloat16)
+        low = (mix - high.astype(jnp.float32)).astype(jnp.bfloat16)
+        total = jnp.dot(high, rows, preferred_element_type=jnp.float32)
+        return total + jnp.dot(low, rows, preferred_element_type=jnp.float32)
+
+    branch_full = mixed(mix_full, back_full)
+    branch_part = [
+        mixed(jnp.where((part_piece == piece)[None, :], mix_part, 0.0), back_rows)
+        for piece in range(pieces)
+    ]
+    branch_sum = branch_full + jnp.concatenate(branch_part, axis=-1)
     residual = hidden_rows.astype(jnp.float32)
-    hit_table = (flat_slots[:, None] == jnp.arange(slot_total, dtype=jnp.int32)[None, :]).astype(
-        jnp.float32
-    )
-    mixing = jnp.sum(
-        hit_table.reshape(row_count, top_count, slot_total) * combine[:, :, None], axis=1
-    )
-    mixing_high = mixing.astype(jnp.bfloat16)
-    mixing_low = (mixing - mixing_high.astype(jnp.float32)).astype(jnp.bfloat16)
-    branch_sum = jnp.dot(mixing_high, returned, preferred_element_type=jnp.float32)
-    branch_sum = branch_sum + jnp.dot(mixing_low, returned, preferred_element_type=jnp.float32)
     return (residual + branch_sum).astype(jnp.bfloat16)
 
 

time: 443 us -> 423 us (0.955)
  local copies, waits for them, and re-layouts: 48.6 us -> 12.8 us
  matrix products: 49.7 us -> 61.2 us
  other arithmetic: 10.5 us -> 18.1 us
  blocking collectives: 166 us -> 159 us
  starting transfers between devices: 14.9 us -> 21.5 us
    another operation x11 -> x3, local copies, waits for them, and re-layouts: 46.2 us -> 0.25 us  [the longest x4 23.1 us: exchange(): wire = chunks.reshape((experts,) + wire_shape(rows, width))]
    dot_general x6 -> x26, matrix products: 14 us -> 31.1 us  [the longest x6 7.09 us: mixed(): return total + jnp.dot(low, rows, preferred_element_type=jnp.float32)]
    all_to_all x2, blocking collectives: 166 us -> 159 us  [the longest x1 80.1 us: apply_layer(): lax.all_to_all(outgoing, 'expert', split_axis=0, concat_axis=0, tiled=True)]
    all_to_all x2, starting transfers between devices: 11.7 us -> 18.3 us  [the longest x1 12.3 us: apply_layer(): lax.all_to_all(outgoing, 'expert', split_axis=0, concat_axis=0, tiled=True)]
    dot_general x2, matrix products: 13.7 us -> 8.08 us  [apply_layer(): up_sum = jnp.dot(inputs, up_w, preferred_element_type=jnp.float32)]
    reshape x0 -> x4, local copies, waits for them, and re-layouts: none -> 5.32 us  [the longest x2 3.46 us: apply_layer(): result_full.reshape(experts, SUBLANE, model_width)]
where the time goes in v2:
time: 423 us; the launch traced here: 422 us
  blocking collectives  159 us (38%)
  waiting for transfers between devices  149 us (35%)
  matrix products  61.2 us (14%)
  starting transfers between devices  21.5 us (5%)
  other arithmetic  18.1 us (4%)
  local copies, waits for them, and re-layouts  12.8 us (3%)
    all_to_all x1, blocking collectives, apply_layer(): lax.all_to_all(outgoing, 'expert', split_axis=0, concat_axis=0, tiled=True)  80.1 us
    all_to_all x1, blocking collectives, apply_layer(): lax.all_to_all(back, 'expert', split_axis=0, concat_axis=0, tiled=True)  79.2 us
    all_to_all x1, waiting for transfers between devices, apply_layer(): lax.all_to_all(outgoing, 'expert', split_axis=0, concat_axis=0, tiled=True)  73.3 us
    all_to_all x1, waiting for transfers between devices, apply_layer(): lax.all_to_all(back, 'expert', split_axis=0, concat_axis=0, tiled=True)  69.3 us
    dot_general x2, matrix products, apply_layer(): jnp.dot(hidden, down_w, preferred_element_type=jnp.float32)  22 us
    all_to_all x1, starting transfers between devices, apply_layer(): lax.all_to_all(outgoing, 'expert', split_axis=0, concat_axis=0, tiled=True)  12.3 us
  transfers between devices with their start and end apart: 3, of which 3 were waited for; matrix products, arithmetic and copies ran while one was open for 1% of the time, Pallas kernels for 0%

profile of v2, /device:TPU:16, one launch (start us, length us, event | category | flops | bytes accessed | tf_op | source)
XLA Modules:
  0.0 422.0 jit_solution(3330295411730406363)
XLA Ops:
  8.7 1.8 fusion.36
  12.2 1.9 pad_maximum_fusion
  14.1 12.3 %all-to-all-start = ((bf16[64,8,3072]{2,1,0:T(8,128)(2,1)}), bf16[64,8,3072]{2,1,0:T(8,128)(2,1)}, u32[]{:S(2)}, u32[]{:S(2)}) async-start(bf16[64,8,3072]{2,1,0:T(8,128)(2,1)} %pad_maximum_fusion), calls=%async_computation | async-start | bytes 6291456 | tf_op jit(solution)/shard_map/all_to_all | solution.py:86
  26.8 73.3 %all-to-all-done = bf16[64,8,3072]{2,1,0:T(8,128)(2,1)} async-done(((bf16[64,8,3072]{2,1,0:T(8,128)(2,1)}), bf16[64,8,3072]{2,1,0:T(8,128)(2,1)}, u32[]{:S(2)}, u32[]{:S(2)}) %all-to-all-start) | async-done | bytes 3145760 | tf_op jit(solution)/shard_map/all_to_all | solution.py:86
  100.0 1.7 slice_bitcast_fusion.5
  101.8 2.5 convolution_convert_fusion.7
  104.3 1.9 convolution_convert_fusion.6
  107.0 4.0 fusion.4
  111.1 11.0 %convolution_convert_fusion.1 = bf16[768,2048]{1,0:T(8,128)(2,1)} fusion(bf16[1,1,768,2048]{3,2,1,0:T(8,128)(2,1)S(1)} %copy-done, f32[768,768]{1,0:T(8,128)} %fusion.4, bf16[1,1,2048,768]{3,2,1,0:T(8,128)(2,1)} %param.11, bf16[256,1024]{1,0:T(8,128)(2,1)} %copy-done.17, bf16[256,1024]{1,0:T(8,128)(2,1)} %copy-done.16, bf16[512,2048]{1,0:T(8,128)(2,1)} %copy-done.2), kind=kOutput, calls=%fused_computation.1 | convolution fusion | flops 4846387200 | bytes 14942208 | tf_op jit(solution)/shard_map/dot_general | solution.py:114
  122.1 1.6 fusion.48
  123.7 1.7 slice_bitcast_fusion.4
  125.4 1.6 fusion.27
  127.0 1.9 pad_maximum_fusion.1
  128.9 5.9 %all-to-all-start.1 = ((bf16[64,8,3072]{2,1,0:T(8,128)(2,1)}), bf16[64,8,3072]{2,1,0:T(8,128)(2,1)}, u32[]{:S(2)}, u32[]{:S(2)}) async-start(bf16[64,8,3072]{2,1,0:T(8,128)(2,1)} %pad_maximum_fusion.1), calls=%async_computation.1 | async-start | bytes 6291456 | tf_op jit(solution)/shard_map/all_to_all | solution.py:131
  136.3 2.8 fusion.38
  139.1 69.3 %all-to-all-done.1 = bf16[64,8,3072]{2,1,0:T(8,128)(2,1)} async-done(((bf16[64,8,3072]{2,1,0:T(8,128)(2,1)}), bf16[64,8,3072]{2,1,0:T(8,128)(2,1)}, u32[]{:S(2)}, u32[]{:S(2)}) %all-to-all-start.1) | async-done | bytes 3145760 | tf_op jit(solution)/shard_map/all_to_all | solution.py:131
  209.9 1.5 fusion.43
  211.5 1.6 convolution_add_fusion.5
  213.1 1.5 convolution_add_fusion.4
  214.6 2.1 fusion.19
  216.7 2.8 fusion.17
  219.5 3.2 collective-permute-start
  222.7 6.1 %collective-permute-done = bf16[64,2048]{1,0:T(8,128)(2,1)} collective-permute-done((bf16[64,2048]{1,0:T(8,128)(2,1)}, bf16[64,2048]{1,0:T(8,128)(2,1)}, u32[]{:S(2)}, u32[]{:S(2)}) %collective-permute-start) | collective-permute-done | bytes 262176 | tf_op jit(solution)/shard_map/ppermute | solution.py:17
  230.2 1.6 fusion.11
  234.8 80.1 %all_to_all.20 = bf16[64,8,3072]{2,1,0:T(8,128)(2,1)S(1)} all-to-all(bf16[64,8,3072]{2,1,0:T(8,128)(2,1)S(1)} %pad_maximum_fusion.2), channel_id=1, replica_groups=mesh['section'=4,'expert'=64] {'expert'}, dimensions={0} | all-to-all | bytes 6291456 | tf_op jit(solution)/shard_map/all_to_all | solution.py:86
  318.5 4.0 fusion.2
  322.6 11.0 %convolution_convert_fusion = bf16[768,2048]{1,0:T(8,128)(2,1)} fusion(bf16[1,1,768,2048]{3,2,1,0:T(8,128)(2,1)S(1)} %copy-done, f32[768,768]{1,0:T(8,128)} %fusion.2, bf16[1,1,2048,768]{3,2,1,0:T(8,128)(2,1)} %param.11, bf16[256,1024]{1,0:T(8,128)(2,1)} %copy-done.19, bf16[256,1024]{1,0:T(8,128)(2,1)} %copy-done.18, bf16[512,2048]{1,0:T(8,128)(2,1)} %copy-done.3), kind=kOutput, calls=%fused_computation | convolution fusion | flops 4846387200 | bytes 14942208 | tf_op jit(solution)/shard_map/dot_general | solution.py:114
  333.6 1.6 fusion.47
  335.2 1.7 slice_bitcast_fusion.1
  336.9 1.6 fusion.28
  338.8 79.2 %all_to_all.21 = bf16[64,8,3072]{2,1,0:T(8,128)(2,1)S(1)} all-to-all(bf16[64,8,3072]{2,1,0:T(8,128)(2,1)S(1)} %pad_maximum_fusion.3), channel_id=1, replica_groups=mesh['section'=4,'expert'=64] {'expert'}, dimensions={0} | all-to-all | bytes 6291456 | tf_op jit(solution)/shard_map/all_to_all | solution.py:131
  420.2 1.8 maximum_bitcast_fusion
  (108 shorter events, 24.7 us)
Async XLA Ops:
  0.0 111.1 %copy-start = (bf16[1,1,768,2048]{3,2,1,0:T(8,128)(2,1)S(1)}, bf16[1,1,768,2048]{3,2,1,0:T(8,128)(2,1)}, u32[]{:S(2)}) copy-start(bf16[1,1,768,2048]{3,2,1,0:T(8,128)(2,1)} %param.13) | copy-start | bytes 9437188
  5.3 6.5 %copy-start.11 = (s32[512]{0:T(512)}, s32[512]{0:T(512)S(1)}, u32[]{:S(2)}) copy-start(s32[512]{0:T(512)S(1)} %add.414) | copy-start | bytes 6148
  5.4 6.3 %copy-start.12 = (s32[512]{0:T(512)}, s32[512]{0:T(512)S(1)}, u32[]{:S(2)}) copy-start(s32[512]{0:T(512)S(1)} %add.407) | copy-start | bytes 6148
  7.5 117.9 %copy-start.7 = (pred[512]{0:T(512)(128)(4,1)}, pred[512]{0:T(512)(128)(4,1)S(1)}, u32[]{:S(2)}) copy-start(pred[512]{0:T(512)(128)(4,1)S(1)} %eq.296) | copy-start | bytes 1540
  8.7 2.6 copy-start.5
  8.7 2.6 copy-start.6
  14.1 85.9 %all-to-all-start = ((bf16[64,8,3072]{2,1,0:T(8,128)(2,1)}), bf16[64,8,3072]{2,1,0:T(8,128)(2,1)}, u32[]{:S(2)}, u32[]{:S(2)}) async-start(bf16[64,8,3072]{2,1,0:T(8,128)(2,1)} %pad_maximum_fusion), calls=%async_computation | async-start | bytes 6291456 | tf_op jit(solution)/shard_map/all_to_all | solution.py:86
  26.7 98.7 %copy-start.9 = (s32[256]{0:T(256)}, s32[256]{0:T(256)S(1)}, u32[]{:S(2)}) copy-start(s32[256]{0:T(256)S(1)} %add.422) | copy-start | bytes 3076
  101.8 4.4 %copy-start.2 = (bf16[512,2048]{1,0:T(8,128)(2,1)}, bf16[512,2048]{1,0:T(8,128)(2,1)S(1)}, u32[]{:S(2)}) copy-start(bf16[512,2048]{1,0:T(8,128)(2,1)S(1)} %slice_bitcast_fusion.5) | copy-start | bytes 6291460
  101.8 5.3 %copy-start.14 = (bf16[1,1,2048,768]{3,2,1,0:T(8,128)(2,1)S(1)}, bf16[1,1,2048,768]{3,2,1,0:T(8,128)(2,1)}, u32[]{:S(2)}) copy-start(bf16[1,1,2048,768]{3,2,1,0:T(8,128)(2,1)} %param.12) | copy-start | bytes 9437188
  104.3 1.9 copy-start.16
  106.2 0.8 copy-start.17
  128.9 6.0 %copy-start.13 = (f32[1,2,64,8]{2,3,1,0:T(8,128)S(1)}, f32[1,2,64,8]{2,3,1,0:T(8,128)}, u32[]{:S(2)}) copy-start(f32[1,2,64,8]{2,3,1,0:T(8,128)} %param.15) | copy-start | bytes 12292
  128.9 79.5 %all-to-all-start.1 = ((bf16[64,8,3072]{2,1,0:T(8,128)(2,1)}), bf16[64,8,3072]{2,1,0:T(8,128)(2,1)}, u32[]{:S(2)}, u32[]{:S(2)}) async-start(bf16[64,8,3072]{2,1,0:T(8,128)(2,1)} %pad_maximum_fusion.1), calls=%async_computation.1 | async-start | bytes 6291456 | tf_op jit(solution)/shard_map/all_to_all | solution.py:131
  211.5 5.2 %copy-start.1 = (bf16[1,64,2048]{2,1,0:T(8,128)(2,1)S(1)}, bf16[1,64,2048]{2,1,0:T(8,128)(2,1)}, u32[]{:S(2)}) copy-start(bf16[1,64,2048]{2,1,0:T(8,128)(2,1)} %param.8) | copy-start | bytes 786436
  219.5 9.3 %collective-permute-start = (bf16[64,2048]{1,0:T(8,128)(2,1)}, bf16[64,2048]{1,0:T(8,128)(2,1)}, u32[]{:S(2)}, u32[]{:S(2)}) collective-permute-start(bf16[64,2048]{1,0:T(8,128)(2,1)} %fusion.17), channel_id=1, source_target_pairs={{0,64},{64,128},{128,192},{1,65},{65,129},{129,193},{2,66},{66,130... | collective-permute-start | bytes 786440 | tf_op jit(solution)/shard_map/ppermute | solution.py:17
  314.9 0.6 copy-start.10
  314.9 1.1 copy-start.8
  315.5 1.4 copy-start.3
  315.5 3.0 copy-start.15
  316.0 1.0 copy-start.18
  317.0 0.8 copy-start.19
  418.0 1.2 copy-start.4

commit v3 on v2

--- a/solution.py
+++ b/solution.py
@@ -111,6 +111,7 @@
     gate_sum = jnp.dot(inputs, gate_w, preferred_element_type=jnp.float32)
     up_sum = jnp.dot(inputs, up_w, preferred_element_type=jnp.float32)
     hidden = (jax.nn.silu(gate_sum) * up_sum).astype(jnp.bfloat16)
+    hidden = lax.optimization_barrier(hidden)
     result = jnp.dot(hidden, down_w, preferred_element_type=jnp.float32).astype(jnp.bfloat16)
     result_full = result[:wire_rows]
     result_joined = result[wire_rows:]
@@ -136,15 +137,25 @@
     mix_full = jnp.sum(jnp.where(hits_full, weights, 0.0), axis=1)
     mix_part = jnp.sum(jnp.where(hits_part, weights, 0.0), axis=1)
 
-    def mixed(mix, rows):
+    def split(mix):
         high = mix.astype(jnp.bfloat16)
         low = (mix - high.astype(jnp.float32)).astype(jnp.bfloat16)
-        total = jnp.dot(high, rows, preferred_element_type=jnp.float32)
-        return total + jnp.dot(low, rows, preferred_element_type=jnp.float32)
-
-    branch_full = mixed(mix_full, back_full)
+        return [high, low]
+
+    full_parts = split(mix_full)
+    full_sum = jnp.dot(
+        jnp.concatenate(full_parts, axis=0), back_full, preferred_element_type=jnp.float32
+    )
+    branch_full = full_sum[:row_count] + full_sum[row_count:]
+    part_parts = []
+    for piece in range(pieces):
+        part_parts += split(jnp.where((part_piece == piece)[None, :], mix_part, 0.0))
+    part_sum = jnp.dot(
+        jnp.concatenate(part_parts, axis=0), back_rows, preferred_element_type=jnp.float32
+    )
     branch_part = [
-        mixed(jnp.where((part_piece == piece)[None, :], mix_part, 0.0), back_rows)
+        part_sum[(2 * piece) * row_count:(2 * piece + 1) * row_count]
+        + part_sum[(2 * piece + 1) * row_count:(2 * piece + 2) * row_count]
         for piece in range(pieces)
     ]
     branch_sum = branch_full + jnp.concatenate(branch_part, axis=-1)

time: 423 us -> 394 us (0.931)
  blocking collectives: 159 us -> 80.1 us
  waiting for transfers between devices: 149 us -> 221 us
  matrix products: 61.2 us -> 36.4 us
  local copies, waits for them, and re-layouts: 12.8 us -> 6.7 us
  starting transfers between devices: 21.5 us -> 27.4 us
    all_to_all x1 -> x0, blocking collectives: 79.2 us -> none  [apply_layer(): lax.all_to_all(back, 'expert', split_axis=0, concat_axis=0, tiled=True)]
    all_to_all x1 -> x2, waiting for transfers between devices: 69.3 us -> 142 us  [apply_layer(): lax.all_to_all(back, 'expert', split_axis=0, concat_axis=0, tiled=True)]
    dot_general x2, matrix products: 22 us -> 5.65 us  [apply_layer(): jnp.dot(hidden, down_w, preferred_element_type=jnp.float32)]
    all_to_all x1 -> x2, starting transfers between devices: 5.94 us -> 11.6 us  [apply_layer(): lax.all_to_all(back, 'expert', split_axis=0, concat_axis=0, tiled=True)]
    dot_general x12 -> x6, matrix products: 13.3 us -> 13.4 us  [the longest x2 5.7 us: apply_layer(): gate_sum = jnp.dot(inputs, gate_w, preferred_element_type=jnp.float32)]
  transfers between devices with their start and end apart: 3 -> 4, of which waited for: 3 -> 4; matrix products, arithmetic and copies ran while one was open for 1% -> 1% of each run, Pallas kernels for 0% -> 0%
where the time goes in v3:
time: 394 us
  waiting for transfers between devices  221 us (56%)
  blocking collectives  80.1 us (20%)
  matrix products  36.4 us (9%)
  starting transfers between devices  27.4 us (7%)
  other arithmetic  21.4 us (5%)
  local copies, waits for them, and re-layouts  6.7 us (2%)
    all_to_all x2, waiting for transfers between devices, apply_layer(): lax.all_to_all(back, 'expert', split_axis=0, concat_axis=0, tiled=True)  142 us
    all_to_all x1, blocking collectives, apply_layer(): lax.all_to_all(outgoing, 'expert', split_axis=0, concat_axis=0, tiled=True)  80.1 us
    all_to_all x1, waiting for transfers between devices, apply_layer(): lax.all_to_all(outgoing, 'expert', split_axis=0, concat_axis=0, tiled=True)  73.3 us
    all_to_all x1, starting transfers between devices, apply_layer(): lax.all_to_all(outgoing, 'expert', split_axis=0, concat_axis=0, tiled=True)  12.3 us
    all_to_all x2, starting transfers between devices, apply_layer(): lax.all_to_all(back, 'expert', split_axis=0, concat_axis=0, tiled=True)  11.6 us
  transfers between devices with their start and end apart: 4, of which 4 were waited for; matrix products, arithmetic and copies ran while one was open for 1% of the time, Pallas kernels for 0%

profile of v3, /device:TPU:16, one launch (start us, length us, event | category | flops | bytes accessed | tf_op | source)
XLA Modules:
  0.0 393.6 jit_solution(2771539305923543061)
XLA Ops:
  3.2 1.2 reduce-window.16
  8.7 1.7 fusion.23
  12.1 1.9 pad_maximum_fusion
  14.0 12.3 %all-to-all-start = ((bf16[64,8,3072]{2,1,0:T(8,128)(2,1)}), bf16[64,8,3072]{2,1,0:T(8,128)(2,1)}, u32[]{:S(2)}, u32[]{:S(2)}) async-start(bf16[64,8,3072]{2,1,0:T(8,128)(2,1)} %pad_maximum_fusion), calls=%async_computation | async-start | bytes 6291456 | tf_op jit(solution)/shard_map/all_to_all | solution.py:86
  26.6 73.3 %all-to-all-done = bf16[64,8,3072]{2,1,0:T(8,128)(2,1)} async-done(((bf16[64,8,3072]{2,1,0:T(8,128)(2,1)}), bf16[64,8,3072]{2,1,0:T(8,128)(2,1)}, u32[]{:S(2)}, u32[]{:S(2)}) %all-to-all-start) | async-done | bytes 3145760 | tf_op jit(solution)/shard_map/all_to_all | solution.py:86
  99.9 1.7 slice_bitcast_fusion.7
  101.6 1.9 convolution_convert_fusion.7
  103.5 1.7 convolution_convert_fusion.6
  105.3 2.6 fusion.4
  107.9 2.8 multiply_convert_fusion.1
  110.7 2.8 convolution_convert_fusion.1
  115.0 1.9 pad_maximum_fusion.1
  116.9 5.7 %all-to-all-start.1 = ((bf16[64,8,3072]{2,1,0:T(8,128)(2,1)}), bf16[64,8,3072]{2,1,0:T(8,128)(2,1)}, u32[]{:S(2)}, u32[]{:S(2)}) async-start(bf16[64,8,3072]{2,1,0:T(8,128)(2,1)} %pad_maximum_fusion.1), calls=%async_computation.1 | async-start | bytes 6291456 | tf_op jit(solution)/shard_map/all_to_all | solution.py:132
  122.8 1.8 fusion.25
  124.7 1.3 select_convert_fusion.3
  126.0 1.3 subtract_convert_fusion.4
  127.3 69.1 %all-to-all-done.1 = bf16[64,8,3072]{2,1,0:T(8,128)(2,1)} async-done(((bf16[64,8,3072]{2,1,0:T(8,128)(2,1)}), bf16[64,8,3072]{2,1,0:T(8,128)(2,1)}, u32[]{:S(2)}, u32[]{:S(2)}) %all-to-all-start.1) | async-done | bytes 3145760 | tf_op jit(solution)/shard_map/all_to_all | solution.py:132
  196.4 1.8 fusion.31
  198.2 2.0 fusion.13
  200.4 3.4 collective-permute-start
  203.8 5.6 %collective-permute-done = bf16[64,2048]{1,0:T(8,128)(2,1)} collective-permute-done((bf16[64,2048]{1,0:T(8,128)(2,1)S(1)}, bf16[64,2048]{1,0:T(8,128)(2,1)}, u32[]{:S(2)}, u32[]{:S(2)}) %collective-permute-start) | collective-permute-done | bytes 262176 | tf_op jit(solution)/shard_map/ppermute | solution.py:17
  209.4 1.2 fusion.34
  210.8 1.6 fusion.11
  214.8 80.1 %all_to_all.20 = bf16[64,8,3072]{2,1,0:T(8,128)(2,1)S(1)} all-to-all(bf16[64,8,3072]{2,1,0:T(8,128)(2,1)S(1)} %pad_maximum_fusion.2), channel_id=1, replica_groups=mesh['section'=4,'expert'=64] {'expert'}, dimensions={0} | all-to-all | bytes 6291456 | tf_op jit(solution)/shard_map/all_to_all | solution.py:86
  297.4 2.6 fusion.2
  300.0 2.9 multiply_convert_fusion
  302.9 2.8 convolution_convert_fusion
  307.1 1.9 pad_maximum_fusion.3
  309.0 5.9 %all-to-all-start.3 = ((bf16[64,8,3072]{2,1,0:T(8,128)(2,1)}), bf16[64,8,3072]{2,1,0:T(8,128)(2,1)}, u32[]{:S(2)}, u32[]{:S(2)}) async-start(bf16[64,8,3072]{2,1,0:T(8,128)(2,1)} %pad_maximum_fusion.3), calls=%async_computation.3 | async-start | bytes 6291456 | tf_op jit(solution)/shard_map/all_to_all | solution.py:132
  315.6 73.1 %all-to-all-done.3 = bf16[64,8,3072]{2,1,0:T(8,128)(2,1)} async-done(((bf16[64,8,3072]{2,1,0:T(8,128)(2,1)}), bf16[64,8,3072]{2,1,0:T(8,128)(2,1)}, u32[]{:S(2)}, u32[]{:S(2)}) %all-to-all-start.3) | async-done | bytes 3145760 | tf_op jit(solution)/shard_map/all_to_all | solution.py:132
  388.7 1.8 fusion.30
  390.6 2.0 fusion.12
  (103 shorter events, 19.0 us)
Async XLA Ops:
  0.0 110.7 %copy-start = (bf16[1,1,768,2048]{3,2,1,0:T(8,128)(2,1)S(1)}, bf16[1,1,768,2048]{3,2,1,0:T(8,128)(2,1)}, u32[]{:S(2)}) copy-start(bf16[1,1,768,2048]{3,2,1,0:T(8,128)(2,1)} %param.13) | copy-start | bytes 9437188
  5.5 108.0 %copy-start.7 = (pred[512]{0:T(512)(128)(4,1)}, pred[512]{0:T(512)(128)(4,1)S(1)}, u32[]{:S(2)}) copy-start(pred[512]{0:T(512)(128)(4,1)S(1)} %eq.292) | copy-start | bytes 1540
  7.5 106.9 %copy-start.9 = (pred[512]{0:T(512)(128)(4,1)}, pred[512]{0:T(512)(128)(4,1)S(1)}, u32[]{:S(2)}) copy-start(pred[512]{0:T(512)(128)(4,1)S(1)} %eq.296) | copy-start | bytes 1540
  14.0 85.9 %all-to-all-start = ((bf16[64,8,3072]{2,1,0:T(8,128)(2,1)}), bf16[64,8,3072]{2,1,0:T(8,128)(2,1)}, u32[]{:S(2)}, u32[]{:S(2)}) async-start(bf16[64,8,3072]{2,1,0:T(8,128)(2,1)} %pad_maximum_fusion), calls=%async_computation | async-start | bytes 6291456 | tf_op jit(solution)/shard_map/all_to_all | solution.py:86
  101.6 3.6 copy-start.12
  105.2 2.6 copy-start.14
  116.9 5.7 %copy-start.11 = (f32[1,2,64,8]{2,3,1,0:T(8,128)S(1)}, f32[1,2,64,8]{2,3,1,0:T(8,128)}, u32[]{:S(2)}) copy-start(f32[1,2,64,8]{2,3,1,0:T(8,128)} %param.15) | copy-start | bytes 12292
  116.9 79.5 %all-to-all-start.1 = ((bf16[64,8,3072]{2,1,0:T(8,128)(2,1)}), bf16[64,8,3072]{2,1,0:T(8,128)(2,1)}, u32[]{:S(2)}, u32[]{:S(2)}) async-start(bf16[64,8,3072]{2,1,0:T(8,128)(2,1)} %pad_maximum_fusion.1), calls=%async_computation.1 | async-start | bytes 6291456 | tf_op jit(solution)/shard_map/all_to_all | solution.py:132
  196.4 3.9 copy-start.1
  200.4 3.4 copy-start.2
  200.4 9.1 %collective-permute-start = (bf16[64,2048]{1,0:T(8,128)(2,1)S(1)}, bf16[64,2048]{1,0:T(8,128)(2,1)}, u32[]{:S(2)}, u32[]{:S(2)}) collective-permute-start(bf16[64,2048]{1,0:T(8,128)(2,1)S(1)} %fusion.41), channel_id=1, source_target_pairs={{0,64},{64,128},{128,192},{1,65},{65,129},{129,193},{2,66},{66,130... | collective-permute-start | bytes 786440 | tf_op jit(solution)/shard_map/ppermute | solution.py:17
  294.9 0.6 copy-start.8
  294.9 1.1 copy-start.10
  295.5 1.9 copy-start.13
  297.4 2.6 copy-start.15
  309.0 5.9 %copy-start.4 = (f32[64,512]{1,0:T(8,128)S(1)}, f32[64,512]{1,0:T(8,128)}, u32[]{:S(2)}) copy-start(f32[64,512]{1,0:T(8,128)} %get-tuple-element.16) | copy-start | bytes 393220
  309.0 79.7 %all-to-all-start.3 = ((bf16[64,8,3072]{2,1,0:T(8,128)(2,1)}), bf16[64,8,3072]{2,1,0:T(8,128)(2,1)}, u32[]{:S(2)}, u32[]{:S(2)}) async-start(bf16[64,8,3072]{2,1,0:T(8,128)(2,1)} %pad_maximum_fusion.3), calls=%async_computation.3 | async-start | bytes 6291456 | tf_op jit(solution)/shard_map/all_to_all | solution.py:132
  315.6 75.0 %copy-start.5 = (bf16[64,512]{1,0:T(8,128)(2,1)S(1)}, bf16[64,512]{1,0:T(8,128)(2,1)}, u32[]{:S(2)}) copy-start(bf16[64,512]{1,0:T(8,128)(2,1)} %get-tuple-element.17) | copy-start | bytes 196612
  315.6 75.0 %copy-start.6 = (bf16[64,512]{1,0:T(8,128)(2,1)S(1)}, bf16[64,512]{1,0:T(8,128)(2,1)}, u32[]{:S(2)}) copy-start(bf16[64,512]{1,0:T(8,128)(2,1)} %get-tuple-element.18) | copy-start | bytes 196612
  390.5 2.2 copy-start.3

commit v4 on v3

--- a/solution.py
+++ b/solution.py
@@ -25,12 +25,17 @@
 
 def slot_table(route_ids, experts, capacity):
     group_count, row_count, top_count = route_ids.shape
-    expert_marks = (route_ids[..., None] == jnp.arange(experts, dtype=jnp.int32)).astype(jnp.int32)
-    expert_marks = expert_marks.reshape(group_count, row_count * top_count, experts)
-    earlier_marks = jnp.cumsum(expert_marks, axis=1) - expert_marks
-    slot_index = jnp.sum(earlier_marks * expert_marks, axis=-1).reshape(
-        group_count, row_count, top_count
-    )
+    flat = row_count * top_count
+    expert_marks = (route_ids[..., None] == jnp.arange(experts, dtype=jnp.int32)).astype(jnp.bfloat16)
+    expert_marks = expert_marks.reshape(group_count, flat, experts)
+    earlier = (
+        jnp.arange(flat, dtype=jnp.int32)[:, None] > jnp.arange(flat, dtype=jnp.int32)[None, :]
+    ).astype(jnp.bfloat16)
+    earlier_marks = jnp.einsum(
+        "ij,gje->gie", earlier, expert_marks, preferred_element_type=jnp.float32
+    )
+    slot_index = jnp.sum(earlier_marks * expert_marks.astype(jnp.float32), axis=-1)
+    slot_index = slot_index.astype(jnp.int32).reshape(group_count, row_count, top_count)
     group_index = jnp.arange(group_count, dtype=jnp.int32)[:, None, None]
     group_width = group_count * capacity
     positions = route_ids * group_width + group_index * capacity + slot_index
@@ -48,7 +53,7 @@
     return full_slot, part_slot, part_piece, pieces
 
 
-def apply_layer(hidden_rows, norm_gain, route_ids, combine, gate_w, up_w, down_w, experts):
+def apply_layer(hidden_rows, norm_gain, route_ids, combine, gate_up_w, down_w, experts):
     normed_rows = rms_normed(hidden_rows, norm_gain)
     row_count, model_width = hidden_rows.shape
     top_count = route_ids.shape[-1]
@@ -66,23 +71,20 @@
     hits_part = positions[:, :, None] == part_slot[None, None, :]
     pick_full = jnp.sum(hits_full.astype(jnp.int32), axis=1).astype(jnp.bfloat16).T
     pick_part = jnp.sum(hits_part.astype(jnp.int32), axis=1).astype(jnp.bfloat16).T
-    send_full = jnp.dot(pick_full, normed_rows, preferred_element_type=jnp.float32)
-    send_part = jnp.zeros((wire_rows, piece_width), jnp.float32)
-    for piece in range(pieces):
-        chosen = (part_piece == piece)[:, None]
+    pick_pieces = [
+        jnp.where((part_piece == piece)[:, None], pick_part, jnp.zeros_like(pick_part))
+        for piece in range(pieces)
+    ]
+    sources = [jnp.pad(normed_rows, ((0, 0), (0, piece_width)))]
+    for piece in range(pieces):
         lanes = normed_rows[:, piece * piece_width:(piece + 1) * piece_width]
-        send_part = send_part + jnp.dot(
-            jnp.where(chosen, pick_part, jnp.zeros_like(pick_part)),
-            lanes,
-            preferred_element_type=jnp.float32,
-        )
-    outgoing = jnp.concatenate(
-        [
-            send_full.astype(jnp.bfloat16).reshape(experts, SUBLANE, model_width),
-            send_part.astype(jnp.bfloat16).reshape(experts, SUBLANE, piece_width),
-        ],
-        axis=-1,
-    )
+        sources.append(jnp.pad(lanes, ((0, 0), (model_width, 0))))
+    outgoing = jnp.dot(
+        jnp.concatenate([pick_full] + pick_pieces, axis=1),
+        jnp.concatenate(sources, axis=0),
+        preferred_element_type=jnp.float32,
+    ).astype(jnp.bfloat16)
+    outgoing = outgoing.reshape(experts, SUBLANE, model_width + piece_width)
     received = lax.all_to_all(outgoing, "expert", split_axis=0, concat_axis=0, tiled=True)
 
     extra = width - SUBLANE
@@ -108,8 +110,9 @@
         )
     joined_rows = jnp.concatenate(gather_pieces, axis=-1)
     inputs = jnp.concatenate([full_rows, joined_rows], axis=0)
-    gate_sum = jnp.dot(inputs, gate_w, preferred_element_type=jnp.float32)
-    up_sum = jnp.dot(inputs, up_w, preferred_element_type=jnp.float32)
+    gate_up = jnp.dot(inputs, gate_up_w, preferred_element_type=jnp.float32)
+    ff = gate_up.shape[-1] // 2
+    gate_sum, up_sum = gate_up[:, :ff], gate_up[:, ff:]
     hidden = (jax.nn.silu(gate_sum) * up_sum).astype(jnp.bfloat16)
     hidden = lax.optimization_barrier(hidden)
     result = jnp.dot(hidden, down_w, preferred_element_type=jnp.float32).astype(jnp.bfloat16)
@@ -167,6 +170,7 @@
     section_index = lax.axis_index("section")
     experts = lax.axis_size("expert") * w_gate.shape[1]
     carried = in_flight[0]
+    gate_up_w = jnp.concatenate([w_gate[0, 0], w_up[0, 0]], axis=-1)
     traced = []
     for tick_index in range(TICKS):
         layer_out = apply_layer(
@@ -174,8 +178,7 @@
             norm_gain[0],
             routes[0, tick_index],
             combine_weight[0, tick_index],
-            w_gate[0, 0],
-            w_up[0, 0],
+            gate_up_w,
             w_down[0, 0],
             experts,
         )

time: 394 us -> 398 us (1.010)
  local copies, waits for them, and re-layouts: 6.7 us -> 11.6 us
    dot_general x10 -> x6, matrix products: 16.3 us -> 15.1 us  [the longest x2 10 us: apply_layer(): gate_up = jnp.dot(inputs, gate_up_w, preferred_element_type=jnp.float32)]
  transfers between devices with their start and end apart: 4 -> 4, of which waited for: 4 -> 4; matrix products, arithmetic and copies ran while one was open for 1% -> 2% of each run, Pallas kernels for 0% -> 0%
where the time goes in v4:
time: 398 us; the launch traced here: 397 us
  waiting for transfers between devices  220 us (55%)
  blocking collectives  80 us (20%)
  matrix products  35.3 us (9%)
  starting transfers between devices  27.1 us (7%)
  other arithmetic  22.7 us (6%)
  local copies, waits for them, and re-layouts  11.6 us (3%)
    all_to_all x2, waiting for transfers between devices, apply_layer(): lax.all_to_all(back, 'expert', split_axis=0, concat_axis=0, tiled=True)  144 us
    all_to_all x1, blocking collectives, apply_layer(): lax.all_to_all(outgoing, 'expert', split_axis=0, concat_axis=0, tiled=True)  80 us
    all_to_all x1, waiting for transfers between devices, apply_layer(): lax.all_to_all(outgoing, 'expert', split_axis=0, concat_axis=0, tiled=True)  71.2 us
    all_to_all x1, starting transfers between devices, apply_layer(): lax.all_to_all(outgoing, 'expert', split_axis=0, concat_axis=0, tiled=True)  12.5 us
    all_to_all x2, starting transfers between devices, apply_layer(): lax.all_to_all(back, 'expert', split_axis=0, concat_axis=0, tiled=True)  11.4 us
    dot_general x2, matrix products, apply_layer(): gate_up = jnp.dot(inputs, gate_up_w, preferred_element_type=jnp.float32)  10 us
  transfers between devices with their start and end apart: 4, of which 4 were waited for; matrix products, arithmetic and copies ran while one was open for 2% of the time, Pallas kernels for 0%

profile of v4, /device:TPU:16, one launch (start us, length us, event | category | flops | bytes accessed | tf_op | source)
XLA Modules:
  0.0 397.1 jit_solution(3794347174311201330)
XLA Ops:
  0.1 1.3 fusion.71
  9.4 1.7 fusion.54
  11.2 2.8 fusion.56
  14.0 1.4 select_bitcast_fusion.3
  15.4 2.7 fusion
  18.1 12.5 %all-to-all-start = ((bf16[64,8,3072]{2,1,0:T(8,128)(2,1)}), bf16[64,8,3072]{2,1,0:T(8,128)(2,1)}, u32[]{:S(2)}, u32[]{:S(2)}) async-start(bf16[64,8,3072]{2,1,0:T(8,128)(2,1)} %fusion), calls=%async_computation | async-start | bytes 6291456 | tf_op jit(solution)/shard_map/all_to_all | solution.py:88
  33.0 71.2 %all-to-all-done = bf16[64,8,3072]{2,1,0:T(8,128)(2,1)} async-done(((bf16[64,8,3072]{2,1,0:T(8,128)(2,1)}), bf16[64,8,3072]{2,1,0:T(8,128)(2,1)}, u32[]{:S(2)}, u32[]{:S(2)}) %all-to-all-start) | async-done | bytes 3145760 | tf_op jit(solution)/shard_map/all_to_all | solution.py:88
  104.1 1.7 convolution_convert_fusion.6
  105.9 1.9 convolution_convert_fusion.7
  107.7 2.0 slice_bitcast_fusion.7
  109.8 5.0 %fusion.3 = f32[768,1536]{1,0:T(8,128)S(1)} fusion(bf16[2048,768]{1,0:T(8,128)(2,1)S(1)} %bitcast.108, bf16[2048,768]{1,0:T(8,128)(2,1)S(1)} %bitcast.110, bf16[256,1024]{1,0:T(8,128)(2,1)S(1)} %convolution_convert_fusion.6, bf16[256,1024]{1,0:T(8,128)(2,1)S(1)} %convolution_convert_fusion.7, bf16[512,2048]{1,0:T(8,128)(2,1)S(1)} %slice_bitcast_fusion.7), kind=kOutput, calls=%fused_computation.6 | convolution fusion | flops 4853858304 | bytes 14155776 | tf_op jit(solution)/shard_map/dot_general | solution.py:113
  115.5 2.8 convolution_convert_fusion.3
  119.8 1.9 pad_maximum_fusion.3
  121.6 5.6 %all-to-all-start.1 = ((bf16[64,8,3072]{2,1,0:T(8,128)(2,1)}), bf16[64,8,3072]{2,1,0:T(8,128)(2,1)}, u32[]{:S(2)}, u32[]{:S(2)}) async-start(bf16[64,8,3072]{2,1,0:T(8,128)(2,1)} %pad_maximum_fusion.3), calls=%async_computation.1 | async-start | bytes 6291456 | tf_op jit(solution)/shard_map/all_to_all | solution.py:135
  127.2 1.6 subtract_convert_fusion.5
  128.9 1.4 subtract_convert_fusion.4
  130.2 70.7 %all-to-all-done.1 = bf16[64,8,3072]{2,1,0:T(8,128)(2,1)} async-done(((bf16[64,8,3072]{2,1,0:T(8,128)(2,1)}), bf16[64,8,3072]{2,1,0:T(8,128)(2,1)}, u32[]{:S(2)}, u32[]{:S(2)}) %all-to-all-start.1) | async-done | bytes 3145760 | tf_op jit(solution)/shard_map/all_to_all | solution.py:135
  201.0 1.8 fusion.62
  202.9 2.0 fusion.24
  205.1 3.2 collective-permute-start
  209.2 4.9 %collective-permute-done = bf16[64,2048]{1,0:T(8,128)(2,1)} collective-permute-done((bf16[64,2048]{1,0:T(8,128)(2,1)S(1)}, bf16[64,2048]{1,0:T(8,128)(2,1)}, u32[]{:S(2)}, u32[]{:S(2)}) %collective-permute-start) | collective-permute-done | bytes 262176 | tf_op jit(solution)/shard_map/ppermute | solution.py:17
  214.1 1.2 fusion.67
  215.5 1.9 fusion.1
  217.5 80.0 %all_to_all.20 = bf16[64,8,3072]{2,1,0:T(8,128)(2,1)S(1)} all-to-all(bf16[64,8,3072]{2,1,0:T(8,128)(2,1)S(1)} %fusion.1), channel_id=1, replica_groups=mesh['section'=4,'expert'=64] {'expert'}, dimensions={0} | all-to-all | bytes 6291456 | tf_op jit(solution)/shard_map/all_to_all | solution.py:88
  298.7 1.2 copy-done.15
  300.9 5.0 %fusion.2 = f32[768,1536]{1,0:T(8,128)S(1)} fusion(bf16[2048,768]{1,0:T(8,128)(2,1)S(1)} %bitcast.109, bf16[2048,768]{1,0:T(8,128)(2,1)S(1)} %bitcast.111, bf16[256,1024]{1,0:T(8,128)(2,1)S(1)} %convolution_convert_fusion.4, bf16[256,1024]{1,0:T(8,128)(2,1)S(1)} %convolution_convert_fusion.5, bf16[512,2048]{1,0:T(8,128)(2,1)S(1)} %slice_bitcast_fusion.3), kind=kOutput, calls=%fused_computation.5 | convolution fusion | flops 4853858304 | bytes 14155776 | tf_op jit(solution)/shard_map/dot_general | solution.py:113
  306.6 2.8 convolution_convert_fusion.2
  310.8 1.9 pad_maximum_fusion.4
  312.7 5.8 %all-to-all-start.3 = ((bf16[64,8,3072]{2,1,0:T(8,128)(2,1)}), bf16[64,8,3072]{2,1,0:T(8,128)(2,1)}, u32[]{:S(2)}, u32[]{:S(2)}) async-start(bf16[64,8,3072]{2,1,0:T(8,128)(2,1)} %pad_maximum_fusion.4), calls=%async_computation.3 | async-start | bytes 6291456 | tf_op jit(solution)/shard_map/all_to_all | solution.py:135
  319.2 73.1 %all-to-all-done.3 = bf16[64,8,3072]{2,1,0:T(8,128)(2,1)} async-done(((bf16[64,8,3072]{2,1,0:T(8,128)(2,1)}), bf16[64,8,3072]{2,1,0:T(8,128)(2,1)}, u32[]{:S(2)}, u32[]{:S(2)}) %all-to-all-start.3) | async-done | bytes 3145760 | tf_op jit(solution)/shard_map/all_to_all | solution.py:135
  392.2 1.8 fusion.61
  394.1 2.0 fusion.23
  (95 shorter events, 19.6 us)
Async XLA Ops:
  0.0 115.5 %copy-start = (bf16[1,1,768,2048]{3,2,1,0:T(8,128)(2,1)S(1)}, bf16[1,1,768,2048]{3,2,1,0:T(8,128)(2,1)}, u32[]{:S(2)}) copy-start(bf16[1,1,768,2048]{3,2,1,0:T(8,128)(2,1)} %param.13) | copy-start | bytes 9437188
  0.1 11.1 %copy-start.12 = (s32[64]{0:T(128)}, s32[64]{0:T(128)S(1)}, u32[]{:S(2)}) copy-start(s32[64]{0:T(128)S(1)} %get-tuple-element.59) | copy-start | bytes 772
  18.1 12.5 %copy-start.13 = (s32[64]{0:T(128)S(1)}, s32[64]{0:T(128)}, u32[]{:S(2)}) copy-start(s32[64]{0:T(128)} %copy-done.12) | copy-start | bytes 772
  18.1 86.1 %all-to-all-start = ((bf16[64,8,3072]{2,1,0:T(8,128)(2,1)}), bf16[64,8,3072]{2,1,0:T(8,128)(2,1)}, u32[]{:S(2)}, u32[]{:S(2)}) async-start(bf16[64,8,3072]{2,1,0:T(8,128)(2,1)} %fusion), calls=%async_computation | async-start | bytes 6291456 | tf_op jit(solution)/shard_map/all_to_all | solution.py:88
  105.8 3.9 copy-start.14
  105.9 3.9 copy-start.16
  115.5 2.9 copy-start.8
  118.4 0.8 copy-start.10
  121.6 79.3 %all-to-all-start.1 = ((bf16[64,8,3072]{2,1,0:T(8,128)(2,1)}), bf16[64,8,3072]{2,1,0:T(8,128)(2,1)}, u32[]{:S(2)}, u32[]{:S(2)}) async-start(bf16[64,8,3072]{2,1,0:T(8,128)(2,1)} %pad_maximum_fusion.3), calls=%async_computation.1 | async-start | bytes 6291456 | tf_op jit(solution)/shard_map/all_to_all | solution.py:135
  130.2 72.7 %copy-start.4 = (bf16[64,512]{1,0:T(8,128)(2,1)S(1)}, bf16[64,512]{1,0:T(8,128)(2,1)}, u32[]{:S(2)}) copy-start(bf16[64,512]{1,0:T(8,128)(2,1)} %get-tuple-element.21) | copy-start | bytes 196612
  130.2 72.7 %copy-start.5 = (bf16[64,512]{1,0:T(8,128)(2,1)S(1)}, bf16[64,512]{1,0:T(8,128)(2,1)}, u32[]{:S(2)}) copy-start(bf16[64,512]{1,0:T(8,128)(2,1)} %get-tuple-element.22) | copy-start | bytes 196612
  201.0 4.0 %copy-start.1 = (bf16[1,64,2048]{2,1,0:T(8,128)(2,1)S(1)}, bf16[1,64,2048]{2,1,0:T(8,128)(2,1)}, u32[]{:S(2)}) copy-start(bf16[1,64,2048]{2,1,0:T(8,128)(2,1)} %param.8) | copy-start | bytes 786436
  205.1 4.1 %copy-start.2 = (bf16[64,2048]{1,0:T(8,128)(2,1)}, bf16[64,2048]{1,0:T(8,128)(2,1)S(1)}, u32[]{:S(2)}) copy-start(bf16[64,2048]{1,0:T(8,128)(2,1)S(1)} %fusion.74) | copy-start | bytes 786436
  205.1 9.0 %collective-permute-start = (bf16[64,2048]{1,0:T(8,128)(2,1)S(1)}, bf16[64,2048]{1,0:T(8,128)(2,1)}, u32[]{:S(2)}, u32[]{:S(2)}) collective-permute-start(bf16[64,2048]{1,0:T(8,128)(2,1)S(1)} %fusion.74), channel_id=1, source_target_pairs={{0,64},{64,128},{128,192},{1,65},{65,129},{129,193},{2,66},{66,130... | collective-permute-start | bytes 786440 | tf_op jit(solution)/shard_map/ppermute | solution.py:17
  217.4 80.1 %copy-start.11 = (pred[512]{0:T(512)(128)(4,1)S(1)}, pred[512]{0:T(512)(128)(4,1)}, u32[]{:S(2)}) copy-start(pred[512]{0:T(512)(128)(4,1)} %eq.274) | copy-start | bytes 1540
  217.4 80.6 %copy-start.9 = (pred[512]{0:T(512)(128)(4,1)S(1)}, pred[512]{0:T(512)(128)(4,1)}, u32[]{:S(2)}) copy-start(pred[512]{0:T(512)(128)(4,1)} %eq.270) | copy-start | bytes 1540
  298.0 1.9 copy-start.15
  298.0 2.8 copy-start.17
  312.7 79.5 %all-to-all-start.3 = ((bf16[64,8,3072]{2,1,0:T(8,128)(2,1)}), bf16[64,8,3072]{2,1,0:T(8,128)(2,1)}, u32[]{:S(2)}, u32[]{:S(2)}) async-start(bf16[64,8,3072]{2,1,0:T(8,128)(2,1)} %pad_maximum_fusion.4), calls=%async_computation.3 | async-start | bytes 6291456 | tf_op jit(solution)/shard_map/all_to_all | solution.py:135
  319.2 75.0 %copy-start.6 = (bf16[64,512]{1,0:T(8,128)(2,1)S(1)}, bf16[64,512]{1,0:T(8,128)(2,1)}, u32[]{:S(2)}) copy-start(bf16[64,512]{1,0:T(8,128)(2,1)} %get-tuple-element.17) | copy-start | bytes 196612
  319.2 75.0 %copy-start.7 = (bf16[64,512]{1,0:T(8,128)(2,1)S(1)}, bf16[64,512]{1,0:T(8,128)(2,1)}, u32[]{:S(2)}) copy-start(bf16[64,512]{1,0:T(8,128)(2,1)} %get-tuple-element.18) | copy-start | bytes 196612
  394.0 2.2 copy-start.3

commit v5 on v3

--- a/solution.py
+++ b/solution.py
@@ -48,7 +48,7 @@
     return full_slot, part_slot, part_piece, pieces
 
 
-def apply_layer(hidden_rows, norm_gain, route_ids, combine, gate_w, up_w, down_w, experts):
+def apply_layer(hidden_rows, norm_gain, route_ids, combine, gate_up_w, down_w, experts):
     normed_rows = rms_normed(hidden_rows, norm_gain)
     row_count, model_width = hidden_rows.shape
     top_count = route_ids.shape[-1]
@@ -108,8 +108,9 @@
         )
     joined_rows = jnp.concatenate(gather_pieces, axis=-1)
     inputs = jnp.concatenate([full_rows, joined_rows], axis=0)
-    gate_sum = jnp.dot(inputs, gate_w, preferred_element_type=jnp.float32)
-    up_sum = jnp.dot(inputs, up_w, preferred_element_type=jnp.float32)
+    gate_up = jnp.dot(inputs, gate_up_w, preferred_element_type=jnp.float32)
+    ff = gate_up.shape[-1] // 2
+    gate_sum, up_sum = gate_up[:, :ff], gate_up[:, ff:]
     hidden = (jax.nn.silu(gate_sum) * up_sum).astype(jnp.bfloat16)
     hidden = lax.optimization_barrier(hidden)
     result = jnp.dot(hidden, down_w, preferred_element_type=jnp.float32).astype(jnp.bfloat16)
@@ -167,6 +168,7 @@
     section_index = lax.axis_index("section")
     experts = lax.axis_size("expert") * w_gate.shape[1]
     carried = in_flight[0]
+    gate_up_w = jnp.concatenate([w_gate[0, 0], w_up[0, 0]], axis=-1)
     traced = []
     for tick_index in range(TICKS):
         layer_out = apply_layer(
@@ -174,8 +176,7 @@
             norm_gain[0],
             routes[0, tick_index],
             combine_weight[0, tick_index],
-            w_gate[0, 0],
-            w_up[0, 0],
+            gate_up_w,
             w_down[0, 0],
             experts,
         )

time: 394 us -> 395 us (level)
    dot_general x4 -> x2, matrix products: 10.9 us -> 10 us  [apply_layer(): gate_up = jnp.dot(inputs, gate_up_w, preferred_element_type=jnp.float32)]
where the time goes in v5:
time: 395 us
  waiting for transfers between devices  221 us (56%)
  blocking collectives  80 us (20%)
  matrix products  35.6 us (9%)
  starting transfers between devices  27.4 us (7%)
  other arithmetic  22.7 us (6%)
  local copies, waits for them, and re-layouts  7.36 us (2%)
    all_to_all x2, waiting for transfers between devices, apply_layer(): lax.all_to_all(back, 'expert', split_axis=0, concat_axis=0, tiled=True)  142 us
    all_to_all x1, blocking collectives, apply_layer(): lax.all_to_all(outgoing, 'expert', split_axis=0, concat_axis=0, tiled=True)  80 us
    all_to_all x1, waiting for transfers between devices, apply_layer(): lax.all_to_all(outgoing, 'expert', split_axis=0, concat_axis=0, tiled=True)  73.3 us
    all_to_all x1, starting transfers between devices, apply_layer(): lax.all_to_all(outgoing, 'expert', split_axis=0, concat_axis=0, tiled=True)  12.3 us
    all_to_all x2, starting transfers between devices, apply_layer(): lax.all_to_all(back, 'expert', split_axis=0, concat_axis=0, tiled=True)  11.6 us
    dot_general x2, matrix products, apply_layer(): gate_up = jnp.dot(inputs, gate_up_w, preferred_element_type=jnp.float32)  10 us
  transfers between devices with their start and end apart: 4, of which 4 were waited for; matrix products, arithmetic and copies ran while one was open for 1% of the time, Pallas kernels for 0%

profile of v5, /device:TPU:16, one launch (start us, length us, event | category | flops | bytes accessed | tf_op | source)
XLA Modules:
  0.0 394.7 jit_solution(1108336449436698118)
XLA Ops:
  1.5 1.2 reduce-window.14
  3.2 1.2 reduce-window.16
  6.3 1.1 fusion.40
  8.7 1.7 fusion.25
  12.1 1.9 pad_maximum_fusion.3
  14.0 12.3 %all-to-all-start = ((bf16[64,8,3072]{2,1,0:T(8,128)(2,1)}), bf16[64,8,3072]{2,1,0:T(8,128)(2,1)}, u32[]{:S(2)}, u32[]{:S(2)}) async-start(bf16[64,8,3072]{2,1,0:T(8,128)(2,1)} %pad_maximum_fusion.3), calls=%async_computation | async-start | bytes 6291456 | tf_op jit(solution)/shard_map/all_to_all | solution.py:86
  26.6 73.3 %all-to-all-done = bf16[64,8,3072]{2,1,0:T(8,128)(2,1)} async-done(((bf16[64,8,3072]{2,1,0:T(8,128)(2,1)}), bf16[64,8,3072]{2,1,0:T(8,128)(2,1)}, u32[]{:S(2)}, u32[]{:S(2)}) %all-to-all-start) | async-done | bytes 3145760 | tf_op jit(solution)/shard_map/all_to_all | solution.py:86
  99.9 1.9 slice_bitcast_fusion.7
  101.8 1.9 convolution_convert_fusion.7
  103.7 1.7 convolution_convert_fusion.6
  105.4 5.0 %fusion.1 = f32[768,1536]{1,0:T(8,128)S(1)} fusion(bf16[2048,768]{1,0:T(8,128)(2,1)S(1)} %bitcast.128, bf16[2048,768]{1,0:T(8,128)(2,1)S(1)} %bitcast.130, bf16[256,1024]{1,0:T(8,128)(2,1)S(1)} %convolution_convert_fusion.6, bf16[256,1024]{1,0:T(8,128)(2,1)S(1)} %convolution_convert_fusion.7, bf16[512,2048]{1,0:T(8,128)(2,1)S(1)} %slice_bitcast_fusion.7), kind=kOutput, calls=%fused_computation.2 | convolution fusion | flops 4853858304 | bytes 14155776 | tf_op jit(solution)/shard_map/dot_general | solution.py:111
  111.1 2.8 convolution_convert_fusion.1
  115.4 1.9 pad_maximum_fusion.4
  117.3 5.7 %all-to-all-start.1 = ((bf16[64,8,3072]{2,1,0:T(8,128)(2,1)}), bf16[64,8,3072]{2,1,0:T(8,128)(2,1)}, u32[]{:S(2)}, u32[]{:S(2)}) async-start(bf16[64,8,3072]{2,1,0:T(8,128)(2,1)} %pad_maximum_fusion.4), calls=%async_computation.1 | async-start | bytes 6291456 | tf_op jit(solution)/shard_map/all_to_all | solution.py:133
  123.2 1.8 fusion.27
  125.1 1.3 select_convert_fusion.3
  126.4 1.3 subtract_convert_fusion.4
  127.7 69.1 %all-to-all-done.1 = bf16[64,8,3072]{2,1,0:T(8,128)(2,1)} async-done(((bf16[64,8,3072]{2,1,0:T(8,128)(2,1)}), bf16[64,8,3072]{2,1,0:T(8,128)(2,1)}, u32[]{:S(2)}, u32[]{:S(2)}) %all-to-all-start.1) | async-done | bytes 3145760 | tf_op jit(solution)/shard_map/all_to_all | solution.py:133
  196.7 1.8 fusion.33
  198.6 2.0 fusion.19
  200.8 3.4 collective-permute-start
  204.2 5.6 %collective-permute-done = bf16[64,2048]{1,0:T(8,128)(2,1)} collective-permute-done((bf16[64,2048]{1,0:T(8,128)(2,1)S(1)}, bf16[64,2048]{1,0:T(8,128)(2,1)}, u32[]{:S(2)}, u32[]{:S(2)}) %collective-permute-start) | collective-permute-done | bytes 262176 | tf_op jit(solution)/shard_map/ppermute | solution.py:17
  209.8 1.2 fusion.36
  211.2 1.6 fusion.15
  215.2 80.0 %all_to_all.20 = bf16[64,8,3072]{2,1,0:T(8,128)(2,1)S(1)} all-to-all(bf16[64,8,3072]{2,1,0:T(8,128)(2,1)S(1)} %pad_maximum_fusion.5), channel_id=1, replica_groups=mesh['section'=4,'expert'=64] {'expert'}, dimensions={0} | all-to-all | bytes 6291456 | tf_op jit(solution)/shard_map/all_to_all | solution.py:86
  298.3 5.0 %fusion = f32[768,1536]{1,0:T(8,128)S(1)} fusion(bf16[2048,768]{1,0:T(8,128)(2,1)S(1)} %bitcast.129, bf16[2048,768]{1,0:T(8,128)(2,1)S(1)} %bitcast.131, bf16[256,1024]{1,0:T(8,128)(2,1)S(1)} %convolution_convert_fusion.4, bf16[256,1024]{1,0:T(8,128)(2,1)S(1)} %convolution_convert_fusion.5, bf16[512,2048]{1,0:T(8,128)(2,1)S(1)} %slice_bitcast_fusion.3), kind=kOutput, calls=%fused_computation.1 | convolution fusion | flops 4853858304 | bytes 14155776 | tf_op jit(solution)/shard_map/dot_general | solution.py:111
  304.0 2.8 convolution_convert_fusion
  308.2 1.9 pad_maximum_fusion.6
  310.1 5.9 %all-to-all-start.3 = ((bf16[64,8,3072]{2,1,0:T(8,128)(2,1)}), bf16[64,8,3072]{2,1,0:T(8,128)(2,1)}, u32[]{:S(2)}, u32[]{:S(2)}) async-start(bf16[64,8,3072]{2,1,0:T(8,128)(2,1)} %pad_maximum_fusion.6), calls=%async_computation.3 | async-start | bytes 6291456 | tf_op jit(solution)/shard_map/all_to_all | solution.py:133
  316.7 73.1 %all-to-all-done.3 = bf16[64,8,3072]{2,1,0:T(8,128)(2,1)} async-done(((bf16[64,8,3072]{2,1,0:T(8,128)(2,1)}), bf16[64,8,3072]{2,1,0:T(8,128)(2,1)}, u32[]{:S(2)}, u32[]{:S(2)}) %all-to-all-start.3) | async-done | bytes 3145760 | tf_op jit(solution)/shard_map/all_to_all | solution.py:133
  389.8 1.8 fusion.32
  391.7 2.0 fusion.18
  (103 shorter events, 18.5 us)
Async XLA Ops:
  0.0 111.1 %copy-start = (bf16[1,1,768,2048]{3,2,1,0:T(8,128)(2,1)S(1)}, bf16[1,1,768,2048]{3,2,1,0:T(8,128)(2,1)}, u32[]{:S(2)}) copy-start(bf16[1,1,768,2048]{3,2,1,0:T(8,128)(2,1)} %param.13) | copy-start | bytes 9437188
  5.5 108.4 %copy-start.7 = (pred[512]{0:T(512)(128)(4,1)}, pred[512]{0:T(512)(128)(4,1)S(1)}, u32[]{:S(2)}) copy-start(pred[512]{0:T(512)(128)(4,1)S(1)} %eq.292) | copy-start | bytes 1540
  7.5 107.3 %copy-start.9 = (pred[512]{0:T(512)(128)(4,1)}, pred[512]{0:T(512)(128)(4,1)S(1)}, u32[]{:S(2)}) copy-start(pred[512]{0:T(512)(128)(4,1)S(1)} %eq.296) | copy-start | bytes 1540
  14.0 85.9 %all-to-all-start = ((bf16[64,8,3072]{2,1,0:T(8,128)(2,1)}), bf16[64,8,3072]{2,1,0:T(8,128)(2,1)}, u32[]{:S(2)}, u32[]{:S(2)}) async-start(bf16[64,8,3072]{2,1,0:T(8,128)(2,1)} %pad_maximum_fusion.3), calls=%async_computation | async-start | bytes 6291456 | tf_op jit(solution)/shard_map/all_to_all | solution.py:86
  99.9 5.5 %copy-start.14 = (bf16[1,1,2048,768]{3,2,1,0:T(8,128)(2,1)S(1)}, bf16[1,1,2048,768]{3,2,1,0:T(8,128)(2,1)}, u32[]{:S(2)}) copy-start(bf16[1,1,2048,768]{3,2,1,0:T(8,128)(2,1)} %param.11) | copy-start | bytes 9437188
  101.8 3.6 copy-start.12
  117.3 5.7 %copy-start.11 = (f32[1,2,64,8]{2,3,1,0:T(8,128)S(1)}, f32[1,2,64,8]{2,3,1,0:T(8,128)}, u32[]{:S(2)}) copy-start(f32[1,2,64,8]{2,3,1,0:T(8,128)} %param.15) | copy-start | bytes 12292
  117.3 79.5 %all-to-all-start.1 = ((bf16[64,8,3072]{2,1,0:T(8,128)(2,1)}), bf16[64,8,3072]{2,1,0:T(8,128)(2,1)}, u32[]{:S(2)}, u32[]{:S(2)}) async-start(bf16[64,8,3072]{2,1,0:T(8,128)(2,1)} %pad_maximum_fusion.4), calls=%async_computation.1 | async-start | bytes 6291456 | tf_op jit(solution)/shard_map/all_to_all | solution.py:133
  196.7 3.9 copy-start.1
  200.8 3.4 copy-start.2
  200.8 9.0 %collective-permute-start = (bf16[64,2048]{1,0:T(8,128)(2,1)S(1)}, bf16[64,2048]{1,0:T(8,128)(2,1)}, u32[]{:S(2)}, u32[]{:S(2)}) collective-permute-start(bf16[64,2048]{1,0:T(8,128)(2,1)S(1)} %fusion.43), channel_id=1, source_target_pairs={{0,64},{64,128},{128,192},{1,65},{65,129},{129,193},{2,66},{66,130... | collective-permute-start | bytes 786440 | tf_op jit(solution)/shard_map/ppermute | solution.py:17
  295.3 0.6 copy-start.8
  295.3 1.1 copy-start.10
  295.3 1.9 copy-start.15
  295.9 2.4 copy-start.13
  310.1 5.9 %copy-start.4 = (f32[64,512]{1,0:T(8,128)S(1)}, f32[64,512]{1,0:T(8,128)}, u32[]{:S(2)}) copy-start(f32[64,512]{1,0:T(8,128)} %get-tuple-element.16) | copy-start | bytes 393220
  310.1 79.7 %all-to-all-start.3 = ((bf16[64,8,3072]{2,1,0:T(8,128)(2,1)}), bf16[64,8,3072]{2,1,0:T(8,128)(2,1)}, u32[]{:S(2)}, u32[]{:S(2)}) async-start(bf16[64,8,3072]{2,1,0:T(8,128)(2,1)} %pad_maximum_fusion.6), calls=%async_computation.3 | async-start | bytes 6291456 | tf_op jit(solution)/shard_map/all_to_all | solution.py:133
  316.7 75.0 %copy-start.5 = (bf16[64,512]{1,0:T(8,128)(2,1)S(1)}, bf16[64,512]{1,0:T(8,128)(2,1)}, u32[]{:S(2)}) copy-start(bf16[64,512]{1,0:T(8,128)(2,1)} %get-tuple-element.17) | copy-start | bytes 196612
  316.7 75.0 %copy-start.6 = (bf16[64,512]{1,0:T(8,128)(2,1)S(1)}, bf16[64,512]{1,0:T(8,128)(2,1)}, u32[]{:S(2)}) copy-start(bf16[64,512]{1,0:T(8,128)(2,1)} %get-tuple-element.18) | copy-start | bytes 196612
  391.6 2.2 copy-start.3

commit v6 on v5

--- a/solution.py
+++ b/solution.py
@@ -1,5 +1,6 @@
 import jax
 import jax.numpy as jnp
+import numpy as np
 from jax import lax
 from jax.sharding import PartitionSpec as P
 
@@ -40,18 +41,16 @@
 def wire_slots(experts, width):
     extra = width - SUBLANE
     pieces = SUBLANE // extra
-    row = jnp.arange(SUBLANE, dtype=jnp.int32)
-    base = jnp.arange(experts, dtype=jnp.int32)[:, None] * width
+    row = np.arange(SUBLANE, dtype=np.int32)
+    base = np.arange(experts, dtype=np.int32)[:, None] * width
     full_slot = (base + row[None, :]).reshape(-1)
     part_slot = (base + SUBLANE + row[None, :] % extra).reshape(-1)
-    part_piece = jnp.broadcast_to(row[None, :] // extra, (experts, SUBLANE)).reshape(-1)
+    part_piece = np.broadcast_to(row[None, :] // extra, (experts, SUBLANE)).reshape(-1)
     return full_slot, part_slot, part_piece, pieces
 
 
-def apply_layer(hidden_rows, norm_gain, route_ids, combine, gate_up_w, down_w, experts):
-    normed_rows = rms_normed(hidden_rows, norm_gain)
-    row_count, model_width = hidden_rows.shape
-    top_count = route_ids.shape[-1]
+def plan(route_ids, combine, experts):
+    row_count, top_count = route_ids.shape
     block_rows = min(BLOCK_ROWS, row_count)
     group_count = row_count // block_rows
     capacity = max(2, min(block_rows, block_rows * top_count // experts * 3 // 2))
@@ -59,22 +58,50 @@
     groups = route_ids.reshape(group_count, block_rows, top_count)
     positions = slot_table(groups, experts, capacity)
     full_slot, part_slot, part_piece, pieces = wire_slots(experts, width)
-    piece_width = model_width // pieces
-    wire_rows = experts * SUBLANE
-
     hits_full = positions[:, :, None] == full_slot[None, None, :]
     hits_part = positions[:, :, None] == part_slot[None, None, :]
     pick_full = jnp.sum(hits_full.astype(jnp.int32), axis=1).astype(jnp.bfloat16).T
     pick_part = jnp.sum(hits_part.astype(jnp.int32), axis=1).astype(jnp.bfloat16).T
+    pick_pieces = [
+        jnp.where((part_piece == piece)[:, None], pick_part, jnp.zeros_like(pick_part))
+        for piece in range(pieces)
+    ]
+    weights = combine[:, :, None]
+    mix_full = jnp.sum(jnp.where(hits_full, weights, 0.0), axis=1)
+    mix_part = jnp.sum(jnp.where(hits_part, weights, 0.0), axis=1)
+
+    def split(mix):
+        high = mix.astype(jnp.bfloat16)
+        low = (mix - high.astype(jnp.float32)).astype(jnp.bfloat16)
+        return [high, low]
+
+    full_lhs = jnp.concatenate(split(mix_full), axis=0)
+    part_parts = []
+    for piece in range(pieces):
+        part_parts += split(jnp.where((part_piece == piece)[None, :], mix_part, 0.0))
+    part_lhs = jnp.concatenate(part_parts, axis=0)
+    return (pick_full, pick_pieces, full_lhs, part_lhs)
+
+
+def apply_layer(hidden_rows, norm_gain, tables, gate_up_w, down_w, experts, width, tie=None):
+    pick_full, pick_pieces, full_lhs, part_lhs = tables
+    extra = width - SUBLANE
+    wire_joined = np.asarray(
+        np.arange(experts)[:, None] * extra + np.arange(SUBLANE)[None, :] % extra, np.int32
+    ).reshape(-1)
+    joined_row = np.arange(experts * extra, dtype=np.int32)
+    normed_rows = rms_normed(hidden_rows, norm_gain)
+    row_count, model_width = hidden_rows.shape
+    full_slot, part_slot, part_piece, pieces = wire_slots(experts, width)
+    piece_width = model_width // pieces
+    wire_rows = experts * SUBLANE
+
     send_full = jnp.dot(pick_full, normed_rows, preferred_element_type=jnp.float32)
     send_part = jnp.zeros((wire_rows, piece_width), jnp.float32)
     for piece in range(pieces):
-        chosen = (part_piece == piece)[:, None]
         lanes = normed_rows[:, piece * piece_width:(piece + 1) * piece_width]
         send_part = send_part + jnp.dot(
-            jnp.where(chosen, pick_part, jnp.zeros_like(pick_part)),
-            lanes,
-            preferred_element_type=jnp.float32,
+            pick_pieces[piece], lanes, preferred_element_type=jnp.float32
         )
     outgoing = jnp.concatenate(
         [
@@ -83,25 +110,19 @@
         ],
         axis=-1,
     )
+    if tie is not None:
+        outgoing, full_lhs, part_lhs, tie = lax.optimization_barrier(
+            (outgoing, full_lhs, part_lhs, tie)
+        )
     received = lax.all_to_all(outgoing, "expert", split_axis=0, concat_axis=0, tiled=True)
 
-    extra = width - SUBLANE
     full_rows = received[:, :, :model_width].reshape(wire_rows, model_width)
     part_rows = received[:, :, model_width:].reshape(wire_rows, piece_width)
-    joined_row = (
-        jnp.arange(experts, dtype=jnp.int32)[:, None] * extra
-        + jnp.arange(extra, dtype=jnp.int32)[None, :]
-    ).reshape(-1)
-    joined_count = experts * extra
-    wire_joined = (
-        jnp.arange(experts, dtype=jnp.int32)[:, None] * extra
-        + jnp.arange(SUBLANE, dtype=jnp.int32)[None, :] % extra
-    ).reshape(-1)
     gather_pieces = []
     spread = []
     for piece in range(pieces):
         table = (wire_joined[None, :] == joined_row[:, None]) & (part_piece == piece)[None, :]
-        table = table.astype(jnp.bfloat16)
+        table = jnp.asarray(table, jnp.bfloat16)
         spread.append(table)
         gather_pieces.append(
             jnp.dot(table, part_rows, preferred_element_type=jnp.float32).astype(jnp.bfloat16)
@@ -134,26 +155,9 @@
     back_full = returned[:, :, :model_width].reshape(wire_rows, model_width)
     back_rows = returned[:, :, model_width:].reshape(wire_rows, piece_width)
 
-    weights = combine[:, :, None]
-    mix_full = jnp.sum(jnp.where(hits_full, weights, 0.0), axis=1)
-    mix_part = jnp.sum(jnp.where(hits_part, weights, 0.0), axis=1)
-
-    def split(mix):
-        high = mix.astype(jnp.bfloat16)
-        low = (mix - high.astype(jnp.float32)).astype(jnp.bfloat16)
-        return [high, low]
-
-    full_parts = split(mix_full)
-    full_sum = jnp.dot(
-        jnp.concatenate(full_parts, axis=0), back_full, preferred_element_type=jnp.float32
-    )
+    full_sum = jnp.dot(full_lhs, back_full, preferred_element_type=jnp.float32)
     branch_full = full_sum[:row_count] + full_sum[row_count:]
-    part_parts = []
-    for piece in range(pieces):
-        part_parts += split(jnp.where((part_piece == piece)[None, :], mix_part, 0.0))
-    part_sum = jnp.dot(
-        jnp.concatenate(part_parts, axis=0), back_rows, preferred_element_type=jnp.float32
-    )
+    part_sum = jnp.dot(part_lhs, back_rows, preferred_element_type=jnp.float32)
     branch_part = [
         part_sum[(2 * piece) * row_count:(2 * piece + 1) * row_count]
         + part_sum[(2 * piece + 1) * row_count:(2 * piece + 2) * row_count]
@@ -161,25 +165,37 @@
     ]
     branch_sum = branch_full + jnp.concatenate(branch_part, axis=-1)
     residual = hidden_rows.astype(jnp.float32)
-    return (residual + branch_sum).astype(jnp.bfloat16)
+    return (residual + branch_sum).astype(jnp.bfloat16), tie
 
 
 def local(in_flight, entering, norm_gain, w_gate, w_up, w_down, routes, combine_weight):
     section_index = lax.axis_index("section")
     experts = lax.axis_size("expert") * w_gate.shape[1]
+    row_count, top_count = routes.shape[2], routes.shape[3]
+    block_rows = min(BLOCK_ROWS, row_count)
+    capacity = max(2, min(block_rows, block_rows * top_count // experts * 3 // 2))
+    width = row_count // block_rows * capacity
+    plans = [
+        plan(routes[0, tick_index], combine_weight[0, tick_index], experts)
+        for tick_index in range(TICKS)
+    ]
     carried = in_flight[0]
     gate_up_w = jnp.concatenate([w_gate[0, 0], w_up[0, 0]], axis=-1)
     traced = []
+    tie = plans
     for tick_index in range(TICKS):
-        layer_out = apply_layer(
+        layer_out, tie = apply_layer(
             carried,
             norm_gain[0],
-            routes[0, tick_index],
-            combine_weight[0, tick_index],
+            plans[tick_index] if tick_index else tie[0],
             gate_up_w,
             w_down[0, 0],
             experts,
-        )
+            width,
+            tie if tick_index == 0 else None,
+        )
+        if tick_index == 0:
+            plans = tie
         traced.append(layer_out)
         if tick_index + 1 < TICKS:
             shifted = passed_along(layer_out, "section", 1)

time: 395 us -> 412 us (1.043)
  blocking collectives: 80 us -> 324 us
  waiting for transfers between devices: 221 us -> 6.26 us
  starting transfers between devices: 27.4 us -> 3.18 us
  local copies, waits for them, and re-layouts: 7.36 us -> 18.8 us
  matrix products: 35.6 us -> 30.9 us
    all_to_all x3 -> x0, waiting for transfers between devices: 215 us -> none  [the longest x2 142 us: apply_layer(): lax.all_to_all(back, 'expert', split_axis=0, concat_axis=0, tiled=True)]
    all_to_all x0 -> x2, blocking collectives: none -> 159 us  [apply_layer(): lax.all_to_all(back, 'expert', split_axis=0, concat_axis=0, tiled=True)]
    all_to_all x1 -> x2, blocking collectives: 80 us -> 166 us  [apply_layer(): lax.all_to_all(outgoing, 'expert', split_axis=0, concat_axis=0, tiled=True)]
    all_to_all x3 -> x0, starting transfers between devices: 24 us -> none  [the longest x1 12.3 us: apply_layer(): lax.all_to_all(outgoing, 'expert', split_axis=0, concat_axis=0, tiled=True)]
    dot_general x8, matrix products: 10.7 us -> 5.25 us  [the longest x4 3.5 us: apply_layer(): jnp.dot(pick_pieces[piece], lanes, preferred_element_type=jnp.float32)]
    concatenate x0 -> x2, local copies, waits for them, and re-layouts: none -> 4.56 us  [apply_layer(): joined_rows = jnp.concatenate(gather_pieces, axis=-1)]
    concatenate x0 -> x6, other arithmetic: none -> 4.22 us  [the longest x2 2.09 us: apply_layer(): joined_rows = jnp.concatenate(gather_pieces, axis=-1)]
  transfers between devices with their start and end apart: 4 -> 1, of which waited for: 4 -> 1; matrix products, arithmetic and copies ran while one was open for 1% -> 0% of each run, Pallas kernels for 0% -> 0%
where the time goes in v6:
time: 412 us; the launch traced here: 410 us
  blocking collectives  324 us (79%)
  matrix products  30.9 us (8%)
  other arithmetic  26.4 us (6%)
  local copies, waits for them, and re-layouts  18.8 us (5%)
  waiting for transfers between devices  6.26 us (2%)
    all_to_all x2, blocking collectives, apply_layer(): lax.all_to_all(outgoing, 'expert', split_axis=0, concat_axis=0, tiled=True)  166 us
    all_to_all x2, blocking collectives, apply_layer(): lax.all_to_all(back, 'expert', split_axis=0, concat_axis=0, tiled=True)  159 us
    dot_general x2, matrix products, apply_layer(): gate_up = jnp.dot(inputs, gate_up_w, preferred_element_type=jnp.float32)  13.8 us
  transfers between devices with their start and end apart: 1, of which 1 were waited for; matrix products, arithmetic and copies ran while one was open for 0% of the time, Pallas kernels for 0%

profile of v6, /device:TPU:16, one launch (start us, length us, event | category | flops | bytes accessed | tf_op | source)
XLA Modules:
  0.0 410.3 jit_solution(17262146203708625569)
XLA Ops:
  0.0 0.9 fusion.80
  2.6 2.4 reduce-window.14
  8.0 2.4 reduce-window.16
  12.5 0.9 fusion.70
  13.4 2.0 fusion.24
  15.4 2.0 fusion.27
  18.2 1.4 select_convert_fusion.3
  24.6 85.7 %all_to_all.20 = bf16[64,8,3072]{2,1,0:T(8,128)(2,1)S(1)} all-to-all(bf16[64,8,3072]{2,1,0:T(8,128)(2,1)S(1)} %pad_maximum_fusion.3), channel_id=1, replica_groups=mesh['section'=4,'expert'=64] {'expert'}, dimensions={0} | all-to-all | bytes 6291456 | tf_op jit(solution)/shard_map/all_to_all | solution.py:117
  110.8 1.2 copy-done.1
  112.5 1.0 pad_maximum_fusion.7
  113.5 2.3 copy.43
  115.8 2.0 slice_bitcast_fusion.7
  117.8 0.8 copy-done.22
  118.7 6.9 %fusion.1 = f32[768,1536]{1,0:T(8,128)S(1)} fusion(bf16[2048,768]{1,0:T(8,128)(2,1)S(1)} %bitcast.160, bf16[2048,768]{1,0:T(8,128)(2,1)} %bitcast.162, bf16[256,2048]{1,0:T(8,128)(2,1)S(1)} %copy-done.6, bf16[512,2048]{1,0:T(8,128)(2,1)S(1)} %slice_bitcast_fusion.7), kind=kOutput, calls=%fused_computation.2 | convolution fusion | flops 4850712576 | bytes 14155776 | tf_op jit(solution)/shard_map/dot_general | solution.py:132
  126.3 2.8 convolution_convert_fusion.1
  130.8 79.3 %all_to_all.21 = bf16[64,8,3072]{2,1,0:T(8,128)(2,1)S(1)} all-to-all(bf16[64,8,3072]{2,1,0:T(8,128)(2,1)S(1)} %pad_maximum_fusion.4), channel_id=1, replica_groups=mesh['section'=4,'expert'=64] {'expert'}, dimensions={0} | all-to-all | bytes 6291456 | tf_op jit(solution)/shard_map/all_to_all | solution.py:154
  212.3 3.2 collective-permute-start
  215.5 6.3 %collective-permute-done = bf16[64,2048]{1,0:T(8,128)(2,1)} collective-permute-done((bf16[64,2048]{1,0:T(8,128)(2,1)}, bf16[64,2048]{1,0:T(8,128)(2,1)}, u32[]{:S(2)}, u32[]{:S(2)}) %collective-permute-start) | collective-permute-done | bytes 262176 | tf_op jit(solution)/shard_map/ppermute | solution.py:18
  221.8 1.2 fusion.34
  223.2 1.6 fusion.11
  224.7 1.3 fusion.58
  226.0 1.3 fusion.17
  227.6 80.0 %all_to_all.22 = bf16[64,8,3072]{2,1,0:T(8,128)(2,1)S(1)} all-to-all(bf16[64,8,3072]{2,1,0:T(8,128)(2,1)S(1)} %pad_maximum_fusion.5), channel_id=1, replica_groups=mesh['section'=4,'expert'=64] {'expert'}, dimensions={0} | all-to-all | bytes 6291456 | tf_op jit(solution)/shard_map/all_to_all | solution.py:117
  308.1 1.2 copy-done.2
  309.8 1.0 pad_maximum_fusion.8
  310.8 2.3 copy.44
  313.1 2.0 slice_bitcast_fusion.3
  315.1 0.8 copy-done.23
  316.0 6.9 %fusion = f32[768,1536]{1,0:T(8,128)S(1)} fusion(bf16[2048,768]{1,0:T(8,128)(2,1)S(1)} %bitcast.161, bf16[2048,768]{1,0:T(8,128)(2,1)} %bitcast.163, bf16[256,2048]{1,0:T(8,128)(2,1)S(1)} %copy-done.7, bf16[512,2048]{1,0:T(8,128)(2,1)S(1)} %slice_bitcast_fusion.3), kind=kOutput, calls=%fused_computation.1 | convolution fusion | flops 4850712576 | bytes 14155776 | tf_op jit(solution)/shard_map/dot_general | solution.py:132
  323.6 2.8 convolution_convert_fusion
  328.1 79.3 %all_to_all.23 = bf16[64,8,3072]{2,1,0:T(8,128)(2,1)S(1)} all-to-all(bf16[64,8,3072]{2,1,0:T(8,128)(2,1)S(1)} %pad_maximum_fusion.6), channel_id=1, replica_groups=mesh['section'=4,'expert'=64] {'expert'}, dimensions={0} | all-to-all | bytes 6291456 | tf_op jit(solution)/shard_map/all_to_all | solution.py:154
  408.5 1.8 maximum_bitcast_fusion
  (108 shorter events, 22.8 us)
Async XLA Ops:
  0.0 126.2 %copy-start = (bf16[1,1,768,2048]{3,2,1,0:T(8,128)(2,1)S(1)}, bf16[1,1,768,2048]{3,2,1,0:T(8,128)(2,1)}, u32[]{:S(2)}) copy-start(bf16[1,1,768,2048]{3,2,1,0:T(8,128)(2,1)} %param.29) | copy-start | bytes 9437188
  0.0 19.6 %copy-start.3 = (bf16[1,64,2048]{2,1,0:T(8,128)(2,1)S(1)}, bf16[1,64,2048]{2,1,0:T(8,128)(2,1)}, u32[]{:S(2)}) copy-start(bf16[1,64,2048]{2,1,0:T(8,128)(2,1)} %param.24) | copy-start | bytes 786436
  1.0 1.0 copy-start.17
  1.2 0.7 copy-start.18
  10.7 8.9 %copy-start.19 = (bf16[1,2048]{1,0:T(2,128)(2,1)S(1)}, bf16[1,2048]{1,0:T(2,128)(2,1)}, u32[]{:S(2)}) copy-start(bf16[1,2048]{1,0:T(2,128)(2,1)} %param.26) | copy-start | bytes 12292
  10.8 9.1 %copy-start.21 = (pred[512]{0:T(512)(128)(4,1)S(1)}, pred[512]{0:T(512)(128)(4,1)}, u32[]{:S(2)}) copy-start(pred[512]{0:T(512)(128)(4,1)} %constant.64) | copy-start | bytes 1540
  12.4 8.0 %copy-start.20 = (pred[512]{0:T(512)(128)(4,1)S(1)}, pred[512]{0:T(512)(128)(4,1)}, u32[]{:S(2)}) copy-start(pred[512]{0:T(512)(128)(4,1)} %constant.66) | copy-start | bytes 1540
  24.6 85.7 %copy-start.8 = (bf16[256,512]{1,0:T(8,128)(2,1)S(1)}, bf16[256,512]{1,0:T(8,128)(2,1)}, u32[]{:S(2)}) copy-start(bf16[256,512]{1,0:T(8,128)(2,1)} %constant.54.clone) | copy-start | bytes 786436
  24.6 87.4 %copy-start.12 = (bf16[256,512]{1,0:T(8,128)(2,1)S(1)}, bf16[256,512]{1,0:T(8,128)(2,1)}, u32[]{:S(2)}) copy-start(bf16[256,512]{1,0:T(8,128)(2,1)} %constant.55.clone) | copy-start | bytes 786436
  110.3 1.7 copy-start.1
  115.8 2.0 copy-start.6
  115.8 2.8 copy-start.22
  126.3 2.9 copy-start.9
  129.1 1.0 copy-start.13
  130.8 79.3 %copy-start.5 = (bf16[256,512]{1,0:T(8,128)(2,1)S(1)}, bf16[256,512]{1,0:T(8,128)(2,1)}, u32[]{:S(2)}) copy-start(bf16[256,512]{1,0:T(8,128)(2,1)} %pad_maximum_fusion.9) | copy-start | bytes 786436
  210.2 0.9 copy-start.16
  212.3 9.5 %collective-permute-start = (bf16[64,2048]{1,0:T(8,128)(2,1)}, bf16[64,2048]{1,0:T(8,128)(2,1)}, u32[]{:S(2)}, u32[]{:S(2)}) collective-permute-start(bf16[64,2048]{1,0:T(8,128)(2,1)} %fusion.41), channel_id=1, source_target_pairs={{0,64},{64,128},{128,192},{1,65},{65,129},{129,193},{2,66},{66,130... | collective-permute-start | bytes 786440 | tf_op jit(solution)/shard_map/ppermute | solution.py:18
  227.6 80.0 %copy-start.10 = (bf16[256,512]{1,0:T(8,128)(2,1)S(1)}, bf16[256,512]{1,0:T(8,128)(2,1)}, u32[]{:S(2)}) copy-start(bf16[256,512]{1,0:T(8,128)(2,1)} %constant.54.clone) | copy-start | bytes 786436
  227.6 81.7 %copy-start.14 = (bf16[256,512]{1,0:T(8,128)(2,1)S(1)}, bf16[256,512]{1,0:T(8,128)(2,1)}, u32[]{:S(2)}) copy-start(bf16[256,512]{1,0:T(8,128)(2,1)} %constant.55.clone) | copy-start | bytes 786436
  307.6 1.7 copy-start.2
  313.1 2.0 copy-start.7
  313.1 2.8 copy-start.23
  323.5 2.9 copy-start.11
  326.4 1.0 copy-start.15
  328.1 79.3 %copy-start.4 = (bf16[256,512]{1,0:T(8,128)(2,1)S(1)}, bf16[256,512]{1,0:T(8,128)(2,1)}, u32[]{:S(2)}) copy-start(bf16[256,512]{1,0:T(8,128)(2,1)} %pad_maximum_fusion.10) | copy-start | bytes 786436

commit v7 on v5

--- a/solution.py
+++ b/solution.py
@@ -1,5 +1,6 @@
 import jax
 import jax.numpy as jnp
+import numpy as np
 from jax import lax
 from jax.sharding import PartitionSpec as P
 
@@ -40,11 +41,11 @@
 def wire_slots(experts, width):
     extra = width - SUBLANE
     pieces = SUBLANE // extra
-    row = jnp.arange(SUBLANE, dtype=jnp.int32)
-    base = jnp.arange(experts, dtype=jnp.int32)[:, None] * width
+    row = np.arange(SUBLANE, dtype=np.int32)
+    base = np.arange(experts, dtype=np.int32)[:, None] * width
     full_slot = (base + row[None, :]).reshape(-1)
     part_slot = (base + SUBLANE + row[None, :] % extra).reshape(-1)
-    part_piece = jnp.broadcast_to(row[None, :] // extra, (experts, SUBLANE)).reshape(-1)
+    part_piece = np.broadcast_to(row[None, :] // extra, (experts, SUBLANE)).reshape(-1)
     return full_slot, part_slot, part_piece, pieces
 
 
@@ -88,20 +89,15 @@
     extra = width - SUBLANE
     full_rows = received[:, :, :model_width].reshape(wire_rows, model_width)
     part_rows = received[:, :, model_width:].reshape(wire_rows, piece_width)
-    joined_row = (
-        jnp.arange(experts, dtype=jnp.int32)[:, None] * extra
-        + jnp.arange(extra, dtype=jnp.int32)[None, :]
-    ).reshape(-1)
-    joined_count = experts * extra
-    wire_joined = (
-        jnp.arange(experts, dtype=jnp.int32)[:, None] * extra
-        + jnp.arange(SUBLANE, dtype=jnp.int32)[None, :] % extra
+    joined_row = np.arange(experts * extra, dtype=np.int32)
+    wire_joined = np.asarray(
+        np.arange(experts)[:, None] * extra + np.arange(SUBLANE)[None, :] % extra, np.int32
     ).reshape(-1)
     gather_pieces = []
     spread = []
     for piece in range(pieces):
         table = (wire_joined[None, :] == joined_row[:, None]) & (part_piece == piece)[None, :]
-        table = table.astype(jnp.bfloat16)
+        table = jnp.asarray(table, jnp.bfloat16)
         spread.append(table)
         gather_pieces.append(
             jnp.dot(table, part_rows, preferred_element_type=jnp.float32).astype(jnp.bfloat16)

time: 395 us -> 405 us (1.025)
  blocking collectives: 80 us -> 166 us
  waiting for transfers between devices: 221 us -> 149 us
  starting transfers between devices: 27.4 us -> 15.3 us
  local copies, waits for them, and re-layouts: 7.36 us -> 16 us
    all_to_all x1 -> x2, blocking collectives: 80 us -> 166 us  [apply_layer(): lax.all_to_all(outgoing, 'expert', split_axis=0, concat_axis=0, tiled=True)]
    all_to_all x1 -> x0, waiting for transfers between devices: 73.3 us -> none  [apply_layer(): lax.all_to_all(outgoing, 'expert', split_axis=0, concat_axis=0, tiled=True)]
    all_to_all x1 -> x0, starting transfers between devices: 12.3 us -> none  [apply_layer(): lax.all_to_all(outgoing, 'expert', split_axis=0, concat_axis=0, tiled=True)]
    concatenate x0 -> x2, local copies, waits for them, and re-layouts: none -> 4.56 us  [apply_layer(): joined_rows = jnp.concatenate(gather_pieces, axis=-1)]
  transfers between devices with their start and end apart: 4 -> 3, of which waited for: 4 -> 3; matrix products, arithmetic and copies ran while one was open for 1% -> 1% of each run, Pallas kernels for 0% -> 0%
where the time goes in v7:
time: 405 us
  blocking collectives  166 us (41%)
  waiting for transfers between devices  149 us (37%)
  matrix products  35.2 us (9%)
  other arithmetic  22.6 us (6%)
  local copies, waits for them, and re-layouts  16 us (4%)
  starting transfers between devices  15.3 us (4%)
    all_to_all x2, blocking collectives, apply_layer(): lax.all_to_all(outgoing, 'expert', split_axis=0, concat_axis=0, tiled=True)  166 us
    all_to_all x2, waiting for transfers between devices, apply_layer(): lax.all_to_all(back, 'expert', split_axis=0, concat_axis=0, tiled=True)  143 us
    dot_general x2, matrix products, apply_layer(): gate_up = jnp.dot(inputs, gate_up_w, preferred_element_type=jnp.float32)  13.8 us
    all_to_all x2, starting transfers between devices, apply_layer(): lax.all_to_all(back, 'expert', split_axis=0, concat_axis=0, tiled=True)  11.9 us
  transfers between devices with their start and end apart: 3, of which 3 were waited for; matrix products, arithmetic and copies ran while one was open for 1% of the time, Pallas kernels for 0%

profile of v7, /device:TPU:16, one launch (start us, length us, event | category | flops | bytes accessed | tf_op | source)
XLA Modules:
  0.0 404.5 jit_solution(4369091901258616359)
XLA Ops:
  1.4 1.2 reduce-window.14
  3.2 1.2 reduce-window.16
  5.8 1.1 fusion.38
  6.9 1.1 fusion.40
  8.1 2.7 fusion.25
  12.7 85.7 %all_to_all.20 = bf16[64,8,3072]{2,1,0:T(8,128)(2,1)S(1)} all-to-all(bf16[64,8,3072]{2,1,0:T(8,128)(2,1)S(1)} %pad_maximum_fusion.3), channel_id=1, replica_groups=mesh['section'=4,'expert'=64] {'expert'}, dimensions={0} | all-to-all | bytes 6291456 | tf_op jit(solution)/shard_map/all_to_all | solution.py:87
  98.9 1.2 copy-done.1
  101.6 2.3 copy.40
  103.9 2.0 slice_bitcast_fusion.7
  106.8 6.9 %fusion.1 = f32[768,1536]{1,0:T(8,128)S(1)} fusion(bf16[2048,768]{1,0:T(8,128)(2,1)S(1)} %bitcast.148, bf16[2048,768]{1,0:T(8,128)(2,1)} %bitcast.150, bf16[256,2048]{1,0:T(8,128)(2,1)S(1)} %copy-done.4, bf16[512,2048]{1,0:T(8,128)(2,1)S(1)} %slice_bitcast_fusion.7), kind=kOutput, calls=%fused_computation.2 | convolution fusion | flops 4850712576 | bytes 14155776 | tf_op jit(solution)/shard_map/dot_general | solution.py:107
  114.4 2.8 convolution_convert_fusion.1
  118.7 1.9 pad_maximum_fusion.4
  120.6 5.9 %all-to-all-start.1 = ((bf16[64,8,3072]{2,1,0:T(8,128)(2,1)}), bf16[64,8,3072]{2,1,0:T(8,128)(2,1)}, u32[]{:S(2)}, u32[]{:S(2)}) async-start(bf16[64,8,3072]{2,1,0:T(8,128)(2,1)} %pad_maximum_fusion.4), calls=%async_computation.1 | async-start | bytes 6291456 | tf_op jit(solution)/shard_map/all_to_all | solution.py:129
  126.8 1.9 fusion.27
  130.0 70.3 %all-to-all-done.1 = bf16[64,8,3072]{2,1,0:T(8,128)(2,1)} async-done(((bf16[64,8,3072]{2,1,0:T(8,128)(2,1)}), bf16[64,8,3072]{2,1,0:T(8,128)(2,1)}, u32[]{:S(2)}, u32[]{:S(2)}) %all-to-all-start.1) | async-done | bytes 3145760 | tf_op jit(solution)/shard_map/all_to_all | solution.py:129
  200.3 1.8 fusion.33
  202.1 2.0 fusion.15
  204.3 3.4 collective-permute-start
  207.7 5.5 %collective-permute-done = bf16[64,2048]{1,0:T(8,128)(2,1)} collective-permute-done((bf16[64,2048]{1,0:T(8,128)(2,1)S(1)}, bf16[64,2048]{1,0:T(8,128)(2,1)}, u32[]{:S(2)}, u32[]{:S(2)}) %collective-permute-start) | collective-permute-done | bytes 262176 | tf_op jit(solution)/shard_map/ppermute | solution.py:18
  213.3 1.2 fusion.34
  214.6 1.6 fusion.11
  217.5 80.3 %all_to_all.21 = bf16[64,8,3072]{2,1,0:T(8,128)(2,1)S(1)} all-to-all(bf16[64,8,3072]{2,1,0:T(8,128)(2,1)S(1)} %pad_maximum_fusion.5), channel_id=1, replica_groups=mesh['section'=4,'expert'=64] {'expert'}, dimensions={0} | all-to-all | bytes 6291456 | tf_op jit(solution)/shard_map/all_to_all | solution.py:87
  298.3 1.2 copy-done.2
  301.0 2.3 copy.44
  303.3 2.0 slice_bitcast_fusion.3
  306.1 6.9 %fusion = f32[768,1536]{1,0:T(8,128)S(1)} fusion(bf16[2048,768]{1,0:T(8,128)(2,1)S(1)} %bitcast.149, bf16[2048,768]{1,0:T(8,128)(2,1)} %bitcast.151, bf16[256,2048]{1,0:T(8,128)(2,1)S(1)} %copy-done.5, bf16[512,2048]{1,0:T(8,128)(2,1)S(1)} %slice_bitcast_fusion.3), kind=kOutput, calls=%fused_computation.1 | convolution fusion | flops 4850712576 | bytes 14155776 | tf_op jit(solution)/shard_map/dot_general | solution.py:107
  313.7 2.8 convolution_convert_fusion
  318.0 1.9 pad_maximum_fusion.6
  319.9 5.9 %all-to-all-start.3 = ((bf16[64,8,3072]{2,1,0:T(8,128)(2,1)}), bf16[64,8,3072]{2,1,0:T(8,128)(2,1)}, u32[]{:S(2)}, u32[]{:S(2)}) async-start(bf16[64,8,3072]{2,1,0:T(8,128)(2,1)} %pad_maximum_fusion.6), calls=%async_computation.3 | async-start | bytes 6291456 | tf_op jit(solution)/shard_map/all_to_all | solution.py:129
  326.5 73.1 %all-to-all-done.3 = bf16[64,8,3072]{2,1,0:T(8,128)(2,1)} async-done(((bf16[64,8,3072]{2,1,0:T(8,128)(2,1)}), bf16[64,8,3072]{2,1,0:T(8,128)(2,1)}, u32[]{:S(2)}, u32[]{:S(2)}) %all-to-all-start.3) | async-done | bytes 3145760 | tf_op jit(solution)/shard_map/all_to_all | solution.py:129
  399.6 1.8 fusion.32
  401.5 2.0 fusion.14
  (115 shorter events, 20.0 us)
Async XLA Ops:
  0.0 114.4 %copy-start = (bf16[1,1,768,2048]{3,2,1,0:T(8,128)(2,1)S(1)}, bf16[1,1,768,2048]{3,2,1,0:T(8,128)(2,1)}, u32[]{:S(2)}) copy-start(bf16[1,1,768,2048]{3,2,1,0:T(8,128)(2,1)} %param.29) | copy-start | bytes 9437188
  0.0 11.5 %copy-start.26 = (pred[512]{0:T(512)(128)(4,1)S(1)}, pred[512]{0:T(512)(128)(4,1)}, u32[]{:S(2)}) copy-start(pred[512]{0:T(512)(128)(4,1)} %constant.64) | copy-start | bytes 1540
  6.9 5.1 %copy-start.25 = (pred[512]{0:T(512)(128)(4,1)S(1)}, pred[512]{0:T(512)(128)(4,1)}, u32[]{:S(2)}) copy-start(pred[512]{0:T(512)(128)(4,1)} %constant.66) | copy-start | bytes 1540
  8.1 3.4 copy-start.16
  8.1 3.4 copy-start.18
  12.7 85.7 %copy-start.8 = (bf16[256,512]{1,0:T(8,128)(2,1)S(1)}, bf16[256,512]{1,0:T(8,128)(2,1)}, u32[]{:S(2)}) copy-start(bf16[256,512]{1,0:T(8,128)(2,1)} %constant.52.clone) | copy-start | bytes 786436
  12.7 87.4 %copy-start.11 = (bf16[256,512]{1,0:T(8,128)(2,1)S(1)}, bf16[256,512]{1,0:T(8,128)(2,1)}, u32[]{:S(2)}) copy-start(bf16[256,512]{1,0:T(8,128)(2,1)} %constant.53.clone) | copy-start | bytes 786436
  98.4 1.7 copy-start.1
  103.9 2.0 copy-start.4
  103.9 2.8 copy-start.27
  117.2 1.0 copy-start.12
  120.6 6.0 %copy-start.24 = (f32[1,2,64,8]{2,3,1,0:T(8,128)S(1)}, f32[1,2,64,8]{2,3,1,0:T(8,128)}, u32[]{:S(2)}) copy-start(f32[1,2,64,8]{2,3,1,0:T(8,128)} %param.31) | copy-start | bytes 12292
  120.6 6.2 %copy-start.17 = (s32[64,8]{1,0:T(8,128)S(1)}, s32[64,8]{1,0:T(8,128)}, u32[]{:S(2)}) copy-start(s32[64,8]{1,0:T(8,128)} %copy-done.16) | copy-start | bytes 6148
  120.6 6.2 %copy-start.19 = (s32[64,8]{1,0:T(8,128)S(1)}, s32[64,8]{1,0:T(8,128)}, u32[]{:S(2)}) copy-start(s32[64,8]{1,0:T(8,128)} %copy-done.18) | copy-start | bytes 6148
  120.6 6.2 %copy-start.22 = (s32[512]{0:T(512)S(1)}, s32[512]{0:T(512)}, u32[]{:S(2)}) copy-start(s32[512]{0:T(512)} %constant.63) | copy-start | bytes 6148
  120.6 6.2 %copy-start.23 = (s32[512]{0:T(512)S(1)}, s32[512]{0:T(512)}, u32[]{:S(2)}) copy-start(s32[512]{0:T(512)} %constant.65) | copy-start | bytes 6148
  120.6 79.7 %all-to-all-start.1 = ((bf16[64,8,3072]{2,1,0:T(8,128)(2,1)}), bf16[64,8,3072]{2,1,0:T(8,128)(2,1)}, u32[]{:S(2)}, u32[]{:S(2)}) async-start(bf16[64,8,3072]{2,1,0:T(8,128)(2,1)} %pad_maximum_fusion.4), calls=%async_computation.1 | async-start | bytes 6291456 | tf_op jit(solution)/shard_map/all_to_all | solution.py:129
  200.3 3.9 copy-start.3
  204.3 3.4 copy-start.6
  204.3 9.0 %collective-permute-start = (bf16[64,2048]{1,0:T(8,128)(2,1)S(1)}, bf16[64,2048]{1,0:T(8,128)(2,1)}, u32[]{:S(2)}, u32[]{:S(2)}) collective-permute-start(bf16[64,2048]{1,0:T(8,128)(2,1)S(1)} %fusion.41), channel_id=1, source_target_pairs={{0,64},{64,128},{128,192},{1,65},{65,129},{129,193},{2,66},{66,130... | collective-permute-start | bytes 786440 | tf_op jit(solution)/shard_map/ppermute | solution.py:18
  217.5 80.3 %copy-start.9 = (bf16[256,512]{1,0:T(8,128)(2,1)S(1)}, bf16[256,512]{1,0:T(8,128)(2,1)}, u32[]{:S(2)}) copy-start(bf16[256,512]{1,0:T(8,128)(2,1)} %constant.52.clone) | copy-start | bytes 786436
  217.5 82.0 %copy-start.13 = (bf16[256,512]{1,0:T(8,128)(2,1)S(1)}, bf16[256,512]{1,0:T(8,128)(2,1)}, u32[]{:S(2)}) copy-start(bf16[256,512]{1,0:T(8,128)(2,1)} %constant.53.clone) | copy-start | bytes 786436
  297.8 1.7 copy-start.2
  303.3 2.0 copy-start.5
  303.3 2.8 copy-start.28
  313.7 2.9 copy-start.10
  316.6 1.0 copy-start.14
  319.9 5.9 %copy-start.15 = (f32[64,512]{1,0:T(8,128)S(1)}, f32[64,512]{1,0:T(8,128)}, u32[]{:S(2)}) copy-start(f32[64,512]{1,0:T(8,128)} %get-tuple-element.16) | copy-start | bytes 393220
  319.9 79.7 %all-to-all-start.3 = ((bf16[64,8,3072]{2,1,0:T(8,128)(2,1)}), bf16[64,8,3072]{2,1,0:T(8,128)(2,1)}, u32[]{:S(2)}, u32[]{:S(2)}) async-start(bf16[64,8,3072]{2,1,0:T(8,128)(2,1)} %pad_maximum_fusion.6), calls=%async_computation.3 | async-start | bytes 6291456 | tf_op jit(solution)/shard_map/all_to_all | solution.py:129
  326.5 75.0 %copy-start.20 = (bf16[64,512]{1,0:T(8,128)(2,1)S(1)}, bf16[64,512]{1,0:T(8,128)(2,1)}, u32[]{:S(2)}) copy-start(bf16[64,512]{1,0:T(8,128)(2,1)} %get-tuple-element.17) | copy-start | bytes 196612
  326.5 75.0 %copy-start.21 = (bf16[64,512]{1,0:T(8,128)(2,1)S(1)}, bf16[64,512]{1,0:T(8,128)(2,1)}, u32[]{:S(2)}) copy-start(bf16[64,512]{1,0:T(8,128)(2,1)} %get-tuple-element.18) | copy-start | bytes 196612
  401.4 2.3 copy-start.7

commit v8 on v5

--- a/solution.py
+++ b/solution.py
@@ -131,6 +131,7 @@
         axis=-1,
     )
     returned = lax.all_to_all(back, "expert", split_axis=0, concat_axis=0, tiled=True)
+    sent_back = back
     back_full = returned[:, :, :model_width].reshape(wire_rows, model_width)
     back_rows = returned[:, :, model_width:].reshape(wire_rows, piece_width)
 
@@ -161,7 +162,7 @@
     ]
     branch_sum = branch_full + jnp.concatenate(branch_part, axis=-1)
     residual = hidden_rows.astype(jnp.float32)
-    return (residual + branch_sum).astype(jnp.bfloat16)
+    return (residual + branch_sum).astype(jnp.bfloat16), sent_back
 
 
 def local(in_flight, entering, norm_gain, w_gate, w_up, w_down, routes, combine_weight):
@@ -170,18 +171,23 @@
     carried = in_flight[0]
     gate_up_w = jnp.concatenate([w_gate[0, 0], w_up[0, 0]], axis=-1)
     traced = []
+    step_routes = routes[0, 0]
+    step_combine = combine_weight[0, 0]
     for tick_index in range(TICKS):
-        layer_out = apply_layer(
+        layer_out, sent_back = apply_layer(
             carried,
             norm_gain[0],
-            routes[0, tick_index],
-            combine_weight[0, tick_index],
+            step_routes,
+            step_combine,
             gate_up_w,
             w_down[0, 0],
             experts,
         )
         traced.append(layer_out)
         if tick_index + 1 < TICKS:
+            _, step_routes, step_combine = lax.optimization_barrier(
+                (sent_back, routes[0, tick_index + 1], combine_weight[0, tick_index + 1])
+            )
             shifted = passed_along(layer_out, "section", 1)
             carried = jnp.where(section_index == 0, entering[tick_index], shifted)
     return jnp.stack(traced)[:, None]

time: 395 us -> 392 us (level)
  waiting for transfers between devices: 221 us -> 216 us
    all_to_all x2, waiting for transfers between devices: 142 us -> 138 us  [apply_layer(): lax.all_to_all(back, 'expert', split_axis=0, concat_axis=0, tiled=True)]
  transfers between devices with their start and end apart: 4 -> 4, of which waited for: 4 -> 4; matrix products, arithmetic and copies ran while one was open for 1% -> 3% of each run, Pallas kernels for 0% -> 0%
where the time goes in v8:
time: 392 us; the launch traced here: 391 us
  waiting for transfers between devices  216 us (55%)
  blocking collectives  80 us (20%)
  matrix products  34.2 us (9%)
  starting transfers between devices  27 us (7%)
  other arithmetic  25.3 us (6%)
  local copies, waits for them, and re-layouts  8.43 us (2%)
    all_to_all x2, waiting for transfers between devices, apply_layer(): lax.all_to_all(back, 'expert', split_axis=0, concat_axis=0, tiled=True)  138 us
    all_to_all x1, blocking collectives, apply_layer(): lax.all_to_all(outgoing, 'expert', split_axis=0, concat_axis=0, tiled=True)  80 us
    all_to_all x1, waiting for transfers between devices, apply_layer(): lax.all_to_all(outgoing, 'expert', split_axis=0, concat_axis=0, tiled=True)  73.5 us
    all_to_all x1, starting transfers between devices, apply_layer(): lax.all_to_all(outgoing, 'expert', split_axis=0, concat_axis=0, tiled=True)  12.2 us
    all_to_all x2, starting transfers between devices, apply_layer(): lax.all_to_all(back, 'expert', split_axis=0, concat_axis=0, tiled=True)  11.7 us
    dot_general x2, matrix products, apply_layer(): gate_up = jnp.dot(inputs, gate_up_w, preferred_element_type=jnp.float32)  10.1 us
  transfers between devices with their start and end apart: 4, of which 4 were waited for; matrix products, arithmetic and copies ran while one was open for 3% of the time, Pallas kernels for 0%

profile of v8, /device:TPU:16, one launch (start us, length us, event | category | flops | bytes accessed | tf_op | source)
XLA Modules:
  0.0 391.4 jit_solution(11759490788731506229)
XLA Ops:
  1.2 1.1 fusion.40
  4.3 1.2 reduce-window.14
  9.6 1.9 pad_maximum_fusion.3
  11.5 12.2 %all-to-all-start = ((bf16[64,8,3072]{2,1,0:T(8,128)(2,1)}), bf16[64,8,3072]{2,1,0:T(8,128)(2,1)}, u32[]{:S(2)}, u32[]{:S(2)}) async-start(bf16[64,8,3072]{2,1,0:T(8,128)(2,1)} %pad_maximum_fusion.3), calls=%async_computation | async-start | bytes 6291456 | tf_op jit(solution)/shard_map/all_to_all | solution.py:86
  23.9 73.5 %all-to-all-done = bf16[64,8,3072]{2,1,0:T(8,128)(2,1)} async-done(((bf16[64,8,3072]{2,1,0:T(8,128)(2,1)}), bf16[64,8,3072]{2,1,0:T(8,128)(2,1)}, u32[]{:S(2)}, u32[]{:S(2)}) %all-to-all-start) | async-done | bytes 3145760 | tf_op jit(solution)/shard_map/all_to_all | solution.py:86
  97.4 1.7 convolution_convert_fusion.6
  99.1 1.9 convolution_convert_fusion.7
  101.0 2.0 slice_bitcast_fusion.7
  103.0 5.0 %fusion.1 = f32[768,1536]{1,0:T(8,128)S(1)} fusion(bf16[2048,768]{1,0:T(8,128)(2,1)S(1)} %bitcast.124, bf16[2048,768]{1,0:T(8,128)(2,1)S(1)} %bitcast.126, bf16[256,1024]{1,0:T(8,128)(2,1)S(1)} %convolution_convert_fusion.6, bf16[256,1024]{1,0:T(8,128)(2,1)S(1)} %convolution_convert_fusion.7, bf16[512,2048]{1,0:T(8,128)(2,1)S(1)} %slice_bitcast_fusion.7), kind=kOutput, calls=%fused_computation.2 | convolution fusion | flops 4853858304 | bytes 14155776 | tf_op jit(solution)/shard_map/dot_general | solution.py:111
  108.7 2.8 convolution_convert_fusion.1
  113.0 1.9 pad_maximum_fusion.4
  114.9 5.9 %all-to-all-start.1 = ((bf16[64,8,3072]{2,1,0:T(8,128)(2,1)}), bf16[64,8,3072]{2,1,0:T(8,128)(2,1)}, u32[]{:S(2)}, u32[]{:S(2)}) async-start(bf16[64,8,3072]{2,1,0:T(8,128)(2,1)} %pad_maximum_fusion.4), calls=%async_computation.1 | async-start | bytes 6291456 | tf_op jit(solution)/shard_map/all_to_all | solution.py:133
  121.8 1.2 reduce-window.16
  124.9 2.0 fusion.27
  127.0 1.4 subtract_convert_fusion.4
  128.3 1.4 select_convert_fusion.3
  129.7 64.9 %all-to-all-done.1 = bf16[64,8,3072]{2,1,0:T(8,128)(2,1)} async-done(((bf16[64,8,3072]{2,1,0:T(8,128)(2,1)}), bf16[64,8,3072]{2,1,0:T(8,128)(2,1)}, u32[]{:S(2)}, u32[]{:S(2)}) %all-to-all-start.1) | async-done | bytes 3145760 | tf_op jit(solution)/shard_map/all_to_all | solution.py:133
  194.6 1.8 fusion.33
  196.4 2.0 fusion.19
  198.6 3.2 collective-permute-start
  201.8 1.5 fusion.29
  203.3 4.4 %collective-permute-done = bf16[64,2048]{1,0:T(8,128)(2,1)} collective-permute-done((bf16[64,2048]{1,0:T(8,128)(2,1)S(1)}, bf16[64,2048]{1,0:T(8,128)(2,1)}, u32[]{:S(2)}, u32[]{:S(2)}) %collective-permute-start) | collective-permute-done | bytes 262176 | tf_op jit(solution)/shard_map/ppermute | solution.py:17
  207.7 1.2 fusion.36
  211.6 80.0 %all_to_all.20 = bf16[64,8,3072]{2,1,0:T(8,128)(2,1)S(1)} all-to-all(bf16[64,8,3072]{2,1,0:T(8,128)(2,1)S(1)} %pad_maximum_fusion.5), channel_id=1, replica_groups=mesh['section'=4,'expert'=64] {'expert'}, dimensions={0} | all-to-all | bytes 6291456 | tf_op jit(solution)/shard_map/all_to_all | solution.py:86
  292.8 1.2 copy-done.17
  295.0 5.0 %fusion = f32[768,1536]{1,0:T(8,128)S(1)} fusion(bf16[2048,768]{1,0:T(8,128)(2,1)S(1)} %bitcast.125, bf16[2048,768]{1,0:T(8,128)(2,1)S(1)} %bitcast.127, bf16[256,1024]{1,0:T(8,128)(2,1)S(1)} %convolution_convert_fusion.4, bf16[256,1024]{1,0:T(8,128)(2,1)S(1)} %convolution_convert_fusion.5, bf16[512,2048]{1,0:T(8,128)(2,1)S(1)} %slice_bitcast_fusion.3), kind=kOutput, calls=%fused_computation.1 | convolution fusion | flops 4853858304 | bytes 14155776 | tf_op jit(solution)/shard_map/dot_general | solution.py:111
  300.8 2.8 convolution_convert_fusion
  305.0 1.9 pad_maximum_fusion.6
  306.9 5.8 %all-to-all-start.3 = ((bf16[64,8,3072]{2,1,0:T(8,128)(2,1)}), bf16[64,8,3072]{2,1,0:T(8,128)(2,1)}, u32[]{:S(2)}, u32[]{:S(2)}) async-start(bf16[64,8,3072]{2,1,0:T(8,128)(2,1)} %pad_maximum_fusion.6), calls=%async_computation.3 | async-start | bytes 6291456 | tf_op jit(solution)/shard_map/all_to_all | solution.py:133
  313.4 73.1 %all-to-all-done.3 = bf16[64,8,3072]{2,1,0:T(8,128)(2,1)} async-done(((bf16[64,8,3072]{2,1,0:T(8,128)(2,1)}), bf16[64,8,3072]{2,1,0:T(8,128)(2,1)}, u32[]{:S(2)}, u32[]{:S(2)}) %all-to-all-start.3) | async-done | bytes 3145760 | tf_op jit(solution)/shard_map/all_to_all | solution.py:133
  386.4 1.8 fusion.32
  388.4 2.0 fusion.18
  (113 shorter events, 21.0 us)
Async XLA Ops:
  0.0 108.7 %copy-start = (bf16[1,1,768,2048]{3,2,1,0:T(8,128)(2,1)S(1)}, bf16[1,1,768,2048]{3,2,1,0:T(8,128)(2,1)}, u32[]{:S(2)}) copy-start(bf16[1,1,768,2048]{3,2,1,0:T(8,128)(2,1)} %param.13) | copy-start | bytes 9437188
  3.0 6.1 %copy-start.15 = (s32[64]{0:T(128)}, s32[64]{0:T(128)S(1)}, u32[]{:S(2)}) copy-start(s32[64]{0:T(128)S(1)} %add.396) | copy-start | bytes 772
  3.1 108.5 %copy-start.10 = (pred[512]{0:T(512)(128)(4,1)}, pred[512]{0:T(512)(128)(4,1)S(1)}, u32[]{:S(2)}) copy-start(pred[512]{0:T(512)(128)(4,1)S(1)} %eq.292) | copy-start | bytes 1540
  3.2 109.2 %copy-start.12 = (pred[512]{0:T(512)(128)(4,1)}, pred[512]{0:T(512)(128)(4,1)S(1)}, u32[]{:S(2)}) copy-start(pred[512]{0:T(512)(128)(4,1)S(1)} %eq.296) | copy-start | bytes 1540
  4.3 4.8 %copy-start.7 = (s32[512]{0:T(512)}, s32[512]{0:T(512)S(1)}, u32[]{:S(2)}) copy-start(s32[512]{0:T(512)S(1)} %add.410) | copy-start | bytes 6148
  11.5 85.9 %all-to-all-start = ((bf16[64,8,3072]{2,1,0:T(8,128)(2,1)}), bf16[64,8,3072]{2,1,0:T(8,128)(2,1)}, u32[]{:S(2)}, u32[]{:S(2)}) async-start(bf16[64,8,3072]{2,1,0:T(8,128)(2,1)} %pad_maximum_fusion.3), calls=%async_computation | async-start | bytes 6291456 | tf_op jit(solution)/shard_map/all_to_all | solution.py:86
  23.8 88.6 %copy-start.8 = (s32[256]{0:T(256)}, s32[256]{0:T(256)S(1)}, u32[]{:S(2)}) copy-start(s32[256]{0:T(256)S(1)} %add.418) | copy-start | bytes 3076
  99.1 3.9 copy-start.16
  99.1 3.9 copy-start.18
  114.9 6.0 %copy-start.14 = (f32[1,2,64,8]{2,3,1,0:T(8,128)S(1)}, f32[1,2,64,8]{2,3,1,0:T(8,128)}, u32[]{:S(2)}) copy-start(f32[1,2,64,8]{2,3,1,0:T(8,128)} %param.15) | copy-start | bytes 12292
  114.9 79.6 %all-to-all-start.1 = ((bf16[64,8,3072]{2,1,0:T(8,128)(2,1)}), bf16[64,8,3072]{2,1,0:T(8,128)(2,1)}, u32[]{:S(2)}, u32[]{:S(2)}) async-start(bf16[64,8,3072]{2,1,0:T(8,128)(2,1)} %pad_maximum_fusion.4), calls=%async_computation.1 | async-start | bytes 6291456 | tf_op jit(solution)/shard_map/all_to_all | solution.py:133
  124.9 73.6 %copy-start.4 = (s32[64,8]{1,0:T(8,128)}, s32[64,8]{1,0:T(8,128)S(1)}, u32[]{:S(2)}) copy-start(s32[64,8]{1,0:T(8,128)S(1)} %add_add_fusion) | copy-start | bytes 6148
  194.6 3.9 %copy-start.1 = (bf16[1,64,2048]{2,1,0:T(8,128)(2,1)S(1)}, bf16[1,64,2048]{2,1,0:T(8,128)(2,1)}, u32[]{:S(2)}) copy-start(bf16[1,64,2048]{2,1,0:T(8,128)(2,1)} %param.8) | copy-start | bytes 786436
  198.6 4.7 %copy-start.2 = (bf16[64,2048]{1,0:T(8,128)(2,1)}, bf16[64,2048]{1,0:T(8,128)(2,1)S(1)}, u32[]{:S(2)}) copy-start(bf16[64,2048]{1,0:T(8,128)(2,1)S(1)} %fusion.43) | copy-start | bytes 786436
  198.6 9.1 %collective-permute-start = (bf16[64,2048]{1,0:T(8,128)(2,1)S(1)}, bf16[64,2048]{1,0:T(8,128)(2,1)}, u32[]{:S(2)}, u32[]{:S(2)}) collective-permute-start(bf16[64,2048]{1,0:T(8,128)(2,1)S(1)} %fusion.43), channel_id=1, source_target_pairs={{0,64},{64,128},{128,192},{1,65},{65,129},{129,193},{2,66},{66,130... | collective-permute-start | bytes 786440 | tf_op jit(solution)/shard_map/ppermute | solution.py:17
  203.3 7.6 %copy-start.13 = (pred[512]{0:T(512)(128)(4,1)S(1)}, pred[512]{0:T(512)(128)(4,1)}, u32[]{:S(2)}) copy-start(pred[512]{0:T(512)(128)(4,1)} %copy-done.12) | copy-start | bytes 1540
  211.6 80.0 %copy-start.9 = (s32[256]{0:T(256)S(1)}, s32[256]{0:T(256)}, u32[]{:S(2)}) copy-start(s32[256]{0:T(256)} %copy-done.8) | copy-start | bytes 3076
  211.6 80.5 %copy-start.11 = (pred[512]{0:T(512)(128)(4,1)S(1)}, pred[512]{0:T(512)(128)(4,1)}, u32[]{:S(2)}) copy-start(pred[512]{0:T(512)(128)(4,1)} %copy-done.10) | copy-start | bytes 1540
  292.2 1.9 copy-start.17
  292.2 2.8 copy-start.19
  306.9 79.5 %all-to-all-start.3 = ((bf16[64,8,3072]{2,1,0:T(8,128)(2,1)}), bf16[64,8,3072]{2,1,0:T(8,128)(2,1)}, u32[]{:S(2)}, u32[]{:S(2)}) async-start(bf16[64,8,3072]{2,1,0:T(8,128)(2,1)} %pad_maximum_fusion.6), calls=%async_computation.3 | async-start | bytes 6291456 | tf_op jit(solution)/shard_map/all_to_all | solution.py:133
  313.4 75.0 %copy-start.5 = (bf16[64,512]{1,0:T(8,128)(2,1)S(1)}, bf16[64,512]{1,0:T(8,128)(2,1)}, u32[]{:S(2)}) copy-start(bf16[64,512]{1,0:T(8,128)(2,1)} %get-tuple-element.19) | copy-start | bytes 196612
  313.4 75.0 %copy-start.6 = (bf16[64,512]{1,0:T(8,128)(2,1)S(1)}, bf16[64,512]{1,0:T(8,128)(2,1)}, u32[]{:S(2)}) copy-start(bf16[64,512]{1,0:T(8,128)(2,1)} %get-tuple-element.20) | copy-start | bytes 196612
  388.3 2.2 copy-start.3

commit v9 on v8

--- a/solution.py
+++ b/solution.py
@@ -97,16 +97,17 @@
         jnp.arange(experts, dtype=jnp.int32)[:, None] * extra
         + jnp.arange(SUBLANE, dtype=jnp.int32)[None, :] % extra
     ).reshape(-1)
-    gather_pieces = []
     spread = []
     for piece in range(pieces):
         table = (wire_joined[None, :] == joined_row[:, None]) & (part_piece == piece)[None, :]
-        table = table.astype(jnp.bfloat16)
-        spread.append(table)
-        gather_pieces.append(
-            jnp.dot(table, part_rows, preferred_element_type=jnp.float32).astype(jnp.bfloat16)
-        )
-    joined_rows = jnp.concatenate(gather_pieces, axis=-1)
+        spread.append(table.astype(jnp.bfloat16))
+    gathered = jnp.dot(
+        jnp.concatenate(spread, axis=0), part_rows, preferred_element_type=jnp.float32
+    ).astype(jnp.bfloat16)
+    joined_rows = jnp.concatenate(
+        [gathered[piece * joined_count:(piece + 1) * joined_count] for piece in range(pieces)],
+        axis=-1,
+    )
     inputs = jnp.concatenate([full_rows, joined_rows], axis=0)
     gate_up = jnp.dot(inputs, gate_up_w, preferred_element_type=jnp.float32)
     ff = gate_up.shape[-1] // 2

time: 392 us -> 392 us (level)
  no operation moved by 1% of the time
where the time goes in v9:
time: 392 us; the launch traced here: 391 us
  waiting for transfers between devices  216 us (55%)
  blocking collectives  80.2 us (20%)
  matrix products  32.2 us (8%)
  starting transfers between devices  27 us (7%)
  other arithmetic  25.4 us (6%)
  local copies, waits for them, and re-layouts  10.3 us (3%)
    all_to_all x2, waiting for transfers between devices, apply_layer(): lax.all_to_all(back, 'expert', split_axis=0, concat_axis=0, tiled=True)  138 us
    all_to_all x1, blocking collectives, apply_layer(): lax.all_to_all(outgoing, 'expert', split_axis=0, concat_axis=0, tiled=True)  80.2 us
    all_to_all x1, waiting for transfers between devices, apply_layer(): lax.all_to_all(outgoing, 'expert', split_axis=0, concat_axis=0, tiled=True)  73.2 us
    all_to_all x1, starting transfers between devices, apply_layer(): lax.all_to_all(outgoing, 'expert', split_axis=0, concat_axis=0, tiled=True)  12.2 us
    all_to_all x2, starting transfers between devices, apply_layer(): lax.all_to_all(back, 'expert', split_axis=0, concat_axis=0, tiled=True)  11.7 us
    dot_general x2, matrix products, apply_layer(): gate_up = jnp.dot(inputs, gate_up_w, preferred_element_type=jnp.float32)  10.1 us
  transfers between devices with their start and end apart: 4, of which 4 were waited for; matrix products, arithmetic and copies ran while one was open for 3% of the time, Pallas kernels for 0%

profile of v9, /device:TPU:16, one launch (start us, length us, event | category | flops | bytes accessed | tf_op | source)
XLA Modules:
  0.0 391.5 jit_solution(16935005833645508329)
XLA Ops:
  1.2 1.1 fusion.38
  4.3 1.2 reduce-window.14
  6.1 1.1 fusion.40
  9.6 1.9 pad_maximum_fusion.3
  11.5 12.2 %all-to-all-start = ((bf16[64,8,3072]{2,1,0:T(8,128)(2,1)}), bf16[64,8,3072]{2,1,0:T(8,128)(2,1)}, u32[]{:S(2)}, u32[]{:S(2)}) async-start(bf16[64,8,3072]{2,1,0:T(8,128)(2,1)} %pad_maximum_fusion.3), calls=%async_computation | async-start | bytes 6291456 | tf_op jit(solution)/shard_map/all_to_all | solution.py:86
  24.2 73.2 %all-to-all-done = bf16[64,8,3072]{2,1,0:T(8,128)(2,1)} async-done(((bf16[64,8,3072]{2,1,0:T(8,128)(2,1)}), bf16[64,8,3072]{2,1,0:T(8,128)(2,1)}, u32[]{:S(2)}, u32[]{:S(2)}) %all-to-all-start) | async-done | bytes 3145760 | tf_op jit(solution)/shard_map/all_to_all | solution.py:86
  97.4 1.9 convolution_convert_fusion.5
  99.4 1.9 slice_bitcast_fusion.7
  102.8 5.0 %fusion.1 = f32[768,1536]{1,0:T(8,128)S(1)} fusion(bf16[2048,768]{1,0:T(8,128)(2,1)S(1)} %bitcast.122, bf16[2048,768]{1,0:T(8,128)(2,1)S(1)} %bitcast.124, bf16[256,1024]{1,0:T(8,128)(2,1)S(1)} %get-tuple-element.32, bf16[256,1024]{1,0:T(8,128)(2,1)S(1)} %get-tuple-element.31, bf16[512,2048]{1,0:T(8,128)(2,1)S(1)} %slice_bitcast_fusion.7), kind=kOutput, calls=%fused_computation.2 | convolution fusion | flops 4853858304 | bytes 14155776 | tf_op jit(solution)/shard_map/dot_general | solution.py:112
  108.5 2.8 convolution_convert_fusion.1
  112.8 1.9 pad_maximum_fusion.4
  114.7 5.9 %all-to-all-start.1 = ((bf16[64,8,3072]{2,1,0:T(8,128)(2,1)}), bf16[64,8,3072]{2,1,0:T(8,128)(2,1)}, u32[]{:S(2)}, u32[]{:S(2)}) async-start(bf16[64,8,3072]{2,1,0:T(8,128)(2,1)} %pad_maximum_fusion.4), calls=%async_computation.1 | async-start | bytes 6291456 | tf_op jit(solution)/shard_map/all_to_all | solution.py:134
  121.6 1.2 reduce-window.16
  124.7 2.0 fusion.27
  126.7 1.3 subtract_convert_fusion.4
  128.1 1.3 select_convert_fusion.3
  129.4 64.9 %all-to-all-done.1 = bf16[64,8,3072]{2,1,0:T(8,128)(2,1)} async-done(((bf16[64,8,3072]{2,1,0:T(8,128)(2,1)}), bf16[64,8,3072]{2,1,0:T(8,128)(2,1)}, u32[]{:S(2)}, u32[]{:S(2)}) %all-to-all-start.1) | async-done | bytes 3145760 | tf_op jit(solution)/shard_map/all_to_all | solution.py:134
  194.3 1.8 fusion.33
  196.2 2.0 fusion.19
  198.4 3.2 collective-permute-start
  201.6 1.5 fusion.29
  203.1 4.4 %collective-permute-done = bf16[64,2048]{1,0:T(8,128)(2,1)} collective-permute-done((bf16[64,2048]{1,0:T(8,128)(2,1)S(1)}, bf16[64,2048]{1,0:T(8,128)(2,1)}, u32[]{:S(2)}, u32[]{:S(2)}) %collective-permute-start) | collective-permute-done | bytes 262176 | tf_op jit(solution)/shard_map/ppermute | solution.py:17
  207.5 1.2 fusion.34
  211.4 80.2 %all_to_all.20 = bf16[64,8,3072]{2,1,0:T(8,128)(2,1)S(1)} all-to-all(bf16[64,8,3072]{2,1,0:T(8,128)(2,1)S(1)} %pad_maximum_fusion.5), channel_id=1, replica_groups=mesh['section'=4,'expert'=64] {'expert'}, dimensions={0} | all-to-all | bytes 6291456 | tf_op jit(solution)/shard_map/all_to_all | solution.py:86
  292.5 1.6 copy-done.20
  295.1 5.1 %fusion = f32[768,1536]{1,0:T(8,128)S(1)} fusion(bf16[2048,768]{1,0:T(8,128)(2,1)S(1)} %bitcast.123, bf16[2048,768]{1,0:T(8,128)(2,1)S(1)} %bitcast.125, bf16[256,1024]{1,0:T(8,128)(2,1)S(1)} %get-tuple-element.28, bf16[256,1024]{1,0:T(8,128)(2,1)S(1)} %get-tuple-element.27, bf16[512,2048]{1,0:T(8,128)(2,1)S(1)} %slice_bitcast_fusion.3), kind=kOutput, calls=%fused_computation.1 | convolution fusion | flops 4853858304 | bytes 14155776 | tf_op jit(solution)/shard_map/dot_general | solution.py:112
  300.9 2.8 convolution_convert_fusion
  305.1 1.9 pad_maximum_fusion.6
  307.0 5.8 %all-to-all-start.3 = ((bf16[64,8,3072]{2,1,0:T(8,128)(2,1)}), bf16[64,8,3072]{2,1,0:T(8,128)(2,1)}, u32[]{:S(2)}, u32[]{:S(2)}) async-start(bf16[64,8,3072]{2,1,0:T(8,128)(2,1)} %pad_maximum_fusion.6), calls=%async_computation.3 | async-start | bytes 6291456 | tf_op jit(solution)/shard_map/all_to_all | solution.py:134
  313.5 73.1 %all-to-all-done.3 = bf16[64,8,3072]{2,1,0:T(8,128)(2,1)} async-done(((bf16[64,8,3072]{2,1,0:T(8,128)(2,1)}), bf16[64,8,3072]{2,1,0:T(8,128)(2,1)}, u32[]{:S(2)}, u32[]{:S(2)}) %all-to-all-start.3) | async-done | bytes 3145760 | tf_op jit(solution)/shard_map/all_to_all | solution.py:134
  386.5 1.8 fusion.32
  388.5 2.0 fusion.18
  (120 shorter events, 21.4 us)
Async XLA Ops:
  0.0 108.5 %copy-start = (bf16[1,1,768,2048]{3,2,1,0:T(8,128)(2,1)S(1)}, bf16[1,1,768,2048]{3,2,1,0:T(8,128)(2,1)}, u32[]{:S(2)}) copy-start(bf16[1,1,768,2048]{3,2,1,0:T(8,128)(2,1)} %param.13) | copy-start | bytes 9437188
  3.0 6.1 %copy-start.18 = (s32[64]{0:T(128)}, s32[64]{0:T(128)S(1)}, u32[]{:S(2)}) copy-start(s32[64]{0:T(128)S(1)} %add.360) | copy-start | bytes 772
  3.1 108.3 %copy-start.13 = (pred[512]{0:T(512)(128)(4,1)}, pred[512]{0:T(512)(128)(4,1)S(1)}, u32[]{:S(2)}) copy-start(pred[512]{0:T(512)(128)(4,1)S(1)} %eq.272) | copy-start | bytes 1540
  3.2 109.0 %copy-start.15 = (pred[512]{0:T(512)(128)(4,1)}, pred[512]{0:T(512)(128)(4,1)S(1)}, u32[]{:S(2)}) copy-start(pred[512]{0:T(512)(128)(4,1)S(1)} %eq.276) | copy-start | bytes 1540
  4.1 5.0 %copy-start.11 = (s32[512]{0:T(512)}, s32[512]{0:T(512)S(1)}, u32[]{:S(2)}) copy-start(s32[512]{0:T(512)S(1)} %add.367) | copy-start | bytes 6148
  4.3 4.8 %copy-start.12 = (s32[512]{0:T(512)}, s32[512]{0:T(512)S(1)}, u32[]{:S(2)}) copy-start(s32[512]{0:T(512)S(1)} %add.374) | copy-start | bytes 6148
  11.5 85.9 %all-to-all-start = ((bf16[64,8,3072]{2,1,0:T(8,128)(2,1)}), bf16[64,8,3072]{2,1,0:T(8,128)(2,1)}, u32[]{:S(2)}, u32[]{:S(2)}) async-start(bf16[64,8,3072]{2,1,0:T(8,128)(2,1)} %pad_maximum_fusion.3), calls=%async_computation | async-start | bytes 6291456 | tf_op jit(solution)/shard_map/all_to_all | solution.py:86
  24.1 77.2 %copy-start.7 = (pred[256,512]{1,0:T(32,128)(4,1)}, pred[256,512]{1,0:T(32,128)(4,1)S(1)}, u32[]{:S(2)}) copy-start(pred[256,512]{1,0:T(32,128)(4,1)S(1)} %get-tuple-element.45) | copy-start | bytes 393220
  24.2 77.2 %copy-start.9 = (pred[256,512]{1,0:T(32,128)(4,1)}, pred[256,512]{1,0:T(32,128)(4,1)S(1)}, u32[]{:S(2)}) copy-start(pred[256,512]{1,0:T(32,128)(4,1)S(1)} %get-tuple-element.46) | copy-start | bytes 393220
  99.3 2.5 copy-start.19
  99.3 3.5 copy-start.21
  114.7 6.0 %copy-start.17 = (f32[1,2,64,8]{2,3,1,0:T(8,128)S(1)}, f32[1,2,64,8]{2,3,1,0:T(8,128)}, u32[]{:S(2)}) copy-start(f32[1,2,64,8]{2,3,1,0:T(8,128)} %param.15) | copy-start | bytes 12292
  114.7 79.6 %all-to-all-start.1 = ((bf16[64,8,3072]{2,1,0:T(8,128)(2,1)}), bf16[64,8,3072]{2,1,0:T(8,128)(2,1)}, u32[]{:S(2)}, u32[]{:S(2)}) async-start(bf16[64,8,3072]{2,1,0:T(8,128)(2,1)} %pad_maximum_fusion.4), calls=%async_computation.1 | async-start | bytes 6291456 | tf_op jit(solution)/shard_map/all_to_all | solution.py:134
  124.7 73.5 %copy-start.4 = (s32[64,8]{1,0:T(8,128)}, s32[64,8]{1,0:T(8,128)S(1)}, u32[]{:S(2)}) copy-start(s32[64,8]{1,0:T(8,128)S(1)} %add_add_fusion) | copy-start | bytes 6148
  194.3 3.9 %copy-start.1 = (bf16[1,64,2048]{2,1,0:T(8,128)(2,1)S(1)}, bf16[1,64,2048]{2,1,0:T(8,128)(2,1)}, u32[]{:S(2)}) copy-start(bf16[1,64,2048]{2,1,0:T(8,128)(2,1)} %param.8) | copy-start | bytes 786436
  198.4 4.7 %copy-start.2 = (bf16[64,2048]{1,0:T(8,128)(2,1)}, bf16[64,2048]{1,0:T(8,128)(2,1)S(1)}, u32[]{:S(2)}) copy-start(bf16[64,2048]{1,0:T(8,128)(2,1)S(1)} %fusion.41) | copy-start | bytes 786436
  198.4 9.0 %collective-permute-start = (bf16[64,2048]{1,0:T(8,128)(2,1)S(1)}, bf16[64,2048]{1,0:T(8,128)(2,1)}, u32[]{:S(2)}, u32[]{:S(2)}) collective-permute-start(bf16[64,2048]{1,0:T(8,128)(2,1)S(1)} %fusion.41), channel_id=1, source_target_pairs={{0,64},{64,128},{128,192},{1,65},{65,129},{129,193},{2,66},{66,130... | collective-permute-start | bytes 786440 | tf_op jit(solution)/shard_map/ppermute | solution.py:17
  203.1 7.5 %copy-start.16 = (pred[512]{0:T(512)(128)(4,1)S(1)}, pred[512]{0:T(512)(128)(4,1)}, u32[]{:S(2)}) copy-start(pred[512]{0:T(512)(128)(4,1)} %copy-done.15) | copy-start | bytes 1540
  211.3 80.2 %copy-start.8 = (pred[256,512]{1,0:T(32,128)(4,1)S(1)}, pred[256,512]{1,0:T(32,128)(4,1)}, u32[]{:S(2)}) copy-start(pred[256,512]{1,0:T(32,128)(4,1)} %copy-done.7) | copy-start | bytes 393220
  211.4 80.2 %copy-start.10 = (pred[256,512]{1,0:T(32,128)(4,1)S(1)}, pred[256,512]{1,0:T(32,128)(4,1)}, u32[]{:S(2)}) copy-start(pred[256,512]{1,0:T(32,128)(4,1)} %copy-done.9) | copy-start | bytes 393220
  292.3 1.9 copy-start.20
  292.3 2.8 copy-start.22
  300.9 2.8 copy-start.14
  307.0 79.5 %all-to-all-start.3 = ((bf16[64,8,3072]{2,1,0:T(8,128)(2,1)}), bf16[64,8,3072]{2,1,0:T(8,128)(2,1)}, u32[]{:S(2)}, u32[]{:S(2)}) async-start(bf16[64,8,3072]{2,1,0:T(8,128)(2,1)} %pad_maximum_fusion.6), calls=%async_computation.3 | async-start | bytes 6291456 | tf_op jit(solution)/shard_map/all_to_all | solution.py:134
  313.5 75.0 %copy-start.5 = (bf16[64,512]{1,0:T(8,128)(2,1)S(1)}, bf16[64,512]{1,0:T(8,128)(2,1)}, u32[]{:S(2)}) copy-start(bf16[64,512]{1,0:T(8,128)(2,1)} %get-tuple-element.19) | copy-start | bytes 196612
  313.5 75.0 %copy-start.6 = (bf16[64,512]{1,0:T(8,128)(2,1)S(1)}, bf16[64,512]{1,0:T(8,128)(2,1)}, u32[]{:S(2)}) copy-start(bf16[64,512]{1,0:T(8,128)(2,1)} %get-tuple-element.20) | copy-start | bytes 196612
  388.4 2.2 copy-start.3

commit v10 on v9

--- a/solution.py
+++ b/solution.py
@@ -48,7 +48,7 @@
     return full_slot, part_slot, part_piece, pieces
 
 
-def apply_layer(hidden_rows, norm_gain, route_ids, combine, gate_up_w, down_w, experts):
+def apply_layer(hidden_rows, norm_gain, route_ids, combine, gate_up_w, down_w, experts, settle=False):
     normed_rows = rms_normed(hidden_rows, norm_gain)
     row_count, model_width = hidden_rows.shape
     top_count = route_ids.shape[-1]
@@ -83,6 +83,22 @@
         ],
         axis=-1,
     )
+    weights = combine[:, :, None]
+    mix_full = jnp.sum(jnp.where(hits_full, weights, 0.0), axis=1)
+    mix_part = jnp.sum(jnp.where(hits_part, weights, 0.0), axis=1)
+
+    def split(mix):
+        high = mix.astype(jnp.bfloat16)
+        low = (mix - high.astype(jnp.float32)).astype(jnp.bfloat16)
+        return [high, low]
+
+    full_lhs = jnp.concatenate(split(mix_full), axis=0)
+    part_parts = []
+    for piece in range(pieces):
+        part_parts += split(jnp.where((part_piece == piece)[None, :], mix_part, 0.0))
+    part_lhs = jnp.concatenate(part_parts, axis=0)
+    if settle:
+        outgoing, full_lhs, part_lhs = lax.optimization_barrier((outgoing, full_lhs, part_lhs))
     received = lax.all_to_all(outgoing, "expert", split_axis=0, concat_axis=0, tiled=True)
 
     extra = width - SUBLANE
@@ -131,31 +147,16 @@
         ],
         axis=-1,
     )
+    if settle:
+        back, full_lhs, part_lhs = lax.optimization_barrier((back, full_lhs, part_lhs))
     returned = lax.all_to_all(back, "expert", split_axis=0, concat_axis=0, tiled=True)
     sent_back = back
     back_full = returned[:, :, :model_width].reshape(wire_rows, model_width)
     back_rows = returned[:, :, model_width:].reshape(wire_rows, piece_width)
 
-    weights = combine[:, :, None]
-    mix_full = jnp.sum(jnp.where(hits_full, weights, 0.0), axis=1)
-    mix_part = jnp.sum(jnp.where(hits_part, weights, 0.0), axis=1)
-
-    def split(mix):
-        high = mix.astype(jnp.bfloat16)
-        low = (mix - high.astype(jnp.float32)).astype(jnp.bfloat16)
-        return [high, low]
-
-    full_parts = split(mix_full)
-    full_sum = jnp.dot(
-        jnp.concatenate(full_parts, axis=0), back_full, preferred_element_type=jnp.float32
-    )
+    full_sum = jnp.dot(full_lhs, back_full, preferred_element_type=jnp.float32)
     branch_full = full_sum[:row_count] + full_sum[row_count:]
-    part_parts = []
-    for piece in range(pieces):
-        part_parts += split(jnp.where((part_piece == piece)[None, :], mix_part, 0.0))
-    part_sum = jnp.dot(
-        jnp.concatenate(part_parts, axis=0), back_rows, preferred_element_type=jnp.float32
-    )
+    part_sum = jnp.dot(part_lhs, back_rows, preferred_element_type=jnp.float32)
     branch_part = [
         part_sum[(2 * piece) * row_count:(2 * piece + 1) * row_count]
         + part_sum[(2 * piece + 1) * row_count:(2 * piece + 2) * row_count]
@@ -183,6 +184,7 @@
             gate_up_w,
             w_down[0, 0],
             experts,
+            tick_index + 1 == TICKS,
         )
         traced.append(layer_out)
         if tick_index + 1 < TICKS:

time: 392 us -> 385 us (0.982)
  blocking collectives: 80.2 us -> 159 us
  waiting for transfers between devices: 216 us -> 143 us
  starting transfers between devices: 27 us -> 21.3 us
  other arithmetic: 25.4 us -> 21.4 us
    all_to_all x0 -> x1, blocking collectives: none -> 79.2 us  [apply_layer(): lax.all_to_all(back, 'expert', split_axis=0, concat_axis=0, tiled=True)]
    all_to_all x2 -> x1, waiting for transfers between devices: 138 us -> 64.8 us  [apply_layer(): lax.all_to_all(back, 'expert', split_axis=0, concat_axis=0, tiled=True)]
    all_to_all x2 -> x1, starting transfers between devices: 11.7 us -> 5.9 us  [apply_layer(): lax.all_to_all(back, 'expert', split_axis=0, concat_axis=0, tiled=True)]
  transfers between devices with their start and end apart: 4 -> 3, of which waited for: 4 -> 3; matrix products, arithmetic and copies ran while one was open for 3% -> 3% of each run, Pallas kernels for 0% -> 0%
where the time goes in v10:
time: 385 us
  blocking collectives  159 us (41%)
  waiting for transfers between devices  143 us (37%)
  matrix products  28.7 us (7%)
  other arithmetic  21.4 us (6%)
  starting transfers between devices  21.3 us (6%)
  local copies, waits for them, and re-layouts  10.4 us (3%)
    all_to_all x1, blocking collectives, apply_layer(): lax.all_to_all(outgoing, 'expert', split_axis=0, concat_axis=0, tiled=True)  80.2 us
    all_to_all x1, blocking collectives, apply_layer(): lax.all_to_all(back, 'expert', split_axis=0, concat_axis=0, tiled=True)  79.2 us
    all_to_all x1, waiting for transfers between devices, apply_layer(): lax.all_to_all(outgoing, 'expert', split_axis=0, concat_axis=0, tiled=True)  73.2 us
    all_to_all x1, waiting for transfers between devices, apply_layer(): lax.all_to_all(back, 'expert', split_axis=0, concat_axis=0, tiled=True)  64.8 us
    all_to_all x1, starting transfers between devices, apply_layer(): lax.all_to_all(outgoing, 'expert', split_axis=0, concat_axis=0, tiled=True)  12.2 us
    dot_general x2, matrix products, apply_layer(): gate_up = jnp.dot(inputs, gate_up_w, preferred_element_type=jnp.float32)  10 us
  transfers between devices with their start and end apart: 3, of which 3 were waited for; matrix products, arithmetic and copies ran while one was open for 3% of the time, Pallas kernels for 0%

profile of v10, /device:TPU:16, one launch (start us, length us, event | category | flops | bytes accessed | tf_op | source)
XLA Modules:
  0.0 384.9 jit_solution(5753696265372041985)
XLA Ops:
  0.1 0.9 fusion.106
  1.2 1.1 fusion.38
  4.3 1.2 reduce-window.14
  6.1 1.1 fusion.40
  7.9 0.7 fusion.14
  9.6 1.9 pad_maximum_fusion.3
  11.5 12.2 %all-to-all-start = ((bf16[64,8,3072]{2,1,0:T(8,128)(2,1)}), bf16[64,8,3072]{2,1,0:T(8,128)(2,1)}, u32[]{:S(2)}, u32[]{:S(2)}) async-start(bf16[64,8,3072]{2,1,0:T(8,128)(2,1)} %pad_maximum_fusion.3), calls=%async_computation | async-start | bytes 6291456 | tf_op jit(solution)/shard_map/all_to_all | solution.py:102
  24.2 73.2 %all-to-all-done = bf16[64,8,3072]{2,1,0:T(8,128)(2,1)} async-done(((bf16[64,8,3072]{2,1,0:T(8,128)(2,1)}), bf16[64,8,3072]{2,1,0:T(8,128)(2,1)}, u32[]{:S(2)}, u32[]{:S(2)}) %all-to-all-start) | async-done | bytes 3145760 | tf_op jit(solution)/shard_map/all_to_all | solution.py:102
  97.4 1.9 convolution_convert_fusion.5
  99.5 1.9 slice_bitcast_fusion.7
  101.9 1.0 copy-done.22
  102.8 5.0 %fusion.1 = f32[768,1536]{1,0:T(8,128)S(1)} fusion(bf16[2048,768]{1,0:T(8,128)(2,1)S(1)} %bitcast.124, bf16[2048,768]{1,0:T(8,128)(2,1)S(1)} %bitcast.126, bf16[256,1024]{1,0:T(8,128)(2,1)S(1)} %get-tuple-element.44, bf16[256,1024]{1,0:T(8,128)(2,1)S(1)} %get-tuple-element.43, bf16[512,2048]{1,0:T(8,128)(2,1)S(1)} %slice_bitcast_fusion.7), kind=kOutput, calls=%fused_computation.2 | convolution fusion | flops 4853858304 | bytes 14155776 | tf_op jit(solution)/shard_map/dot_general | solution.py:128
  108.5 2.8 convolution_convert_fusion.1
  112.8 1.9 pad_maximum_fusion.4
  114.7 5.9 %all-to-all-start.1 = ((bf16[64,8,3072]{2,1,0:T(8,128)(2,1)}), bf16[64,8,3072]{2,1,0:T(8,128)(2,1)}, u32[]{:S(2)}, u32[]{:S(2)}) async-start(bf16[64,8,3072]{2,1,0:T(8,128)(2,1)} %pad_maximum_fusion.4), calls=%async_computation.1 | async-start | bytes 6291456 | tf_op jit(solution)/shard_map/all_to_all | solution.py:152
  121.7 1.2 reduce-window.16
  123.1 0.8 fusion.60
  124.7 2.0 fusion.27
  126.8 1.4 subtract_convert_fusion.4
  128.1 1.4 select_convert_fusion.3
  129.5 64.8 %all-to-all-done.1 = bf16[64,8,3072]{2,1,0:T(8,128)(2,1)} async-done(((bf16[64,8,3072]{2,1,0:T(8,128)(2,1)}), bf16[64,8,3072]{2,1,0:T(8,128)(2,1)}, u32[]{:S(2)}, u32[]{:S(2)}) %all-to-all-start.1) | async-done | bytes 3145760 | tf_op jit(solution)/shard_map/all_to_all | solution.py:152
  194.3 1.8 fusion.33
  196.3 2.1 fusion.19
  198.6 3.2 collective-permute-start
  202.5 5.0 %collective-permute-done = bf16[64,2048]{1,0:T(8,128)(2,1)S(1)} collective-permute-done((bf16[64,2048]{1,0:T(8,128)(2,1)S(1)}, bf16[64,2048]{1,0:T(8,128)(2,1)S(1)}, u32[]{:S(2)}, u32[]{:S(2)}) %collective-permute-start) | collective-permute-done | bytes 262176 | tf_op jit(solution)/shard_map/ppermute | solution.py:17
  209.8 80.2 %all_to_all.20 = bf16[64,8,3072]{2,1,0:T(8,128)(2,1)S(1)} all-to-all(bf16[64,8,3072]{2,1,0:T(8,128)(2,1)S(1)} %pad_maximum_fusion.5), channel_id=1, replica_groups=mesh['section'=4,'expert'=64] {'expert'}, dimensions={0} | all-to-all | bytes 6291456 | tf_op jit(solution)/shard_map/all_to_all | solution.py:102
  291.0 1.6 copy-done.21
  292.6 1.0 copy-done.23
  293.6 5.0 %fusion = f32[768,1536]{1,0:T(8,128)S(1)} fusion(bf16[2048,768]{1,0:T(8,128)(2,1)S(1)} %bitcast.125, bf16[2048,768]{1,0:T(8,128)(2,1)S(1)} %bitcast.127, bf16[256,1024]{1,0:T(8,128)(2,1)S(1)} %get-tuple-element.40, bf16[256,1024]{1,0:T(8,128)(2,1)S(1)} %get-tuple-element.39, bf16[512,2048]{1,0:T(8,128)(2,1)S(1)} %slice_bitcast_fusion.3), kind=kOutput, calls=%fused_computation.1 | convolution fusion | flops 4853858304 | bytes 14155776 | tf_op jit(solution)/shard_map/dot_general | solution.py:128
  299.3 2.8 convolution_convert_fusion
  303.8 79.2 %all_to_all.21 = bf16[64,8,3072]{2,1,0:T(8,128)(2,1)S(1)} all-to-all(bf16[64,8,3072]{2,1,0:T(8,128)(2,1)S(1)} %pad_maximum_fusion.6), channel_id=1, replica_groups=mesh['section'=4,'expert'=64] {'expert'}, dimensions={0} | all-to-all | bytes 6291456 | tf_op jit(solution)/shard_map/all_to_all | solution.py:152
  384.0 0.8 maximum_bitcast_fusion
  (123 shorter events, 17.1 us)
Async XLA Ops:
  0.0 108.5 %copy-start = (bf16[1,1,768,2048]{3,2,1,0:T(8,128)(2,1)S(1)}, bf16[1,1,768,2048]{3,2,1,0:T(8,128)(2,1)}, u32[]{:S(2)}) copy-start(bf16[1,1,768,2048]{3,2,1,0:T(8,128)(2,1)} %param.13) | copy-start | bytes 9437188
  3.0 6.1 %copy-start.19 = (s32[64]{0:T(128)}, s32[64]{0:T(128)S(1)}, u32[]{:S(2)}) copy-start(s32[64]{0:T(128)S(1)} %add.360) | copy-start | bytes 772
  3.1 108.3 %copy-start.14 = (pred[512]{0:T(512)(128)(4,1)}, pred[512]{0:T(512)(128)(4,1)S(1)}, u32[]{:S(2)}) copy-start(pred[512]{0:T(512)(128)(4,1)S(1)} %eq.272) | copy-start | bytes 1540
  3.2 109.0 %copy-start.16 = (pred[512]{0:T(512)(128)(4,1)}, pred[512]{0:T(512)(128)(4,1)S(1)}, u32[]{:S(2)}) copy-start(pred[512]{0:T(512)(128)(4,1)S(1)} %eq.276) | copy-start | bytes 1540
  4.1 5.0 %copy-start.10 = (s32[512]{0:T(512)}, s32[512]{0:T(512)S(1)}, u32[]{:S(2)}) copy-start(s32[512]{0:T(512)S(1)} %add.367) | copy-start | bytes 6148
  4.3 4.8 %copy-start.12 = (s32[512]{0:T(512)}, s32[512]{0:T(512)S(1)}, u32[]{:S(2)}) copy-start(s32[512]{0:T(512)S(1)} %add.374) | copy-start | bytes 6148
  11.5 85.9 %all-to-all-start = ((bf16[64,8,3072]{2,1,0:T(8,128)(2,1)}), bf16[64,8,3072]{2,1,0:T(8,128)(2,1)}, u32[]{:S(2)}, u32[]{:S(2)}) async-start(bf16[64,8,3072]{2,1,0:T(8,128)(2,1)} %pad_maximum_fusion.3), calls=%async_computation | async-start | bytes 6291456 | tf_op jit(solution)/shard_map/all_to_all | solution.py:102
  24.2 77.2 %copy-start.6 = (pred[256,512]{1,0:T(32,128)(4,1)}, pred[256,512]{1,0:T(32,128)(4,1)S(1)}, u32[]{:S(2)}) copy-start(pred[256,512]{1,0:T(32,128)(4,1)S(1)} %get-tuple-element.57) | copy-start | bytes 393220
  24.2 77.2 %copy-start.8 = (pred[256,512]{1,0:T(32,128)(4,1)}, pred[256,512]{1,0:T(32,128)(4,1)S(1)}, u32[]{:S(2)}) copy-start(pred[256,512]{1,0:T(32,128)(4,1)S(1)} %get-tuple-element.58) | copy-start | bytes 393220
  99.3 2.5 copy-start.20
  99.4 3.5 copy-start.22
  114.7 6.0 %copy-start.18 = (f32[1,2,64,8]{2,3,1,0:T(8,128)S(1)}, f32[1,2,64,8]{2,3,1,0:T(8,128)}, u32[]{:S(2)}) copy-start(f32[1,2,64,8]{2,3,1,0:T(8,128)} %param.15) | copy-start | bytes 12292
  114.7 79.6 %all-to-all-start.1 = ((bf16[64,8,3072]{2,1,0:T(8,128)(2,1)}), bf16[64,8,3072]{2,1,0:T(8,128)(2,1)}, u32[]{:S(2)}, u32[]{:S(2)}) async-start(bf16[64,8,3072]{2,1,0:T(8,128)(2,1)} %pad_maximum_fusion.4), calls=%async_computation.1 | async-start | bytes 6291456 | tf_op jit(solution)/shard_map/all_to_all | solution.py:152
  194.3 4.1 %copy-start.1 = (bf16[1,64,2048]{2,1,0:T(8,128)(2,1)S(1)}, bf16[1,64,2048]{2,1,0:T(8,128)(2,1)}, u32[]{:S(2)}) copy-start(bf16[1,64,2048]{2,1,0:T(8,128)(2,1)} %param.8) | copy-start | bytes 786436
  196.3 5.5 %copy-start.3 = (bf16[64,512]{1,0:T(8,128)(2,1)S(1)}, bf16[64,512]{1,0:T(8,128)(2,1)}, u32[]{:S(2)}) copy-start(bf16[64,512]{1,0:T(8,128)(2,1)} %get-tuple-element.60) | copy-start | bytes 196612
  196.3 5.5 %copy-start.4 = (bf16[64,512]{1,0:T(8,128)(2,1)S(1)}, bf16[64,512]{1,0:T(8,128)(2,1)}, u32[]{:S(2)}) copy-start(bf16[64,512]{1,0:T(8,128)(2,1)} %get-tuple-element.61) | copy-start | bytes 196612
  196.3 5.5 %copy-start.5 = (bf16[64,512]{1,0:T(8,128)(2,1)S(1)}, bf16[64,512]{1,0:T(8,128)(2,1)}, u32[]{:S(2)}) copy-start(bf16[64,512]{1,0:T(8,128)(2,1)} %get-tuple-element.62) | copy-start | bytes 196612
  196.3 5.5 %copy-start.11 = (s32[512]{0:T(512)S(1)}, s32[512]{0:T(512)}, u32[]{:S(2)}) copy-start(s32[512]{0:T(512)} %copy-done.10) | copy-start | bytes 6148
  196.3 5.5 %copy-start.13 = (s32[512]{0:T(512)S(1)}, s32[512]{0:T(512)}, u32[]{:S(2)}) copy-start(s32[512]{0:T(512)} %copy-done.12) | copy-start | bytes 6148
  196.3 11.2 %copy-start.2 = (bf16[1,64,2048]{2,1,0:T(8,128)(2,1)S(1)}, bf16[1,64,2048]{2,1,0:T(8,128)(2,1)}, u32[]{:S(2)}) copy-start(bf16[1,64,2048]{2,1,0:T(8,128)(2,1)} %param.9) | copy-start | bytes 786436
  198.4 10.1 %copy-start.15 = (pred[512]{0:T(512)(128)(4,1)S(1)}, pred[512]{0:T(512)(128)(4,1)}, u32[]{:S(2)}) copy-start(pred[512]{0:T(512)(128)(4,1)} %copy-done.14) | copy-start | bytes 1540
  198.6 8.9 %collective-permute-start = (bf16[64,2048]{1,0:T(8,128)(2,1)S(1)}, bf16[64,2048]{1,0:T(8,128)(2,1)S(1)}, u32[]{:S(2)}, u32[]{:S(2)}) collective-permute-start(bf16[64,2048]{1,0:T(8,128)(2,1)S(1)} %fusion.41), channel_id=1, source_target_pairs={{0,64},{64,128},{128,192},{1,65},{65,129},{129,193},{2,66},{66,130... | collective-permute-start | bytes 786440 | tf_op jit(solution)/shard_map/ppermute | solution.py:17
  202.5 6.5 %copy-start.17 = (pred[512]{0:T(512)(128)(4,1)S(1)}, pred[512]{0:T(512)(128)(4,1)}, u32[]{:S(2)}) copy-start(pred[512]{0:T(512)(128)(4,1)} %copy-done.16) | copy-start | bytes 1540
  209.8 80.2 %copy-start.7 = (pred[256,512]{1,0:T(32,128)(4,1)S(1)}, pred[256,512]{1,0:T(32,128)(4,1)}, u32[]{:S(2)}) copy-start(pred[256,512]{1,0:T(32,128)(4,1)} %copy-done.6) | copy-start | bytes 393220
  209.8 80.2 %copy-start.9 = (pred[256,512]{1,0:T(32,128)(4,1)S(1)}, pred[256,512]{1,0:T(32,128)(4,1)}, u32[]{:S(2)}) copy-start(pred[256,512]{1,0:T(32,128)(4,1)} %copy-done.8) | copy-start | bytes 393220
  290.7 1.9 copy-start.21
  290.7 2.8 copy-start.23

commit v11 on v10

--- a/solution.py
+++ b/solution.py
@@ -48,7 +48,38 @@
     return full_slot, part_slot, part_piece, pieces
 
 
-def apply_layer(hidden_rows, norm_gain, route_ids, combine, gate_up_w, down_w, experts, settle=False):
+def step_tables(route_ids, combine, experts):
+    row_count, top_count = route_ids.shape
+    block_rows = min(BLOCK_ROWS, row_count)
+    group_count = row_count // block_rows
+    capacity = max(2, min(block_rows, block_rows * top_count // experts * 3 // 2))
+    width = group_count * capacity
+    positions = slot_table(route_ids.reshape(group_count, block_rows, top_count), experts, capacity)
+    full_slot, part_slot, part_piece, pieces = wire_slots(experts, width)
+    hits_full = positions[:, :, None] == full_slot[None, None, :]
+    hits_part = positions[:, :, None] == part_slot[None, None, :]
+    weights = combine[:, :, None]
+    mix_full = jnp.sum(jnp.where(hits_full, weights, 0.0), axis=1)
+    mix_part = jnp.sum(jnp.where(hits_part, weights, 0.0), axis=1)
+
+    def split(mix):
+        high = mix.astype(jnp.bfloat16)
+        low = (mix - high.astype(jnp.float32)).astype(jnp.bfloat16)
+        return [high, low]
+
+    full_lhs = jnp.concatenate(split(mix_full), axis=0)
+    part_parts = []
+    for piece in range(pieces):
+        part_parts += split(jnp.where((part_piece == piece)[None, :], mix_part, 0.0))
+    pick_full = jnp.sum(hits_full.astype(jnp.int32), axis=1).astype(jnp.bfloat16).T
+    pick_part = jnp.sum(hits_part.astype(jnp.int32), axis=1).astype(jnp.bfloat16).T
+    return full_lhs, jnp.concatenate(part_parts, axis=0), pick_full, pick_part
+
+
+def apply_layer(
+    hidden_rows, norm_gain, route_ids, combine, gate_up_w, down_w, experts, settle=False,
+    mix=None, carry=(),
+):
     normed_rows = rms_normed(hidden_rows, norm_gain)
     row_count, model_width = hidden_rows.shape
     top_count = route_ids.shape[-1]
@@ -66,6 +97,8 @@
     hits_part = positions[:, :, None] == part_slot[None, None, :]
     pick_full = jnp.sum(hits_full.astype(jnp.int32), axis=1).astype(jnp.bfloat16).T
     pick_part = jnp.sum(hits_part.astype(jnp.int32), axis=1).astype(jnp.bfloat16).T
+    if mix is not None:
+        pick_full, pick_part = mix[2], mix[3]
     send_full = jnp.dot(pick_full, normed_rows, preferred_element_type=jnp.float32)
     send_part = jnp.zeros((wire_rows, piece_width), jnp.float32)
     for piece in range(pieces):
@@ -97,6 +130,8 @@
     for piece in range(pieces):
         part_parts += split(jnp.where((part_piece == piece)[None, :], mix_part, 0.0))
     part_lhs = jnp.concatenate(part_parts, axis=0)
+    if mix is not None:
+        full_lhs, part_lhs = mix[0], mix[1]
     if settle:
         outgoing, full_lhs, part_lhs = lax.optimization_barrier((outgoing, full_lhs, part_lhs))
     received = lax.all_to_all(outgoing, "expert", split_axis=0, concat_axis=0, tiled=True)
@@ -147,10 +182,8 @@
         ],
         axis=-1,
     )
-    if settle:
-        back, full_lhs, part_lhs = lax.optimization_barrier((back, full_lhs, part_lhs))
+    back, full_lhs, part_lhs, carry = lax.optimization_barrier((back, full_lhs, part_lhs, carry))
     returned = lax.all_to_all(back, "expert", split_axis=0, concat_axis=0, tiled=True)
-    sent_back = back
     back_full = returned[:, :, :model_width].reshape(wire_rows, model_width)
     back_rows = returned[:, :, model_width:].reshape(wire_rows, piece_width)
 
@@ -164,7 +197,7 @@
     ]
     branch_sum = branch_full + jnp.concatenate(branch_part, axis=-1)
     residual = hidden_rows.astype(jnp.float32)
-    return (residual + branch_sum).astype(jnp.bfloat16), sent_back
+    return (residual + branch_sum).astype(jnp.bfloat16), carry
 
 
 def local(in_flight, entering, norm_gain, w_gate, w_up, w_down, routes, combine_weight):
@@ -173,24 +206,26 @@
     carried = in_flight[0]
     gate_up_w = jnp.concatenate([w_gate[0, 0], w_up[0, 0]], axis=-1)
     traced = []
-    step_routes = routes[0, 0]
-    step_combine = combine_weight[0, 0]
+    step_mix = [None] + [
+        step_tables(routes[0, t], combine_weight[0, t], experts) for t in range(1, TICKS)
+    ]
     for tick_index in range(TICKS):
-        layer_out, sent_back = apply_layer(
+        layer_out, carry = apply_layer(
             carried,
             norm_gain[0],
-            step_routes,
-            step_combine,
+            routes[0, tick_index],
+            combine_weight[0, tick_index],
             gate_up_w,
             w_down[0, 0],
             experts,
             tick_index + 1 == TICKS,
+            step_mix[tick_index],
+            tuple(step_mix[tick_index + 1:]) if tick_index == 0 else (),
         )
+        if tick_index == 0:
+            step_mix = [None] + list(carry)
         traced.append(layer_out)
         if tick_index + 1 < TICKS:
-            _, step_routes, step_combine = lax.optimization_barrier(
-                (sent_back, routes[0, tick_index + 1], combine_weight[0, tick_index + 1])
-            )
             shifted = passed_along(layer_out, "section", 1)
             carried = jnp.where(section_index == 0, entering[tick_index], shifted)
     return jnp.stack(traced)[:, None]

time: 385 us -> 392 us (1.018)
  blocking collectives: 159 us -> 238 us
  waiting for transfers between devices: 143 us -> 72.2 us
  starting transfers between devices: 21.3 us -> 15.9 us
    all_to_all x1 -> x2, blocking collectives: 79.2 us -> 158 us  [apply_layer(): lax.all_to_all(back, 'expert', split_axis=0, concat_axis=0, tiled=True)]
    all_to_all x1 -> x0, waiting for transfers between devices: 64.8 us -> none  [apply_layer(): lax.all_to_all(back, 'expert', split_axis=0, concat_axis=0, tiled=True)]
    all_to_all x1, waiting for transfers between devices: 73.2 us -> 66.2 us  [apply_layer(): lax.all_to_all(outgoing, 'expert', split_axis=0, concat_axis=0, tiled=True)]
    all_to_all x1 -> x0, starting transfers between devices: 5.9 us -> none  [apply_layer(): lax.all_to_all(back, 'expert', split_axis=0, concat_axis=0, tiled=True)]
  transfers between devices with their start and end apart: 3 -> 2, of which waited for: 3 -> 2; matrix products, arithmetic and copies ran while one was open for 3% -> 2% of each run, Pallas kernels for 0% -> 0%
where the time goes in v11:
time: 392 us; the launch traced here: 391 us
  blocking collectives  238 us (61%)
  waiting for transfers between devices  72.2 us (18%)
  matrix products  27 us (7%)
  other arithmetic  24.5 us (6%)
  starting transfers between devices  15.9 us (4%)
  local copies, waits for them, and re-layouts  12.5 us (3%)
    all_to_all x2, blocking collectives, apply_layer(): lax.all_to_all(back, 'expert', split_axis=0, concat_axis=0, tiled=True)  158 us
    all_to_all x1, blocking collectives, apply_layer(): lax.all_to_all(outgoing, 'expert', split_axis=0, concat_axis=0, tiled=True)  80 us
    all_to_all x1, waiting for transfers between devices, apply_layer(): lax.all_to_all(outgoing, 'expert', split_axis=0, concat_axis=0, tiled=True)  66.2 us
    all_to_all x1, starting transfers between devices, apply_layer(): lax.all_to_all(outgoing, 'expert', split_axis=0, concat_axis=0, tiled=True)  12.5 us
    dot_general x2, matrix products, apply_layer(): gate_up = jnp.dot(inputs, gate_up_w, preferred_element_type=jnp.float32)  10 us
  transfers between devices with their start and end apart: 2, of which 2 were waited for; matrix products, arithmetic and copies ran while one was open for 2% of the time, Pallas kernels for 0%

profile of v11, /device:TPU:16, one launch (start us, length us, event | category | flops | bytes accessed | tf_op | source)
XLA Modules:
  0.0 390.9 jit_solution(13233134621157807732)
XLA Ops:
  0.0 0.9 fusion.92
  3.0 1.2 reduce-window.14
  4.8 1.2 reduce-window.16
  9.1 1.1 fusion.38
  11.0 1.1 fusion.40
  12.2 1.8 fusion.24
  15.6 1.9 pad_maximum_fusion.3
  17.5 12.5 %all-to-all-start = ((bf16[64,8,3072]{2,1,0:T(8,128)(2,1)}), bf16[64,8,3072]{2,1,0:T(8,128)(2,1)}, u32[]{:S(2)}, u32[]{:S(2)}) async-start(bf16[64,8,3072]{2,1,0:T(8,128)(2,1)} %pad_maximum_fusion.3), calls=%async_computation | async-start | bytes 6291456 | tf_op jit(solution)/shard_map/all_to_all | solution.py:137
  30.5 1.3 fusion.27
  34.0 0.9 convert_bitcast_fusion
  34.9 0.9 convert_bitcast_fusion.1
  35.8 1.6 compare_and_fusion.1
  37.4 66.2 %all-to-all-done = bf16[64,8,3072]{2,1,0:T(8,128)(2,1)} async-done(((bf16[64,8,3072]{2,1,0:T(8,128)(2,1)}), bf16[64,8,3072]{2,1,0:T(8,128)(2,1)}, u32[]{:S(2)}, u32[]{:S(2)}) %all-to-all-start) | async-done | bytes 3145760 | tf_op jit(solution)/shard_map/all_to_all | solution.py:137
  103.6 2.1 convolution_convert_fusion.5
  105.8 1.9 slice_bitcast_fusion.7
  108.2 1.0 copy-done.16
  109.2 5.0 %fusion.1 = f32[768,1536]{1,0:T(8,128)S(1)} fusion(bf16[2048,768]{1,0:T(8,128)(2,1)S(1)} %bitcast.134, bf16[2048,768]{1,0:T(8,128)(2,1)S(1)} %bitcast.136, bf16[256,1024]{1,0:T(8,128)(2,1)S(1)} %get-tuple-element.56, bf16[256,1024]{1,0:T(8,128)(2,1)S(1)} %get-tuple-element.55, bf16[512,2048]{1,0:T(8,128)(2,1)S(1)} %slice_bitcast_fusion.7), kind=kOutput, calls=%fused_computation.2 | convolution fusion | flops 4853858304 | bytes 14155776 | tf_op jit(solution)/shard_map/dot_general | solution.py:163
  114.9 2.8 convolution_convert_fusion.1
  119.4 79.1 %all_to_all.20 = bf16[64,8,3072]{2,1,0:T(8,128)(2,1)S(1)} all-to-all(bf16[64,8,3072]{2,1,0:T(8,128)(2,1)S(1)} %pad_maximum_fusion.4), channel_id=1, replica_groups=mesh['section'=4,'expert'=64] {'expert'}, dimensions={0} | all-to-all | bytes 6291456 | tf_op jit(solution)/shard_map/all_to_all | solution.py:186
  199.8 0.8 fusion.41
  200.6 3.4 collective-permute-start
  204.0 6.0 %collective-permute-done = bf16[64,2048]{1,0:T(8,128)(2,1)} collective-permute-done((bf16[64,2048]{1,0:T(8,128)(2,1)}, bf16[64,2048]{1,0:T(8,128)(2,1)}, u32[]{:S(2)}, u32[]{:S(2)}) %collective-permute-start) | collective-permute-done | bytes 262176 | tf_op jit(solution)/shard_map/ppermute | solution.py:17
  210.0 1.2 fusion.34
  212.2 1.1 fusion.58
  213.3 1.1 fusion.21
  214.7 80.0 %all_to_all.21 = bf16[64,8,3072]{2,1,0:T(8,128)(2,1)S(1)} all-to-all(bf16[64,8,3072]{2,1,0:T(8,128)(2,1)S(1)} %pad_maximum_fusion.5), channel_id=1, replica_groups=mesh['section'=4,'expert'=64] {'expert'}, dimensions={0} | all-to-all | bytes 6291456 | tf_op jit(solution)/shard_map/all_to_all | solution.py:137
  295.6 1.6 copy-done.15
  297.3 1.0 copy-done.17
  298.2 5.0 %fusion = f32[768,1536]{1,0:T(8,128)S(1)} fusion(bf16[2048,768]{1,0:T(8,128)(2,1)S(1)} %bitcast.135, bf16[2048,768]{1,0:T(8,128)(2,1)S(1)} %bitcast.137, bf16[256,1024]{1,0:T(8,128)(2,1)S(1)} %get-tuple-element.52, bf16[256,1024]{1,0:T(8,128)(2,1)S(1)} %get-tuple-element.51, bf16[512,2048]{1,0:T(8,128)(2,1)S(1)} %slice_bitcast_fusion.3), kind=kOutput, calls=%fused_computation.1 | convolution fusion | flops 4853858304 | bytes 14155776 | tf_op jit(solution)/shard_map/dot_general | solution.py:163
  303.9 2.8 convolution_convert_fusion
  308.4 79.2 %all_to_all.22 = bf16[64,8,3072]{2,1,0:T(8,128)(2,1)S(1)} all-to-all(bf16[64,8,3072]{2,1,0:T(8,128)(2,1)S(1)} %pad_maximum_fusion.6), channel_id=1, replica_groups=mesh['section'=4,'expert'=64] {'expert'}, dimensions={0} | all-to-all | bytes 6291456 | tf_op jit(solution)/shard_map/all_to_all | solution.py:186
  389.1 1.8 maximum_bitcast_fusion
  (112 shorter events, 20.9 us)
Async XLA Ops:
  0.0 114.8 %copy-start = (bf16[1,1,768,2048]{3,2,1,0:T(8,128)(2,1)S(1)}, bf16[1,1,768,2048]{3,2,1,0:T(8,128)(2,1)}, u32[]{:S(2)}) copy-start(bf16[1,1,768,2048]{3,2,1,0:T(8,128)(2,1)} %param.13) | copy-start | bytes 9437188
  8.4 24.8 %copy-start.7 = (pred[512]{0:T(512)(128)(4,1)}, pred[512]{0:T(512)(128)(4,1)S(1)}, u32[]{:S(2)}) copy-start(pred[512]{0:T(512)(128)(4,1)S(1)} %eq.272) | copy-start | bytes 1540
  11.0 22.2 %copy-start.10 = (pred[512]{0:T(512)(128)(4,1)}, pred[512]{0:T(512)(128)(4,1)S(1)}, u32[]{:S(2)}) copy-start(pred[512]{0:T(512)(128)(4,1)S(1)} %eq.276) | copy-start | bytes 1540
  17.5 12.8 %copy-start.13 = (f32[1,2,64,8]{2,3,1,0:T(8,128)S(1)}, f32[1,2,64,8]{2,3,1,0:T(8,128)}, u32[]{:S(2)}) copy-start(f32[1,2,64,8]{2,3,1,0:T(8,128)} %param.15) | copy-start | bytes 12292
  17.5 86.1 %all-to-all-start = ((bf16[64,8,3072]{2,1,0:T(8,128)(2,1)}), bf16[64,8,3072]{2,1,0:T(8,128)(2,1)}, u32[]{:S(2)}, u32[]{:S(2)}) async-start(bf16[64,8,3072]{2,1,0:T(8,128)(2,1)} %pad_maximum_fusion.3), calls=%async_computation | async-start | bytes 6291456 | tf_op jit(solution)/shard_map/all_to_all | solution.py:137
  105.7 2.5 copy-start.14
  105.7 3.5 copy-start.16
  114.9 2.8 copy-start.8
  117.7 0.8 copy-start.11
  119.4 79.1 %copy-start.2 = (bf16[256,512]{1,0:T(8,128)(2,1)S(1)}, bf16[256,512]{1,0:T(8,128)(2,1)}, u32[]{:S(2)}) copy-start(bf16[256,512]{1,0:T(8,128)(2,1)} %pad_maximum_fusion.7) | copy-start | bytes 786436
  198.4 0.9 copy-start.4
  198.4 1.4 copy-start.1
  200.6 9.4 %collective-permute-start = (bf16[64,2048]{1,0:T(8,128)(2,1)}, bf16[64,2048]{1,0:T(8,128)(2,1)}, u32[]{:S(2)}, u32[]{:S(2)}) collective-permute-start(bf16[64,2048]{1,0:T(8,128)(2,1)} %fusion.41), channel_id=1, source_target_pairs={{0,64},{64,128},{128,192},{1,65},{65,129},{129,193},{2,66},{66,130... | collective-permute-start | bytes 786440 | tf_op jit(solution)/shard_map/ppermute | solution.py:17
  214.6 80.0 %copy-start.5 = (pred[256,512]{1,0:T(32,128)(4,1)S(1)}, pred[256,512]{1,0:T(32,128)(4,1)}, u32[]{:S(2)}) copy-start(pred[256,512]{1,0:T(32,128)(4,1)} %get-tuple-element.69) | copy-start | bytes 393220
  214.7 80.0 %copy-start.6 = (pred[256,512]{1,0:T(32,128)(4,1)S(1)}, pred[256,512]{1,0:T(32,128)(4,1)}, u32[]{:S(2)}) copy-start(pred[256,512]{1,0:T(32,128)(4,1)} %get-tuple-element.70) | copy-start | bytes 393220
  295.4 1.9 copy-start.15
  295.4 2.8 copy-start.17
  303.9 2.8 copy-start.9
  306.8 0.8 copy-start.12
  387.6 0.9 copy-start.3
